TPU v7x, 512 devices: a whole 4x8x8 slice. The times are simulated.
512 devices in a mesh: pairs: 64 (over x, y, core), aux: 8 (over z).
Axes of the slice: x: 4, y: 8, z: 8, core: 2. Of those that a mesh axis runs over, the one named last changes fastest.
Arguments:
- amplitudes: bfloat16 [1024, 128, 128], P('pairs'), may hold values from -6 to 6
- pno_coef: bfloat16 [1024, 256, 128], P('pairs'), may hold values from -0.625 to 0.625
- ladder_ints: bfloat16 [320, 128, 128], P('aux'), may hold values from -0.3125 to 0.3125
- coulomb_ints: bfloat16 [1024, 128, 128], P(('pairs', 'aux')), may hold values from -6 to 6
- pno_energy: float32 [1024, 128], P(('pairs', 'aux')), may hold values from 0.3 to 3
- link_owner: int32 [49152, 1], P(('pairs', 'aux')), may hold values from 0 to 63; in each aligned block of 96 rows (0 to 95, 96 to 191, ...) at most 2 rows name the same one
- link_local: int32 [49152, 1], P(('pairs', 'aux')), may hold values from 0 to 15
Outputs:
- updated: float32 [1024, 128, 128], P(('pairs', 'aux'))
Inputs may be any that keep to these rules, and one draw needn't show every extreme that they name: `link_owner`: in each device's aligned block of 96 rows no owner group is named by more than 2 rows, a bound that some block reaches.
All inputs are finite; a program needn't handle non-finite values.
Results may differ from a plain program's by a relative error of at most 0.0033.
Values may be sent and summed in bfloat16 or wider, within the bound.
No kernel may reach another device: no remote copies, remote signals or barrier semaphores. Data moves between devices by JAX's collectives and lax.ppermute only.
A program may use at most 128 MiB of HBM per device.

v0:
```python
import jax
import jax.numpy as jnp
from jax import lax
from jax.sharding import PartitionSpec as P


def local(amplitudes, pno_coef, ladder_ints, coulomb_ints, pno_energy, link_owner, link_local):
    groups = lax.axis_size("pairs")
    pair_dev = amplitudes.shape[0]
    own_rows = coulomb_ints.shape[0]
    slot_count = link_owner.shape[0]
    per_slice = slot_count // pair_dev
    capacity = max(2, (5 * slot_count + 4 * groups - 1) // (4 * groups))
    pno_width = amplitudes.shape[1]
    pao_width = pno_coef.shape[1]
    owner_group = link_owner[:, 0]
    local_index = link_local[:, 0]
    slot_order = jnp.arange(slot_count, dtype=jnp.int32)
    same_owner = (owner_group[:, None] == owner_group[None, :]) & (
        slot_order[None, :] < slot_order[:, None]
    )
    slot_rank = jnp.sum(same_owner.astype(jnp.int32), axis=1)
    bucket = owner_group * capacity + slot_rank
    places = jnp.arange(groups * capacity, dtype=jnp.int32)
    match_table = (bucket[:, None] == places[None, :]).astype(jnp.int32)
    wanted = jnp.sum(match_table * (local_index[:, None] + 1), axis=0) - 1
    asked_rows = lax.all_to_all(
        wanted.reshape(groups, capacity), "pairs", split_axis=0, concat_axis=0, tiled=True
    )
    present = asked_rows >= 0
    picked = jnp.maximum(asked_rows, 0)
    nothing = jnp.zeros((), jnp.bfloat16)
    amp_items = jnp.where(present[:, :, None, None], amplitudes[picked], nothing)
    coef_items = jnp.where(present[:, :, None, None], pno_coef[picked], nothing)
    got_amp, got_coef = (
        lax.all_to_all(amp_items, "pairs", split_axis=0, concat_axis=0, tiled=True),
        lax.all_to_all(coef_items, "pairs", split_axis=0, concat_axis=0, tiled=True),
    )
    flat_amp = got_amp.reshape(groups * capacity, pno_width, pno_width)
    flat_coef = got_coef.reshape(groups * capacity, pao_width, pno_width)
    key_rows = bucket.reshape(pair_dev, per_slice)

    def pair_terms(inputs):
        coef_p, amp_p, key_row = inputs
        coef_q = flat_coef[key_row]
        amp_q = flat_amp[key_row]
        intersection = jnp.einsum(
            "ac,lad->lcd", coef_p, coef_q, preferred_element_type=jnp.float32
        ).astype(jnp.bfloat16)
        halfway = jnp.einsum(
            "lcd,lde->lce", intersection, amp_q, preferred_element_type=jnp.float32
        ).astype(jnp.bfloat16)
        total = jnp.einsum("lce,lfe->cf", halfway, intersection, preferred_element_type=jnp.float32)
        ladder_half = jnp.einsum(
            "qcd,de->qce", ladder_ints, amp_p, preferred_element_type=jnp.float32
        ).astype(jnp.bfloat16)
        total = total + jnp.einsum(
            "qce,qfe->cf", ladder_half, ladder_ints, preferred_element_type=jnp.float32
        )
        return total

    partial_value = lax.map(pair_terms, (pno_coef, amplitudes, key_rows))
    first_row = lax.axis_index("aux") * own_rows
    amp_mine = lax.dynamic_slice_in_dim(amplitudes, first_row, own_rows, 0)
    summed = lax.psum(partial_value, "aux")
    reduced = lax.dynamic_slice_in_dim(summed, first_row, own_rows, 0)
    residual = coulomb_ints.astype(jnp.float32) + reduced
    denominator = pno_energy[:, :, None] + pno_energy[:, None, :]
    return amp_mine.astype(jnp.float32) - residual / denominator


def solution(mesh):
    in_specs = (
        P("pairs", None, None),
        P("pairs", None, None),
        P("aux", None, None),
        P(("pairs", "aux"), None, None),
        P(("pairs", "aux"), None),
        P(("pairs", "aux"), None),
        P(("pairs", "aux"), None),
    )
    out_specs = P(("pairs", "aux"), None, None)
    return jax.shard_map(local, mesh=mesh, in_specs=in_specs, out_specs=out_specs, check_vma=False)
```

profile of v0, /device:TPU:1, one launch (start us, length us, event | category | flops | bytes accessed | tf_op | source)
XLA Modules:
  0.0 576.1 jit_solution(16118599690050762865)
XLA Ops:
  6.5 0.9 convert_reduce_fusion
  7.4 0.7 fusion.21
  8.1 0.7 add_bitcast_fusion
  9.0 20.7 %all_to_all.16 = s32[64,1,2]{2,1,0:T(1,128)S(1)} all-to-all(s32[64,1,2]{2,1,0:T(1,128)S(1)} %bitcast.97), channel_id=1, replica_groups=mesh['pairs'=64,'aux'=8] {'pairs'}, dimensions={0} | all-to-all | bytes 1024 | tf_op jit(solution)/shard_map/all_to_all | solution.py:27
  30.3 4.1 gather_fusion.3
  34.3 4.5 broadcast_select_fusion.1
  38.8 5.8 %all-to-all-start.2 = ((bf16[64,2,128,128]{3,2,1,0:T(8,128)(2,1)}), bf16[64,2,128,128]{3,2,1,0:T(8,128)(2,1)}, u32[]{:S(2)}, u32[]{:S(2)}) async-start(bf16[64,2,128,128]{3,2,1,0:T(8,128)(2,1)} %broadcast_select_fusion.1), calls=%async_computation.2 | async-start | bytes 8388608 | tf_op jit(solution)/shard_map/all_to_all | solution.py:36
  44.7 6.5 %gather_fusion.2 = bf16[128,256,128]{2,1,0:T(8,128)(2,1)} fusion(bf16[16,256,128]{2,1,0:T(8,128)(2,1)S(1)} %copy-done.1, s32[1024]{0:T(1024)S(1)} %pad_clamp_fusion.1), kind=kCustom, calls=%fused_computation.2 | custom fusion | bytes 16777728 | tf_op jit(solution)/shard_map/gather | solution.py:34
  51.2 7.2 %broadcast_select_fusion = bf16[64,2,256,128]{3,2,1,0:T(8,128)(2,1)} fusion(bf16[64,2,256,128]{3,2,1,0:T(8,128)(2,1)} %bitcast.95, pred[64,2]{1,0:T(8,128)(4,1)S(1)} %copy.33), kind=kLoop, calls=%fused_computation.27 | loop fusion | flops 4194304 | bytes 16777344 | tf_op jit(solution)/shard_map/jit(_where)/select_n | solution.py:34
  58.4 82.2 %all-to-all-done.2 = bf16[64,2,128,128]{3,2,1,0:T(8,128)(2,1)} async-done(((bf16[64,2,128,128]{3,2,1,0:T(8,128)(2,1)}), bf16[64,2,128,128]{3,2,1,0:T(8,128)(2,1)}, u32[]{:S(2)}, u32[]{:S(2)}) %all-to-all-start.2) | async-done | bytes 4194336 | tf_op jit(solution)/shard_map/all_to_all | solution.py:36
  140.6 6.0 %all-to-all-start.1 = ((bf16[64,2,256,128]{3,2,1,0:T(8,128)(2,1)}), bf16[64,2,256,128]{3,2,1,0:T(8,128)(2,1)}, u32[]{:S(2)}, u32[]{:S(2)}) async-start(bf16[64,2,256,128]{3,2,1,0:T(8,128)(2,1)} %broadcast_select_fusion), calls=%async_computation.1 | async-start | bytes 16777216 | tf_op jit(solution)/shard_map/all_to_all | solution.py:37
  146.8 185.5 %all-to-all-done.1 = bf16[64,2,256,128]{3,2,1,0:T(8,128)(2,1)} async-done(((bf16[64,2,256,128]{3,2,1,0:T(8,128)(2,1)}), bf16[64,2,256,128]{3,2,1,0:T(8,128)(2,1)}, u32[]{:S(2)}, u32[]{:S(2)}) %all-to-all-start.1) | async-done | bytes 8388640 | tf_op jit(solution)/shard_map/all_to_all | solution.py:37
  332.4 156.8 %while.10 = (s32[]{:T(128)}, f32[16,128,128]{2,1,0:T(8,128)}, s32[16,6]{1,0:T(8,128)S(1)}, bf16[128,256,128]{2,1,0:T(8,128)(2,1)}, bf16[16,256,128]{2,1,0:T(8,12...) while((s32[]{:T(128)}, f32[16,128,128]{2,1,0:T(8,128)}, ...), condition=%wide.region_3.4_spmd, body=%wide.region_2.3_spmd.sunk | while | flops 437076992 | bytes 5084381 | solution.py:62
  332.4 4.0 gather_fusion
  336.8 2.8 gather_fusion.1
  339.5 0.4 fusion.47
  340.0 2.3 fusion.48
  342.2 4.0 gather_fusion
  346.6 2.8 gather_fusion.1
  349.8 2.3 fusion.48
  352.0 4.0 gather_fusion
  356.4 2.8 gather_fusion.1
  359.6 2.3 fusion.48
  361.8 4.0 gather_fusion
  366.2 2.8 gather_fusion.1
  369.4 2.3 fusion.48
  371.6 4.0 gather_fusion
  376.0 2.8 gather_fusion.1
  379.2 2.3 fusion.48
  381.4 4.0 gather_fusion
  385.8 2.8 gather_fusion.1
  389.0 2.3 fusion.48
  391.2 4.0 gather_fusion
  395.6 2.8 gather_fusion.1
  398.8 2.3 fusion.48
  401.0 4.0 gather_fusion
  405.4 2.8 gather_fusion.1
  408.6 2.3 fusion.48
  410.8 4.0 gather_fusion
  415.2 2.8 gather_fusion.1
  418.4 2.3 fusion.48
  420.6 4.0 gather_fusion
  425.0 2.8 gather_fusion.1
  428.2 2.3 fusion.48
  430.4 4.0 gather_fusion
  434.8 2.8 gather_fusion.1
  438.0 2.3 fusion.48
  440.2 4.0 gather_fusion
  444.6 2.8 gather_fusion.1
  447.8 2.3 fusion.48
  450.0 4.0 gather_fusion
  454.4 2.8 gather_fusion.1
  457.6 2.3 fusion.48
  459.8 4.0 gather_fusion
  464.2 2.8 gather_fusion.1
  467.4 2.3 fusion.48
  469.7 4.0 gather_fusion
  474.0 2.8 gather_fusion.1
  477.2 2.3 fusion.48
  479.5 4.0 gather_fusion
  483.8 2.8 gather_fusion.1
  487.0 2.3 fusion.48
  489.3 78.3 %all-reduce.2.cloned.1.call-done = f32[16,128,128]{2,1,0:T(8,128)} async-done(((f32[16,128,128]{2,1,0:T(8,128)}), f32[16,128,128]{2,1,0:T(8,128)}) %all-reduce.2.cloned.1.call-update) | async-done | bytes 1048592 | tf_op jit(solution)/shard_map/psum | solution.py:65
  567.6 1.7 divide_subtract_fusion
  (86 shorter events, 12.3 us)
Async XLA Ops:
  38.8 5.8 %copy-start.1 = (bf16[16,256,128]{2,1,0:T(8,128)(2,1)S(1)}, bf16[16,256,128]{2,1,0:T(8,128)(2,1)}, u32[]{:S(2)}) copy-start(bf16[16,256,128]{2,1,0:T(8,128)(2,1)} %param.10) | copy-start | bytes 3145732
  38.8 101.8 %all-to-all-start.2 = ((bf16[64,2,128,128]{3,2,1,0:T(8,128)(2,1)}), bf16[64,2,128,128]{3,2,1,0:T(8,128)(2,1)}, u32[]{:S(2)}, u32[]{:S(2)}) async-start(bf16[64,2,128,128]{3,2,1,0:T(8,128)(2,1)} %broadcast_select_fusion.1), calls=%async_computation.2 | async-start | bytes 8388608 | tf_op jit(solution)/shard_map/all_to_all | solution.py:36
  58.4 273.9 %copy-start = (bf16[40,128,128]{2,1,0:T(8,128)(2,1)S(1)}, bf16[40,128,128]{2,1,0:T(8,128)(2,1)}, u32[]{:S(2)}) copy-start(bf16[40,128,128]{2,1,0:T(8,128)(2,1)} %param.11) | copy-start | bytes 3932164
  140.6 191.8 %all-to-all-start.1 = ((bf16[64,2,256,128]{3,2,1,0:T(8,128)(2,1)}), bf16[64,2,256,128]{3,2,1,0:T(8,128)(2,1)}, u32[]{:S(2)}, u32[]{:S(2)}) async-start(bf16[64,2,256,128]{3,2,1,0:T(8,128)(2,1)} %broadcast_select_fusion), calls=%async_computation.1 | async-start | bytes 16777216 | tf_op jit(solution)/shard_map/all_to_all | solution.py:37
  146.6 420.9 %all-reduce.2.cloned.1.call-start = ((), (), s32[]{:S(2)}) async-start(), calls=%async_computation.3 | async-start | bytes 2097152 | tf_op jit(solution)/shard_map/psum | solution.py:65
  332.4 235.2 %copy-start.2 = (bf16[2,128,128]{2,1,0:T(8,128)(2,1)S(1)}, bf16[2,128,128]{2,1,0:T(8,128)(2,1)}, u32[]{:S(2)}) copy-start(bf16[2,128,128]{2,1,0:T(8,128)(2,1)} %param.12) | copy-start | bytes 196612
  332.4 235.2 %copy-start.3 = (f32[2,128]{1,0:T(2,128)S(1)}, f32[2,128]{1,0:T(2,128)}, u32[]{:S(2)}) copy-start(f32[2,128]{1,0:T(2,128)} %param.13) | copy-start | bytes 3076
Sparse Core Ops, SparseCore 0:
  489.4 78.1 all-reduce.1
where the time goes:
time: 582 us; the launch traced here: 576 us
  waiting for transfers between devices  346 us (59%)
  local copies, waits for them, and re-layouts  120 us (21%)
  matrix products  47.7 us (8%)
  blocking collectives  20.7 us (4%)
  other arithmetic  16.2 us (3%)
  between operations  13.5 us (2%)
  starting transfers between devices  11.9 us (2%)
    all_to_all x1, waiting for transfers between devices, local(): lax.all_to_all(coef_items, 'pairs', split_axis=0, concat_axis=0, tiled=True)  186 us
    all_to_all x1, waiting for transfers between devices, local(): lax.all_to_all(amp_items, 'pairs', split_axis=0, concat_axis=0, tiled=True)  82.2 us
    psum x1, waiting for transfers between devices, local(): summed = lax.psum(partial_value, 'aux')  78.3 us
    gather x16, local copies, waits for them, and re-layouts, pair_terms(): coef_q = flat_coef[key_row]  64 us
    gather x16, local copies, waits for them, and re-layouts, pair_terms(): amp_q = flat_amp[key_row]  44.3 us
    dot_general x16, matrix products, pair_terms(): jnp.einsum('qce,qfe->cf', ladder_half, ladder_ints, preferred_element_typ...  36.2 us
    all_to_all x1, blocking collectives, local(): lax.all_to_all(wanted.reshape(groups, capacity), 'pairs', split_axis=0, c...  20.7 us
  transfers between devices with their start and end apart: 3, of which 3 were waited for; matrix products, arithmetic and copies ran while one was open for 2% of the time, Pallas kernels for 0%

commit v1 on v0

v1 whole, which is shorter than its diff:
```python
import jax
import jax.numpy as jnp
from jax import lax
from jax.sharding import PartitionSpec as P


def local(amplitudes, pno_coef, ladder_ints, coulomb_ints, pno_energy, link_owner, link_local):
    groups = lax.axis_size("pairs")
    pair_dev = amplitudes.shape[0]
    own_rows = coulomb_ints.shape[0]
    slot_count = link_owner.shape[0]
    per_slice = slot_count // pair_dev
    capacity = max(2, (5 * slot_count + 4 * groups - 1) // (4 * groups))
    pno_width = amplitudes.shape[1]
    pao_width = pno_coef.shape[1]
    owner_group = link_owner[:, 0]
    local_index = link_local[:, 0]
    slot_order = jnp.arange(slot_count, dtype=jnp.int32)
    same_owner = (owner_group[:, None] == owner_group[None, :]) & (
        slot_order[None, :] < slot_order[:, None]
    )
    slot_rank = jnp.sum(same_owner.astype(jnp.int32), axis=1)
    bucket = owner_group * capacity + slot_rank
    places = jnp.arange(groups * capacity, dtype=jnp.int32)
    match_table = (bucket[:, None] == places[None, :]).astype(jnp.int32)
    wanted = jnp.sum(match_table * (local_index[:, None] + 1), axis=0) - 1
    asked_rows = lax.all_to_all(
        wanted.reshape(groups, capacity), "pairs", split_axis=0, concat_axis=0, tiled=True
    )
    picked = jnp.maximum(asked_rows, 0)
    amp_items = amplitudes[picked]
    coef_items = pno_coef[picked]
    got_coef = lax.all_to_all(coef_items, "pairs", split_axis=0, concat_axis=0, tiled=True)
    got_amp = lax.all_to_all(amp_items, "pairs", split_axis=0, concat_axis=0, tiled=True)
    flat_amp = got_amp.reshape(groups * capacity, pno_width, pno_width)
    flat_coef = got_coef.reshape(groups * capacity, pao_width, pno_width)

    ladder_half = jnp.einsum(
        "qcd,pde->pqce", ladder_ints, amplitudes, preferred_element_type=jnp.float32
    ).astype(jnp.bfloat16)
    ladder = jnp.einsum(
        "pqce,qfe->pcf", ladder_half, ladder_ints, preferred_element_type=jnp.float32
    )
    ladder = lax.optimization_barrier(ladder)

    coef_q = flat_coef[bucket].reshape(pair_dev, per_slice, pao_width, pno_width)
    amp_q = flat_amp[bucket].reshape(pair_dev, per_slice, pno_width, pno_width)
    intersection = jnp.einsum(
        "pac,plad->plcd", pno_coef, coef_q, preferred_element_type=jnp.float32
    ).astype(jnp.bfloat16)
    halfway = jnp.einsum(
        "plcd,plde->plce", intersection, amp_q, preferred_element_type=jnp.float32
    ).astype(jnp.bfloat16)
    linked = jnp.einsum(
        "plce,plfe->pcf", halfway, intersection, preferred_element_type=jnp.float32
    )

    partial_value = linked + ladder
    reduced = lax.psum_scatter(partial_value, "aux", scatter_dimension=0, tiled=True)
    first_row = lax.axis_index("aux") * own_rows
    amp_mine = lax.dynamic_slice_in_dim(amplitudes, first_row, own_rows, 0)
    residual = coulomb_ints.astype(jnp.float32) + reduced
    denominator = pno_energy[:, :, None] + pno_energy[:, None, :]
    return amp_mine.astype(jnp.float32) - residual / denominator


def solution(mesh):
    in_specs = (
        P("pairs", None, None),
        P("pairs", None, None),
        P("aux", None, None),
        P(("pairs", "aux"), None, None),
        P(("pairs", "aux"), None),
        P(("pairs", "aux"), None),
        P(("pairs", "aux"), None),
    )
    out_specs = P(("pairs", "aux"), None, None)
    return jax.shard_map(local, mesh=mesh, in_specs=in_specs, out_specs=out_specs, check_vma=False)
```

time: 582 us -> 400 us (0.69)
  local copies, waits for them, and re-layouts: 120 us -> 25.1 us
  waiting for transfers between devices: 346 us -> 292 us
  matrix products: 47.7 us -> 28.6 us
  other arithmetic: 16.2 us -> 3.53 us
    gather x34 -> x4, local copies, waits for them, and re-layouts: 119 us -> 24.8 us  [the longest x1 9.43 us: local(): flat_coef[bucket].reshape(pair_dev, per_slice, pao_width, pno_width)]
    psum x1 -> x0, waiting for transfers between devices: 78.3 us -> none  [local(): summed = lax.psum(partial_value, 'aux')]
    reduce_scatter x0 -> x1, waiting for transfers between devices: none -> 37 us  [local(): lax.psum_scatter(partial_value, 'aux', scatter_dimension=0, tiled=True)]
    all_to_all x1, waiting for transfers between devices: 186 us -> 165 us  [local(): lax.all_to_all(coef_items, 'pairs', split_axis=0, concat_axis=0, tiled=True)]
    dot_general x48 -> x3, matrix products: 47.7 us -> 28.6 us  [the longest x1 15.2 us: local(): jnp.einsum('pqce,qfe->pcf', ladder_half, ladder_ints, preferred_element_t...]
    select_n x18 -> x1, other arithmetic: 11.9 us -> 0.69 us  [local(): flat_coef[bucket].reshape(pair_dev, per_slice, pao_width, pno_width)]
    all_to_all x1, waiting for transfers between devices: 82.2 us -> 89.5 us  [local(): lax.all_to_all(amp_items, 'pairs', split_axis=0, concat_axis=0, tiled=True)]
  transfers between devices with their start and end apart: 3 -> 3, of which waited for: 3 -> 3; matrix products, arithmetic and copies ran while one was open for 2% -> 7% of each run, Pallas kernels for 0% -> 0%
where the time goes in v1:
time: 400 us; the launch traced here: 395 us
  waiting for transfers between devices  292 us (73%)
  matrix products  28.6 us (7%)
  local copies, waits for them, and re-layouts  25.1 us (6%)
  blocking collectives  20.7 us (5%)
  between operations  13.5 us (3%)
  starting transfers between devices  12.2 us (3%)
    all_to_all x1, waiting for transfers between devices, local(): lax.all_to_all(coef_items, 'pairs', split_axis=0, concat_axis=0, tiled=True)  165 us
    all_to_all x1, waiting for transfers between devices, local(): lax.all_to_all(amp_items, 'pairs', split_axis=0, concat_axis=0, tiled=True)  89.5 us
    reduce_scatter x1, waiting for transfers between devices, local(): lax.psum_scatter(partial_value, 'aux', scatter_dimension=0, tiled=True)  37 us
    all_to_all x1, blocking collectives, local(): lax.all_to_all(wanted.reshape(groups, capacity), 'pairs', split_axis=0, c...  20.7 us
    dot_general x1, matrix products, local(): jnp.einsum('pqce,qfe->pcf', ladder_half, ladder_ints, preferred_element_t...  15.2 us
    gather x1, local copies, waits for them, and re-layouts, local(): flat_coef[bucket].reshape(pair_dev, per_slice, pao_width, pno_width)  9.43 us
  transfers between devices with their start and end apart: 3, of which 3 were waited for; matrix products, arithmetic and copies ran while one was open for 7% of the time, Pallas kernels for 0%

profile of v1, /device:TPU:1, one launch (start us, length us, event | category | flops | bytes accessed | tf_op | source)
XLA Modules:
  0.0 395.5 jit_solution(10647062247686651199)
XLA Ops:
  6.5 0.0 copy-start
  6.5 1.0 convert_reduce_fusion
  7.5 0.7 fusion.36
  8.2 0.1 select_reduce_fusion
  8.3 0.1 sub.10
  8.4 20.7 %all_to_all.16 = s32[64,1,2]{2,1,0:T(1,128)S(1)} all-to-all(s32[64,1,2]{2,1,0:T(1,128)S(1)} %bitcast.62), channel_id=1, replica_groups=mesh['pairs'=64,'aux'=8] {'pairs'}, dimensions={0} | all-to-all | bytes 1024 | tf_op jit(solution)/shard_map/all_to_all | solution.py:27
  29.1 0.1 maximum_reduce_fusion
  29.2 0.1 reshape.51
  29.4 4.1 %gather_fusion.2 = bf16[128,128,128]{2,1,0:T(8,128)(2,1)} fusion(bf16[16,128,128]{2,1,0:T(8,128)(2,1)} %param.7, s32[1024]{0:T(1024)S(1)} %pad_clamp_fusion.1), kind=kCustom, calls=%fused_computation.2 | custom fusion | bytes 8389120 | tf_op jit(solution)/shard_map/gather | solution.py:31
  33.5 0.0 copy-start.1
  33.5 5.8 %all-to-all-start.2 = ((bf16[64,2,128,128]{3,2,1,0:T(8,128)(2,1)}), bf16[64,2,128,128]{3,2,1,0:T(8,128)(2,1)}, u32[]{:S(2)}, u32[]{:S(2)}) async-start(bf16[64,2,128,128]{3,2,1,0:T(8,128)(2,1)} %bitcast.60), calls=%async_computation.2 | async-start | bytes 8388608 | tf_op jit(solution)/shard_map/all_to_all | solution.py:34
  39.3 0.0 copy-done.1
  39.3 6.4 %gather_fusion = bf16[128,256,128]{2,1,0:T(8,128)(2,1)} fusion(bf16[16,256,128]{2,1,0:T(8,128)(2,1)S(1)} %copy-done.1, s32[1024]{0:T(1024)S(1)} %pad_clamp_fusion.1), kind=kCustom, calls=%fused_computation | custom fusion | bytes 16777728 | tf_op jit(solution)/shard_map/gather | solution.py:32
  45.7 89.5 %all-to-all-done.2 = bf16[64,2,128,128]{3,2,1,0:T(8,128)(2,1)} async-done(((bf16[64,2,128,128]{3,2,1,0:T(8,128)(2,1)}), bf16[64,2,128,128]{3,2,1,0:T(8,128)(2,1)}, u32[]{:S(2)}, u32[]{:S(2)}) %all-to-all-start.2) | async-done | bytes 4194336 | tf_op jit(solution)/shard_map/all_to_all | solution.py:34
  135.2 0.0 copy-start.2
  135.2 6.1 %all-to-all-start.1 = ((bf16[64,2,256,128]{3,2,1,0:T(8,128)(2,1)}), bf16[64,2,256,128]{3,2,1,0:T(8,128)(2,1)}, u32[]{:S(2)}, u32[]{:S(2)}) async-start(bf16[64,2,256,128]{3,2,1,0:T(8,128)(2,1)} %bitcast.58), calls=%async_computation.1 | async-start | bytes 16777216 | tf_op jit(solution)/shard_map/all_to_all | solution.py:33
  141.4 0.2 reduce-scatter.2.cloned.1.call-start
  141.6 0.0 copy-done
  141.6 0.0 copy-done.2
  141.6 15.2 %fusion.19 = f32[16,128,128]{2,1,0:T(8,128)} fusion(bf16[40,128,128]{2,1,0:T(8,128)(2,1)S(1)} %copy-done, bf16[16,128,128]{2,1,0:T(8,128)(2,1)S(1)} %copy-done.2), kind=kOutput, calls=%fused_computation.14 | convolution fusion | flops 5379194880 | bytes 2883584 | tf_op jit(solution)/shard_map/pqce,qfe->pcf/dot_general | solution.py:41
  156.9 4.9 %gather_fusion.3 = bf16[96,128,128]{2,1,0:T(8,128)(2,1)} fusion(bf16[128,128,128]{2,1,0:T(8,128)(2,1)} %bitcast.12, s32[1024]{0:T(1024)S(1)} %pad_clamp_fusion), kind=kCustom, calls=%fused_computation.3 | custom fusion | bytes 6291840 | tf_op jit(solution)/shard_map/gather | solution.py:47
  161.8 165.4 %all-to-all-done.1 = bf16[64,2,256,128]{3,2,1,0:T(8,128)(2,1)} async-done(((bf16[64,2,256,128]{3,2,1,0:T(8,128)(2,1)}), bf16[64,2,256,128]{3,2,1,0:T(8,128)(2,1)}, u32[]{:S(2)}, u32[]{:S(2)}) %all-to-all-start.1) | async-done | bytes 8388640 | tf_op jit(solution)/shard_map/all_to_all | solution.py:33
  327.1 9.4 %gather_fusion.1 = bf16[96,256,128]{2,1,0:T(8,128)(2,1)} fusion(bf16[128,256,128]{2,1,0:T(8,128)(2,1)} %bitcast.6, s32[1024]{0:T(1024)S(1)} %pad_clamp_fusion), kind=kCustom, calls=%fused_computation.1 | custom fusion | bytes 12583296 | tf_op jit(solution)/shard_map/gather | solution.py:46
  336.6 6.4 %fusion.31 = bf16[16,6,128,128]{3,2,1,0:T(8,128)(2,1)} fusion(bf16[16,6,256,128]{3,2,1,0:T(8,128)(2,1)} %bitcast.59, bf16[16,256,128]{2,1,0:T(8,128)(2,1)S(1)} %copy-done.1), kind=kOutput, calls=%fused_computation.17 | convolution fusion | flops 805306368 | bytes 10485760 | tf_op jit(solution)/shard_map/pac,plad->plcd/dot_general | solution.py:48
  342.9 0.0 copy-start.3
  342.9 0.0 copy-start.4
  342.9 7.0 %fusion.24 = f32[16,128,128]{2,1,0:T(8,128)} fusion(f32[16,128,128]{2,1,0:T(8,128)} %fusion.19, bf16[16,6,128,128]{3,2,1,0:T(8,128)(2,1)} %fusion.31, bf16[16,6,128,128]{3,2,1,0:T(8,128)(2,1)} %bitcast.61), kind=kOutput, calls=%fused_computation.16 | convolution fusion | flops 807141376 | bytes 8388608 | tf_op jit(solution)/shard_map/plce,plfe->pcf/dot_general | solution.py:54
  349.9 0.0 reduce-scatter.2.cloned.1.call-update
  350.0 37.0 %reduce-scatter.2.cloned.1.call-done = f32[2,128,128]{2,1,0:T(8,128)} async-done(((f32[16,128,128]{2,1,0:T(8,128)}), f32[2,128,128]{2,1,0:T(8,128)}) %reduce-scatter.2.cloned.1.call-update) | async-done | bytes 131088 | tf_op jit(solution)/shard_map/reduce_scatter | solution.py:59
  386.9 0.0 copy-done.3
  386.9 0.0 copy-done.4
  386.9 1.7 divide_subtract_fusion
  (3 shorter events, 0.0 us)
Async XLA Ops:
  6.5 135.1 %copy-start = (bf16[40,128,128]{2,1,0:T(8,128)(2,1)S(1)}, bf16[40,128,128]{2,1,0:T(8,128)(2,1)}, u32[]{:S(2)}) copy-start(bf16[40,128,128]{2,1,0:T(8,128)(2,1)} %param.9) | copy-start | bytes 3932164
  33.5 5.8 %copy-start.1 = (bf16[16,256,128]{2,1,0:T(8,128)(2,1)S(1)}, bf16[16,256,128]{2,1,0:T(8,128)(2,1)}, u32[]{:S(2)}) copy-start(bf16[16,256,128]{2,1,0:T(8,128)(2,1)} %param.8) | copy-start | bytes 3145732
  33.5 101.8 %all-to-all-start.2 = ((bf16[64,2,128,128]{3,2,1,0:T(8,128)(2,1)}), bf16[64,2,128,128]{3,2,1,0:T(8,128)(2,1)}, u32[]{:S(2)}, u32[]{:S(2)}) async-start(bf16[64,2,128,128]{3,2,1,0:T(8,128)(2,1)} %bitcast.60), calls=%async_computation.2 | async-start | bytes 8388608 | tf_op jit(solution)/shard_map/all_to_all | solution.py:34
  135.2 6.4 %copy-start.2 = (bf16[16,128,128]{2,1,0:T(8,128)(2,1)S(1)}, bf16[16,128,128]{2,1,0:T(8,128)(2,1)}, u32[]{:S(2)}) copy-start(bf16[16,128,128]{2,1,0:T(8,128)(2,1)} %param.7) | copy-start | bytes 1572868
  135.2 191.9 %all-to-all-start.1 = ((bf16[64,2,256,128]{3,2,1,0:T(8,128)(2,1)}), bf16[64,2,256,128]{3,2,1,0:T(8,128)(2,1)}, u32[]{:S(2)}, u32[]{:S(2)}) async-start(bf16[64,2,256,128]{3,2,1,0:T(8,128)(2,1)} %bitcast.58), calls=%async_computation.1 | async-start | bytes 16777216 | tf_op jit(solution)/shard_map/all_to_all | solution.py:33
  141.4 245.6 %reduce-scatter.2.cloned.1.call-start = ((), (), s32[]{:S(2)}) async-start(), calls=%async_computation.4 | async-start | bytes 1179648 | tf_op jit(solution)/shard_map/reduce_scatter | solution.py:59
  342.9 44.0 %copy-start.3 = (bf16[2,128,128]{2,1,0:T(8,128)(2,1)S(1)}, bf16[2,128,128]{2,1,0:T(8,128)(2,1)}, u32[]{:S(2)}) copy-start(bf16[2,128,128]{2,1,0:T(8,128)(2,1)} %param.10) | copy-start | bytes 196612
  342.9 44.0 %copy-start.4 = (f32[2,128]{1,0:T(2,128)S(1)}, f32[2,128]{1,0:T(2,128)}, u32[]{:S(2)}) copy-start(f32[2,128]{1,0:T(2,128)} %param.11) | copy-start | bytes 3076
Sparse Core Ops, SparseCore 0:
  350.1 36.8 reduce-scatter.1

commit v2 on v1

--- a/solution.py
+++ b/solution.py
@@ -28,12 +28,9 @@
         wanted.reshape(groups, capacity), "pairs", split_axis=0, concat_axis=0, tiled=True
     )
     picked = jnp.maximum(asked_rows, 0)
-    amp_items = amplitudes[picked]
-    coef_items = pno_coef[picked]
-    got_coef = lax.all_to_all(coef_items, "pairs", split_axis=0, concat_axis=0, tiled=True)
-    got_amp = lax.all_to_all(amp_items, "pairs", split_axis=0, concat_axis=0, tiled=True)
-    flat_amp = got_amp.reshape(groups * capacity, pno_width, pno_width)
-    flat_coef = got_coef.reshape(groups * capacity, pao_width, pno_width)
+    both = jnp.concatenate([pno_coef, amplitudes], axis=1)
+    items = both[picked.reshape(groups * capacity)]
+    flat = lax.all_to_all(items, "pairs", split_axis=0, concat_axis=0, tiled=True)
 
     ladder_half = jnp.einsum(
         "qcd,pde->pqce", ladder_ints, amplitudes, preferred_element_type=jnp.float32
@@ -43,8 +40,9 @@
     )
     ladder = lax.optimization_barrier(ladder)
 
-    coef_q = flat_coef[bucket].reshape(pair_dev, per_slice, pao_width, pno_width)
-    amp_q = flat_amp[bucket].reshape(pair_dev, per_slice, pno_width, pno_width)
+    rows = flat[bucket]
+    coef_q = rows[:, :pao_width].reshape(pair_dev, per_slice, pao_width, pno_width)
+    amp_q = rows[:, pao_width:].reshape(pair_dev, per_slice, pno_width, pno_width)
     intersection = jnp.einsum(
         "pac,plad->plcd", pno_coef, coef_q, preferred_element_type=jnp.float32
     ).astype(jnp.bfloat16)
@@ -56,7 +54,11 @@
     )
 
     partial_value = linked + ladder
-    reduced = lax.psum_scatter(partial_value, "aux", scatter_dimension=0, tiled=True)
+    aux_count = lax.axis_size("aux")
+    pieces = partial_value.reshape(aux_count, own_rows, pno_width, pno_width)
+    reduced = jnp.sum(
+        lax.all_to_all(pieces, "aux", split_axis=0, concat_axis=0, tiled=True), axis=0
+    )
     first_row = lax.axis_index("aux") * own_rows
     amp_mine = lax.dynamic_slice_in_dim(amplitudes, first_row, own_rows, 0)
     residual = coulomb_ints.astype(jnp.float32) + reduced

time: 400 us -> 385 us (0.963); the launches traced: 395 us -> 385 us
  blocking collectives: 20.7 us -> 0 us
  starting transfers between devices: 12.2 us -> 27.5 us
  between operations: 13.5 us -> 0.11 us
  waiting for transfers between devices: 292 us -> 298 us
    all_to_all x2 -> x3, waiting for transfers between devices: 255 us -> 298 us  [the longest x1 261 us: local(): lax.all_to_all(items, 'pairs', split_axis=0, concat_axis=0, tiled=True)]
    reduce_scatter x1 -> x0, waiting for transfers between devices: 37 us -> none  [local(): lax.psum_scatter(partial_value, 'aux', scatter_dimension=0, tiled=True)]
    all_to_all x1 -> x0, blocking collectives: 20.7 us -> none  [local(): lax.all_to_all(wanted.reshape(groups, capacity), 'pairs', split_axis=0, c...]
    all_to_all x2 -> x3, starting transfers between devices: 11.9 us -> 27.5 us  [the longest x1 11.6 us: local(): lax.all_to_all(wanted.reshape(groups, capacity), 'pairs', split_axis=0, c...]
    gather x4 -> x2, local copies, waits for them, and re-layouts: 24.8 us -> 20.3 us  [the longest x1 12 us: local(): rows = flat[bucket]]
  transfers between devices with their start and end apart: 3 -> 3, of which waited for: 3 -> 3; matrix products, arithmetic and copies ran while one was open for 7% -> 4% of each run, Pallas kernels for 0% -> 0%
where the time goes in v2:
time: 385 us
  waiting for transfers between devices  298 us (77%)
  local copies, waits for them, and re-layouts  28.9 us (8%)
  starting transfers between devices  27.5 us (7%)
  matrix products  25 us (6%)
  other arithmetic  5.04 us (1%)
    all_to_all x1, waiting for transfers between devices, local(): lax.all_to_all(items, 'pairs', split_axis=0, concat_axis=0, tiled=True)  261 us
    all_to_all x1, waiting for transfers between devices, local(): lax.all_to_all(pieces, 'aux', split_axis=0, concat_axis=0, tiled=True)  29.3 us
    dot_general x1, matrix products, local(): jnp.einsum('pqce,qfe->pcf', ladder_half, ladder_ints, preferred_element_t...  14.5 us
    gather x1, local copies, waits for them, and re-layouts, local(): rows = flat[bucket]  12 us
    all_to_all x1, starting transfers between devices, local(): lax.all_to_all(wanted.reshape(groups, capacity), 'pairs', split_axis=0, c...  11.6 us
    all_to_all x1, starting transfers between devices, local(): lax.all_to_all(pieces, 'aux', split_axis=0, concat_axis=0, tiled=True)  10.2 us
    gather x1, local copies, waits for them, and re-layouts, local(): items = both[picked.reshape(groups * capacity)]  8.33 us
    all_to_all x1, waiting for transfers between devices, local(): lax.all_to_all(wanted.reshape(groups, capacity), 'pairs', split_axis=0, c...  7.7 us
  transfers between devices with their start and end apart: 3, of which 3 were waited for; matrix products, arithmetic and copies ran while one was open for 4% of the time, Pallas kernels for 0%

profile of v2, /device:TPU:1, one launch (start us, length us, event | category | flops | bytes accessed | tf_op | source)
XLA Modules:
  0.0 384.7 jit_solution(3174345628065996716)
XLA Ops:
  0.0 0.0 copy-start
  0.0 1.0 convert_reduce_fusion
  1.0 0.7 fusion.36
  1.6 0.1 select_reduce_fusion
  1.8 0.8 sub.10
  2.5 11.6 %all-to-all-start = ((s32[64,1,2]{2,1,0:T(1,128)}), s32[64,1,2]{2,1,0:T(1,128)S(1)}, u32[]{:S(2)}, u32[]{:S(2)}) async-start(s32[64,1,2]{2,1,0:T(1,128)} %bitcast.4), calls=%async_computation | async-start | bytes 65536 | tf_op jit(solution)/shard_map/all_to_all | solution.py:27
  14.2 1.5 pad_maximum_fusion
  15.7 7.7 %all-to-all-done = s32[64,1,2]{2,1,0:T(1,128)S(1)} async-done(((s32[64,1,2]{2,1,0:T(1,128)}), s32[64,1,2]{2,1,0:T(1,128)S(1)}, u32[]{:S(2)}, u32[]{:S(2)}) %all-to-all-start) | async-done | bytes 544 | tf_op jit(solution)/shard_map/all_to_all | solution.py:27
  23.4 0.1 maximum_reduce_fusion
  23.5 0.1 reshape.49
  23.6 8.3 %gather_fusion = bf16[128,384,128]{2,1,0:T(8,128)(2,1)} fusion(bf16[16,384,128]{2,1,0:T(8,128)(2,1)S(1)} %pad_maximum_fusion, s32[1024]{0:T(1024)S(1)} %pad_clamp_fusion.1), kind=kCustom, calls=%fused_computation | custom fusion | bytes 25166336 | tf_op jit(solution)/shard_map/gather | solution.py:32
  31.9 0.0 copy-start.3
  31.9 5.7 %all-to-all-start.1 = ((bf16[128,384,128]{2,1,0:T(8,128)(2,1)}), bf16[128,384,128]{2,1,0:T(8,128)(2,1)}, u32[]{:S(2)}, u32[]{:S(2)}) async-start(bf16[128,384,128]{2,1,0:T(8,128)(2,1)} %gather_fusion), calls=%async_computation.1 | async-start | bytes 25165824 | tf_op jit(solution)/shard_map/all_to_all | solution.py:33
  37.7 0.0 copy-done
  37.7 0.0 copy-done.3
  37.7 14.5 %fusion.19 = f32[16,128,128]{2,1,0:T(8,128)S(1)} fusion(bf16[40,128,128]{2,1,0:T(8,128)(2,1)S(1)} %copy-done, bf16[16,128,128]{2,1,0:T(8,128)(2,1)S(1)} %copy-done.3), kind=kOutput, calls=%fused_computation.13 | convolution fusion | flops 5379194880 | bytes 2883584 | tf_op jit(solution)/shard_map/pqce,qfe->pcf/dot_general | solution.py:38
  52.2 261.2 %all-to-all-done.1 = bf16[128,384,128]{2,1,0:T(8,128)(2,1)} async-done(((bf16[128,384,128]{2,1,0:T(8,128)(2,1)}), bf16[128,384,128]{2,1,0:T(8,128)(2,1)}, u32[]{:S(2)}, u32[]{:S(2)}) %all-to-all-start.1) | async-done | bytes 12582944 | tf_op jit(solution)/shard_map/all_to_all | solution.py:33
  313.4 12.0 %gather_fusion.1 = bf16[96,384,128]{2,1,0:T(8,128)(2,1)} fusion(bf16[128,384,128]{2,1,0:T(8,128)(2,1)} %all-to-all-done.1, s32[1024]{0:T(1024)S(1)} %pad_clamp_fusion), kind=kCustom, calls=%fused_computation.1 | custom fusion | bytes 18874752 | tf_op jit(solution)/shard_map/gather | solution.py:43
  325.4 0.0 copy-start.1
  325.4 0.0 copy-start.2
  325.4 3.7 copy-done.1
  329.0 0.0 slice-start
  329.0 1.9 slice.13
  330.9 0.0 copy-done.2
  330.9 2.1 slice-done
  333.0 3.7 fusion.31
  336.7 6.8 %fusion.24 = f32[16,128,128]{2,1,0:T(8,128)} fusion(f32[16,128,128]{2,1,0:T(8,128)S(1)} %fusion.19, bf16[16,6,128,128]{3,2,1,0:T(8,128)(2,1)} %fusion.31, bf16[16,6,128,128]{3,2,1,0:T(8,128)(2,1)} %bitcast.57), kind=kOutput, calls=%fused_computation.15 | convolution fusion | flops 807141376 | bytes 8388608 | tf_op jit(solution)/shard_map/plce,plfe->pcf/dot_general | solution.py:52
  343.5 0.0 copy-start.4
  343.5 0.0 copy-start.5
  343.5 10.2 %all-to-all-start.2 = ((f32[8,2,128,128]{3,2,1,0:T(8,128)}), f32[8,2,128,128]{3,2,1,0:T(8,128)S(1)}, u32[]{:S(2)}, u32[]{:S(2)}) async-start(f32[8,2,128,128]{3,2,1,0:T(8,128)} %bitcast.18), calls=%async_computation.2 | async-start | bytes 2097152 | tf_op jit(solution)/shard_map/all_to_all | solution.py:60
  353.7 29.3 %all-to-all-done.2 = f32[8,2,128,128]{3,2,1,0:T(8,128)S(1)} async-done(((f32[8,2,128,128]{3,2,1,0:T(8,128)}), f32[8,2,128,128]{3,2,1,0:T(8,128)S(1)}, u32[]{:S(2)}, u32[]{:S(2)}) %all-to-all-start.2) | async-done | bytes 1048608 | tf_op jit(solution)/shard_map/all_to_all | solution.py:60
  383.0 0.1 reduce_sum.32
  383.0 0.0 copy-done.4
  383.0 0.0 copy-done.5
  383.1 1.6 divide_subtract_fusion
  (3 shorter events, 0.0 us)
Async XLA Ops:
  0.0 37.7 %copy-start = (bf16[40,128,128]{2,1,0:T(8,128)(2,1)S(1)}, bf16[40,128,128]{2,1,0:T(8,128)(2,1)}, u32[]{:S(2)}) copy-start(bf16[40,128,128]{2,1,0:T(8,128)(2,1)} %param.9) | copy-start | bytes 3932164
  2.5 20.8 %all-to-all-start = ((s32[64,1,2]{2,1,0:T(1,128)}), s32[64,1,2]{2,1,0:T(1,128)S(1)}, u32[]{:S(2)}, u32[]{:S(2)}) async-start(s32[64,1,2]{2,1,0:T(1,128)} %bitcast.4), calls=%async_computation | async-start | bytes 65536 | tf_op jit(solution)/shard_map/all_to_all | solution.py:27
  31.9 5.7 %copy-start.3 = (bf16[16,128,128]{2,1,0:T(8,128)(2,1)S(1)}, bf16[16,128,128]{2,1,0:T(8,128)(2,1)}, u32[]{:S(2)}) copy-start(bf16[16,128,128]{2,1,0:T(8,128)(2,1)} %param.7) | copy-start | bytes 1572868
  31.9 281.4 %all-to-all-start.1 = ((bf16[128,384,128]{2,1,0:T(8,128)(2,1)}), bf16[128,384,128]{2,1,0:T(8,128)(2,1)}, u32[]{:S(2)}, u32[]{:S(2)}) async-start(bf16[128,384,128]{2,1,0:T(8,128)(2,1)} %gather_fusion), calls=%async_computation.1 | async-start | bytes 25165824 | tf_op jit(solution)/shard_map/all_to_all | solution.py:33
  325.4 3.7 copy-start.1
  325.4 5.5 %copy-start.2 = (bf16[16,256,128]{2,1,0:T(8,128)(2,1)S(1)}, bf16[16,256,128]{2,1,0:T(8,128)(2,1)}, u32[]{:S(2)}) copy-start(bf16[16,256,128]{2,1,0:T(8,128)(2,1)} %param.8) | copy-start | bytes 3145732
  329.0 4.0 %slice-start = ((bf16[96,384,128]{2,1,0:T(8,128)(2,1)}), bf16[96,256,128]{2,1,0:T(8,128)(2,1)S(1)}, s32[]{:S(2)}) async-start(bf16[96,384,128]{2,1,0:T(8,128)(2,1)} %gather_fusion.1), calls=%async_computation.3 | async-start | bytes 12582912 | tf_op jit(solution)/shard_map/slice | solution.py:44
  343.5 39.5 %copy-start.4 = (bf16[2,128,128]{2,1,0:T(8,128)(2,1)S(1)}, bf16[2,128,128]{2,1,0:T(8,128)(2,1)}, u32[]{:S(2)}) copy-start(bf16[2,128,128]{2,1,0:T(8,128)(2,1)} %param.10) | copy-start | bytes 196612
  343.5 39.5 %copy-start.5 = (f32[2,128]{1,0:T(2,128)S(1)}, f32[2,128]{1,0:T(2,128)}, u32[]{:S(2)}) copy-start(f32[2,128]{1,0:T(2,128)} %param.11) | copy-start | bytes 3076
  343.5 39.5 %all-to-all-start.2 = ((f32[8,2,128,128]{3,2,1,0:T(8,128)}), f32[8,2,128,128]{3,2,1,0:T(8,128)S(1)}, u32[]{:S(2)}, u32[]{:S(2)}) async-start(f32[8,2,128,128]{3,2,1,0:T(8,128)} %bitcast.18), calls=%async_computation.2 | async-start | bytes 2097152 | tf_op jit(solution)/shard_map/all_to_all | solution.py:60

commit v3 on v2

--- a/solution.py
+++ b/solution.py
@@ -38,7 +38,7 @@
     ladder = jnp.einsum(
         "pqce,qfe->pcf", ladder_half, ladder_ints, preferred_element_type=jnp.float32
     )
-    ladder = lax.optimization_barrier(ladder)
+    ladder_mine = lax.psum_scatter(ladder, "aux", scatter_dimension=0, tiled=True)
 
     rows = flat[bucket]
     coef_q = rows[:, :pao_width].reshape(pair_dev, per_slice, pao_width, pno_width)
@@ -53,12 +53,13 @@
         "plce,plfe->pcf", halfway, intersection, preferred_element_type=jnp.float32
     )
 
-    partial_value = linked + ladder
     aux_count = lax.axis_size("aux")
-    pieces = partial_value.reshape(aux_count, own_rows, pno_width, pno_width)
-    reduced = jnp.sum(
-        lax.all_to_all(pieces, "aux", split_axis=0, concat_axis=0, tiled=True), axis=0
+    pieces = linked.astype(jnp.bfloat16).reshape(aux_count, own_rows, pno_width, pno_width)
+    linked_mine = jnp.sum(
+        lax.all_to_all(pieces, "aux", split_axis=0, concat_axis=0, tiled=True).astype(jnp.float32),
+        axis=0,
     )
+    reduced = ladder_mine + linked_mine
     first_row = lax.axis_index("aux") * own_rows
     amp_mine = lax.dynamic_slice_in_dim(amplitudes, first_row, own_rows, 0)
     residual = coulomb_ints.astype(jnp.float32) + reduced

time: 385 us -> 387 us (level)
  between operations: 0.11 us -> 13.5 us
  waiting for transfers between devices: 298 us -> 286 us
    all_to_all x1, waiting for transfers between devices: 29.3 us -> 18.1 us  [local(): lax.all_to_all(pieces, 'aux', split_axis=0, concat_axis=0, tiled=True)]
  transfers between devices with their start and end apart: 3 -> 4, of which waited for: 3 -> 3; matrix products, arithmetic and copies ran while one was open for 4% -> 11% of each run, Pallas kernels for 0% -> 0%
where the time goes in v3:
time: 387 us
  waiting for transfers between devices  286 us (74%)
  local copies, waits for them, and re-layouts  28.6 us (7%)
  starting transfers between devices  27.8 us (7%)
  matrix products  25.5 us (7%)
  between operations  13.5 us (3%)
  other arithmetic  5.11 us (1%)
    all_to_all x1, waiting for transfers between devices, local(): lax.all_to_all(items, 'pairs', split_axis=0, concat_axis=0, tiled=True)  260 us
    all_to_all x1, waiting for transfers between devices, local(): lax.all_to_all(pieces, 'aux', split_axis=0, concat_axis=0, tiled=True)  18.1 us
    dot_general x1, matrix products, local(): jnp.einsum('pqce,qfe->pcf', ladder_half, ladder_ints, preferred_element_t...  15.3 us
    gather x1, local copies, waits for them, and re-layouts, local(): rows = flat[bucket]  12 us
    all_to_all x1, starting transfers between devices, local(): lax.all_to_all(wanted.reshape(groups, capacity), 'pairs', split_axis=0, c...  11.6 us
    all_to_all x1, starting transfers between devices, local(): lax.all_to_all(pieces, 'aux', split_axis=0, concat_axis=0, tiled=True)  10 us
    gather x1, local copies, waits for them, and re-layouts, local(): items = both[picked.reshape(groups * capacity)]  8.07 us
  transfers between devices with their start and end apart: 4, of which 3 were waited for; matrix products, arithmetic and copies ran while one was open for 11% of the time, Pallas kernels for 0%

profile of v3, /device:TPU:1, one launch (start us, length us, event | category | flops | bytes accessed | tf_op | source)
XLA Modules:
  0.0 386.5 jit_solution(11911031775581852522)
XLA Ops:
  6.5 0.0 copy-start
  6.5 1.0 convert_reduce_fusion.1
  7.5 0.7 fusion.36
  8.2 0.1 select_reduce_fusion
  8.3 0.8 sub.10
  9.1 11.6 %all-to-all-start = ((s32[64,1,2]{2,1,0:T(1,128)}), s32[64,1,2]{2,1,0:T(1,128)S(1)}, u32[]{:S(2)}, u32[]{:S(2)}) async-start(s32[64,1,2]{2,1,0:T(1,128)} %bitcast.9), calls=%async_computation.1 | async-start | bytes 65536 | tf_op jit(solution)/shard_map/all_to_all | solution.py:27
  20.7 1.5 pad_maximum_fusion
  22.2 7.7 %all-to-all-done = s32[64,1,2]{2,1,0:T(1,128)S(1)} async-done(((s32[64,1,2]{2,1,0:T(1,128)}), s32[64,1,2]{2,1,0:T(1,128)S(1)}, u32[]{:S(2)}, u32[]{:S(2)}) %all-to-all-start) | async-done | bytes 544 | tf_op jit(solution)/shard_map/all_to_all | solution.py:27
  29.9 0.1 maximum_reduce_fusion
  30.0 0.1 reshape.49
  30.2 8.1 %gather_fusion = bf16[128,384,128]{2,1,0:T(8,128)(2,1)} fusion(bf16[16,384,128]{2,1,0:T(8,128)(2,1)S(1)} %pad_maximum_fusion, s32[1024]{0:T(1024)S(1)} %pad_clamp_fusion.1), kind=kCustom, calls=%fused_computation | custom fusion | bytes 25166336 | tf_op jit(solution)/shard_map/gather | solution.py:32
  38.2 0.0 copy-start.3
  38.2 5.9 %all-to-all-start.1 = ((bf16[128,384,128]{2,1,0:T(8,128)(2,1)}), bf16[128,384,128]{2,1,0:T(8,128)(2,1)}, u32[]{:S(2)}, u32[]{:S(2)}) async-start(bf16[128,384,128]{2,1,0:T(8,128)(2,1)} %gather_fusion), calls=%async_computation.2 | async-start | bytes 25165824 | tf_op jit(solution)/shard_map/all_to_all | solution.py:33
  44.2 0.2 reduce-scatter.2.cloned.1.call-start
  44.4 0.0 copy-done
  44.4 0.0 copy-done.3
  44.4 15.3 %fusion.19 = f32[16,128,128]{2,1,0:T(8,128)} fusion(bf16[40,128,128]{2,1,0:T(8,128)(2,1)S(1)} %copy-done, bf16[16,128,128]{2,1,0:T(8,128)(2,1)S(1)} %copy-done.3), kind=kOutput, calls=%fused_computation.13 | convolution fusion | flops 5379194880 | bytes 2883584 | tf_op jit(solution)/shard_map/pqce,qfe->pcf/dot_general | solution.py:38
  59.7 0.0 reduce-scatter.2.cloned.1.call-update
  59.7 260.2 %all-to-all-done.1 = bf16[128,384,128]{2,1,0:T(8,128)(2,1)} async-done(((bf16[128,384,128]{2,1,0:T(8,128)(2,1)}), bf16[128,384,128]{2,1,0:T(8,128)(2,1)}, u32[]{:S(2)}, u32[]{:S(2)}) %all-to-all-start.1) | async-done | bytes 12582944 | tf_op jit(solution)/shard_map/all_to_all | solution.py:33
  319.9 12.0 %gather_fusion.1 = bf16[96,384,128]{2,1,0:T(8,128)(2,1)} fusion(bf16[128,384,128]{2,1,0:T(8,128)(2,1)} %all-to-all-done.1, s32[1024]{0:T(1024)S(1)} %pad_clamp_fusion), kind=kCustom, calls=%fused_computation.1 | custom fusion | bytes 18874752 | tf_op jit(solution)/shard_map/gather | solution.py:43
  331.9 0.0 copy-start.1
  331.9 0.0 copy-start.2
  331.9 3.7 copy-done.1
  335.6 0.0 slice-start
  335.6 1.9 slice.13
  337.4 0.0 copy-done.2
  337.4 2.1 slice-done
  339.5 3.7 fusion.31
  343.2 0.0 copy-start.4
  343.2 0.0 copy-start.5
  343.2 6.6 %fusion.24 = bf16[16,128,128]{2,1,0:T(8,128)(2,1)} fusion(bf16[16,6,128,128]{3,2,1,0:T(8,128)(2,1)} %fusion.31, bf16[16,6,128,128]{3,2,1,0:T(8,128)(2,1)} %bitcast.57), kind=kOutput, calls=%fused_computation.15 | convolution fusion | flops 807141376 | bytes 6815744 | tf_op jit(solution)/shard_map/plce,plfe->pcf/dot_general | solution.py:52
  349.8 10.0 %all-to-all-start.2 = ((bf16[8,2,128,128]{3,2,1,0:T(8,128)(2,1)}), bf16[8,2,128,128]{3,2,1,0:T(8,128)(2,1)S(1)}, u32[]{:S(2)}, u32[]{:S(2)}) async-start(bf16[8,2,128,128]{3,2,1,0:T(8,128)(2,1)} %bitcast.18), calls=%async_computation.3 | async-start | bytes 1048576 | tf_op jit(solution)/shard_map/all_to_all | solution.py:59
  359.8 18.1 %all-to-all-done.2 = bf16[8,2,128,128]{3,2,1,0:T(8,128)(2,1)S(1)} async-done(((bf16[8,2,128,128]{3,2,1,0:T(8,128)(2,1)}), bf16[8,2,128,128]{3,2,1,0:T(8,128)(2,1)S(1)}, u32[]{:S(2)}, u32[]{:S(2)}) %all-to-all-start.2) | async-done | bytes 524320 | tf_op jit(solution)/shard_map/all_to_all | solution.py:59
  377.9 0.1 convert_reduce_fusion
  378.0 0.0 reduce-scatter.2.cloned.1.call-done
  378.0 0.0 copy-done.4
  378.0 0.0 copy-done.5
  378.0 1.7 divide_subtract_fusion
  (3 shorter events, 0.0 us)
Async XLA Ops:
  6.5 37.9 %copy-start = (bf16[40,128,128]{2,1,0:T(8,128)(2,1)S(1)}, bf16[40,128,128]{2,1,0:T(8,128)(2,1)}, u32[]{:S(2)}) copy-start(bf16[40,128,128]{2,1,0:T(8,128)(2,1)} %param.9) | copy-start | bytes 3932164
  9.1 20.8 %all-to-all-start = ((s32[64,1,2]{2,1,0:T(1,128)}), s32[64,1,2]{2,1,0:T(1,128)S(1)}, u32[]{:S(2)}, u32[]{:S(2)}) async-start(s32[64,1,2]{2,1,0:T(1,128)} %bitcast.9), calls=%async_computation.1 | async-start | bytes 65536 | tf_op jit(solution)/shard_map/all_to_all | solution.py:27
  38.2 6.2 %copy-start.3 = (bf16[16,128,128]{2,1,0:T(8,128)(2,1)S(1)}, bf16[16,128,128]{2,1,0:T(8,128)(2,1)}, u32[]{:S(2)}) copy-start(bf16[16,128,128]{2,1,0:T(8,128)(2,1)} %param.7) | copy-start | bytes 1572868
  38.2 281.7 %all-to-all-start.1 = ((bf16[128,384,128]{2,1,0:T(8,128)(2,1)}), bf16[128,384,128]{2,1,0:T(8,128)(2,1)}, u32[]{:S(2)}, u32[]{:S(2)}) async-start(bf16[128,384,128]{2,1,0:T(8,128)(2,1)} %gather_fusion), calls=%async_computation.2 | async-start | bytes 25165824 | tf_op jit(solution)/shard_map/all_to_all | solution.py:33
  44.2 333.8 %reduce-scatter.2.cloned.1.call-start = ((), (), s32[]{:S(2)}) async-start(), calls=%async_computation.4 | async-start | bytes 1179648 | tf_op jit(solution)/shard_map/reduce_scatter | solution.py:41
  331.9 3.7 copy-start.1
  331.9 5.5 %copy-start.2 = (bf16[16,256,128]{2,1,0:T(8,128)(2,1)S(1)}, bf16[16,256,128]{2,1,0:T(8,128)(2,1)}, u32[]{:S(2)}) copy-start(bf16[16,256,128]{2,1,0:T(8,128)(2,1)} %param.8) | copy-start | bytes 3145732
  335.6 4.0 %slice-start = ((bf16[96,384,128]{2,1,0:T(8,128)(2,1)}), bf16[96,256,128]{2,1,0:T(8,128)(2,1)S(1)}, s32[]{:S(2)}) async-start(bf16[96,384,128]{2,1,0:T(8,128)(2,1)} %gather_fusion.1), calls=%async_computation.5 | async-start | bytes 12582912 | tf_op jit(solution)/shard_map/slice | solution.py:44
  343.2 34.8 %copy-start.4 = (bf16[2,128,128]{2,1,0:T(8,128)(2,1)S(1)}, bf16[2,128,128]{2,1,0:T(8,128)(2,1)}, u32[]{:S(2)}) copy-start(bf16[2,128,128]{2,1,0:T(8,128)(2,1)} %param.10) | copy-start | bytes 196612
  343.2 34.8 %copy-start.5 = (f32[2,128]{1,0:T(2,128)S(1)}, f32[2,128]{1,0:T(2,128)}, u32[]{:S(2)}) copy-start(f32[2,128]{1,0:T(2,128)} %param.11) | copy-start | bytes 3076
  349.8 28.1 %all-to-all-start.2 = ((bf16[8,2,128,128]{3,2,1,0:T(8,128)(2,1)}), bf16[8,2,128,128]{3,2,1,0:T(8,128)(2,1)S(1)}, u32[]{:S(2)}, u32[]{:S(2)}) async-start(bf16[8,2,128,128]{3,2,1,0:T(8,128)(2,1)} %bitcast.18), calls=%async_computation.3 | async-start | bytes 1048576 | tf_op jit(solution)/shard_map/all_to_all | solution.py:59
Sparse Core Ops, SparseCore 0:
  59.8 42.5 reduce-scatter.1

commit v4 on v3

--- a/solution.py
+++ b/solution.py
@@ -1,7 +1,52 @@
 import jax
 import jax.numpy as jnp
 from jax import lax
+from jax.experimental import pallas as pl
+from jax.experimental.pallas import tpu as pltpu
 from jax.sharding import PartitionSpec as P
+
+
+def linked_kernel(links, pao_width, bucket_ref, coef_t_ref, *refs):
+    slot_refs, out_ref = refs[:links], refs[links]
+    coef_t = coef_t_ref[0]
+    total = None
+    for slot_ref in slot_refs:
+        coef_q = slot_ref[0, :pao_width, :]
+        amp_q = slot_ref[0, pao_width:, :]
+        overlap = jnp.dot(coef_t, coef_q, preferred_element_type=jnp.float32).astype(jnp.bfloat16)
+        half = jnp.dot(overlap, amp_q, preferred_element_type=jnp.float32).astype(jnp.bfloat16)
+        term = lax.dot_general(
+            half, overlap, (((1,), (1,)), ((), ())), preferred_element_type=jnp.float32
+        )
+        total = term if total is None else total + term
+    out_ref[0] = total.astype(out_ref.dtype)
+
+
+def linked_sum(bucket, coef_t, flat, links):
+    pair_dev, pno_width, pao_width = coef_t.shape
+    row_width = flat.shape[1]
+
+    def slot_spec(j):
+        return pl.BlockSpec((1, row_width, pno_width), lambda p, b: (b[p * links + j], 0, 0))
+
+    grid_spec = pltpu.PrefetchScalarGridSpec(
+        num_scalar_prefetch=1,
+        grid=(pair_dev,),
+        in_specs=[pl.BlockSpec((1, pno_width, pao_width), lambda p, b: (p, 0, 0))]
+        + [slot_spec(j) for j in range(links)],
+        out_specs=pl.BlockSpec((1, pno_width, pno_width), lambda p, b: (p, 0, 0)),
+    )
+    flops = pair_dev * links * 2 * pno_width * pno_width * (pao_width + 2 * pno_width)
+    return pl.pallas_call(
+        lambda *r: linked_kernel(links, pao_width, *r),
+        grid_spec=grid_spec,
+        out_shape=jax.ShapeDtypeStruct((pair_dev, pno_width, pno_width), jnp.bfloat16),
+        cost_estimate=pl.CostEstimate(
+            flops=flops,
+            bytes_accessed=pair_dev * (links * row_width + pao_width + pno_width) * pno_width * 2,
+            transcendentals=0,
+        ),
+    )(bucket, coef_t, *([flat] * links))
 
 
 def local(amplitudes, pno_coef, ladder_ints, coulomb_ints, pno_energy, link_owner, link_local):
@@ -40,21 +85,11 @@
     )
     ladder_mine = lax.psum_scatter(ladder, "aux", scatter_dimension=0, tiled=True)
 
-    rows = flat[bucket]
-    coef_q = rows[:, :pao_width].reshape(pair_dev, per_slice, pao_width, pno_width)
-    amp_q = rows[:, pao_width:].reshape(pair_dev, per_slice, pno_width, pno_width)
-    intersection = jnp.einsum(
-        "pac,plad->plcd", pno_coef, coef_q, preferred_element_type=jnp.float32
-    ).astype(jnp.bfloat16)
-    halfway = jnp.einsum(
-        "plcd,plde->plce", intersection, amp_q, preferred_element_type=jnp.float32
-    ).astype(jnp.bfloat16)
-    linked = jnp.einsum(
-        "plce,plfe->pcf", halfway, intersection, preferred_element_type=jnp.float32
-    )
+    coef_t = jnp.transpose(pno_coef, (0, 2, 1))
+    linked = linked_sum(bucket, coef_t, flat, per_slice)
 
     aux_count = lax.axis_size("aux")
-    pieces = linked.astype(jnp.bfloat16).reshape(aux_count, own_rows, pno_width, pno_width)
+    pieces = linked.reshape(aux_count, own_rows, pno_width, pno_width)
     linked_mine = jnp.sum(
         lax.all_to_all(pieces, "aux", split_axis=0, concat_axis=0, tiled=True).astype(jnp.float32),
         axis=0,

time: 387 us -> 378 us (0.977)
  Pallas kernels: 0 us -> 20.8 us
  local copies, waits for them, and re-layouts: 28.6 us -> 11.5 us
  matrix products: 25.5 us -> 15.3 us
    pallas_call x0 -> x1, Pallas kernels: none -> 20.8 us  [linked_sum(): pl.pallas_call(lambda *r: linked_kernel(links, pao_width, *r), grid_spec=...]
    gather x1 -> x0, local copies, waits for them, and re-layouts: 12 us -> none  [local(): rows = flat[bucket]]
    dot_general x2 -> x0, matrix products: 10.3 us -> none  [the longest x1 6.6 us: local(): jnp.einsum('plce,plfe->pcf', halfway, intersection, preferred_element_typ...]
    slice x3 -> x0, local copies, waits for them, and re-layouts: 3.97 us -> none  [the longest x2 2.11 us: local(): rows[:, :pao_width].reshape(pair_dev, per_slice, pao_width, pno_width)]
  transfers between devices with their start and end apart: 4 -> 4, of which waited for: 3 -> 3; matrix products, arithmetic and copies ran while one was open for 11% -> 5% of each run, Pallas kernels for 0% -> 6%
where the time goes in v4:
time: 378 us
  waiting for transfers between devices  283 us (75%)
  starting transfers between devices  27.8 us (7%)
  Pallas kernels  20.8 us (6%)
  matrix products  15.3 us (4%)
  between operations  13.5 us (4%)
  local copies, waits for them, and re-layouts  11.5 us (3%)
  other arithmetic  5.62 us (1%)
    all_to_all x1, waiting for transfers between devices, local(): lax.all_to_all(items, 'pairs', split_axis=0, concat_axis=0, tiled=True)  257 us
    pallas_call x1, Pallas kernels, linked_sum(): pl.pallas_call(lambda *r: linked_kernel(links, pao_width, *r), grid_spec=...  20.8 us
    all_to_all x1, waiting for transfers between devices, local(): lax.all_to_all(pieces, 'aux', split_axis=0, concat_axis=0, tiled=True)  18.1 us
    dot_general x1, matrix products, local(): jnp.einsum('pqce,qfe->pcf', ladder_half, ladder_ints, preferred_element_t...  15.3 us
    all_to_all x1, starting transfers between devices, local(): lax.all_to_all(wanted.reshape(groups, capacity), 'pairs', split_axis=0, c...  11.6 us
    all_to_all x1, starting transfers between devices, local(): lax.all_to_all(pieces, 'aux', split_axis=0, concat_axis=0, tiled=True)  10.2 us
    gather x1, local copies, waits for them, and re-layouts, local(): items = both[picked.reshape(groups * capacity)]  8.06 us
    all_to_all x1, waiting for transfers between devices, local(): lax.all_to_all(wanted.reshape(groups, capacity), 'pairs', split_axis=0, c...  7.7 us
  transfers between devices with their start and end apart: 4, of which 3 were waited for; matrix products, arithmetic and copies ran while one was open for 5% of the time, Pallas kernels for 6%

profile of v4, /device:TPU:1, one launch (start us, length us, event | category | flops | bytes accessed | tf_op | source)
XLA Modules:
  0.0 377.6 jit_solution(2884195017822039961)
XLA Ops:
  6.5 0.0 copy-start
  6.5 1.0 convert_reduce_fusion.1
  7.5 0.7 fusion.13
  8.2 0.1 select_reduce_fusion
  8.3 0.8 sub.10
  9.1 11.6 %all-to-all-start = ((s32[64,1,2]{2,1,0:T(1,128)}), s32[64,1,2]{2,1,0:T(1,128)S(1)}, u32[]{:S(2)}, u32[]{:S(2)}) async-start(s32[64,1,2]{2,1,0:T(1,128)} %bitcast.10), calls=%async_computation.1 | async-start | bytes 65536 | tf_op jit(solution)/shard_map/all_to_all | solution.py:72
  20.7 1.5 pad_maximum_fusion
  22.2 7.7 %all-to-all-done = s32[64,1,2]{2,1,0:T(1,128)S(1)} async-done(((s32[64,1,2]{2,1,0:T(1,128)}), s32[64,1,2]{2,1,0:T(1,128)S(1)}, u32[]{:S(2)}, u32[]{:S(2)}) %all-to-all-start) | async-done | bytes 544 | tf_op jit(solution)/shard_map/all_to_all | solution.py:72
  29.9 0.1 maximum_reduce_fusion
  30.0 0.1 reshape.40
  30.2 8.1 %gather_fusion = bf16[128,384,128]{2,1,0:T(8,128)(2,1)} fusion(bf16[16,384,128]{2,1,0:T(8,128)(2,1)S(1)} %pad_maximum_fusion, s32[1024]{0:T(1024)S(1)} %pad_clamp_fusion), kind=kCustom, calls=%fused_computation | custom fusion | bytes 25166336 | tf_op jit(solution)/shard_map/gather | solution.py:77
  38.2 0.0 copy-start.2
  38.2 5.9 %all-to-all-start.1 = ((bf16[128,384,128]{2,1,0:T(8,128)(2,1)}), bf16[128,384,128]{2,1,0:T(8,128)(2,1)}, u32[]{:S(2)}, u32[]{:S(2)}) async-start(bf16[128,384,128]{2,1,0:T(8,128)(2,1)} %gather_fusion), calls=%async_computation.2 | async-start | bytes 25165824 | tf_op jit(solution)/shard_map/all_to_all | solution.py:78
  44.1 0.0 reduce-scatter.2.cloned.1.call-start
  44.2 0.0 copy-done
  44.2 0.0 copy-done.2
  44.2 15.3 %fusion.5 = f32[16,128,128]{2,1,0:T(8,128)} fusion(bf16[40,128,128]{2,1,0:T(8,128)(2,1)S(1)} %copy-done, bf16[16,128,128]{2,1,0:T(8,128)(2,1)S(1)} %copy-done.2), kind=kOutput, calls=%fused_computation.6 | convolution fusion | flops 5379194880 | bytes 2883584 | tf_op jit(solution)/shard_map/pqce,qfe->pcf/dot_general | solution.py:83
  59.5 0.0 copy-start.1
  59.5 0.0 copy-start.5
  59.5 0.0 reduce-scatter.2.cloned.1.call-update
  59.6 1.2 copy-done.1
  60.8 1.3 copy.16
  62.1 0.0 copy-done.5
  62.1 0.5 multiply_add_fusion.r_0_
  62.6 257.3 %all-to-all-done.1.r_2_.r_3_.r_4_.r_5_.r_6_.r_7_ = bf16[128,384,128]{2,1,0:T(8,128)(2,1)} async-done(((bf16[128,384,128]{2,1,0:T(8,128)(2,1)}), bf16[128,384,128]{2,1,0:T(8,128)(2,1)}, u32[]{:S(2)}, u32[]{:S(2)}) %all-to-all-start.1) | async-done | bytes 12582944 | tf_op jit(solution)/shard_map/all_to_all | solution.py:78
  319.9 20.8 %shard_map.73 = bf16[16,128,128]{2,1,0:T(8,128)(2,1)} custom-call(s32[96]{0:T(128)} %multiply_add_fusion.r_0_, bf16[16,128,256]{2,1,0:T(8,128)(2,1)} %bitcast.31, bf16[128,384,128]{2,1,0:T(8,128)(2,1)} %all-to-all-done.1.r_2_.r_3_.r_4_.r_5_.r_6_.r_7_, bf16[128,384,128]{2,1,0:T(8,128)(2,1)} %all-to-all-done.1.r_2_.r_3_.r_4_.r_5_.r_6_.r_7_, ...), custom_call_target="tpu_custom_call" | custom-call | flops 1610612736 | bytes 11010048 | tf_op jit(solution)/shard_map/pallas_call | solution.py:40
  340.7 0.0 copy-start.3
  340.7 0.0 copy-start.4
  340.7 10.2 %all-to-all-start.2 = ((bf16[8,2,128,128]{3,2,1,0:T(8,128)(2,1)}), bf16[8,2,128,128]{3,2,1,0:T(8,128)(2,1)S(1)}, u32[]{:S(2)}, u32[]{:S(2)}) async-start(bf16[8,2,128,128]{3,2,1,0:T(8,128)(2,1)} %bitcast.32), calls=%async_computation.3 | async-start | bytes 1048576 | tf_op jit(solution)/shard_map/all_to_all | solution.py:94
  350.9 18.1 %all-to-all-done.2 = bf16[8,2,128,128]{3,2,1,0:T(8,128)(2,1)S(1)} async-done(((bf16[8,2,128,128]{3,2,1,0:T(8,128)(2,1)}), bf16[8,2,128,128]{3,2,1,0:T(8,128)(2,1)S(1)}, u32[]{:S(2)}, u32[]{:S(2)}) %all-to-all-start.2) | async-done | bytes 524320 | tf_op jit(solution)/shard_map/all_to_all | solution.py:94
  368.9 0.1 convert_reduce_fusion
  369.0 0.0 reduce-scatter.2.cloned.1.call-done
  369.0 0.0 copy-done.3
  369.0 0.0 copy-done.4
  369.1 1.7 divide_subtract_fusion
  (2 shorter events, 0.0 us)
Async XLA Ops:
  6.5 37.7 %copy-start = (bf16[40,128,128]{2,1,0:T(8,128)(2,1)S(1)}, bf16[40,128,128]{2,1,0:T(8,128)(2,1)}, u32[]{:S(2)}) copy-start(bf16[40,128,128]{2,1,0:T(8,128)(2,1)} %param.9) | copy-start | bytes 3932164
  9.1 20.8 %all-to-all-start = ((s32[64,1,2]{2,1,0:T(1,128)}), s32[64,1,2]{2,1,0:T(1,128)S(1)}, u32[]{:S(2)}, u32[]{:S(2)}) async-start(s32[64,1,2]{2,1,0:T(1,128)} %bitcast.10), calls=%async_computation.1 | async-start | bytes 65536 | tf_op jit(solution)/shard_map/all_to_all | solution.py:72
  38.2 6.0 %copy-start.2 = (bf16[16,128,128]{2,1,0:T(8,128)(2,1)S(1)}, bf16[16,128,128]{2,1,0:T(8,128)(2,1)}, u32[]{:S(2)}) copy-start(bf16[16,128,128]{2,1,0:T(8,128)(2,1)} %param.7) | copy-start | bytes 1572868
  38.2 281.6 %all-to-all-start.1 = ((bf16[128,384,128]{2,1,0:T(8,128)(2,1)}), bf16[128,384,128]{2,1,0:T(8,128)(2,1)}, u32[]{:S(2)}, u32[]{:S(2)}) async-start(bf16[128,384,128]{2,1,0:T(8,128)(2,1)} %gather_fusion), calls=%async_computation.2 | async-start | bytes 25165824 | tf_op jit(solution)/shard_map/all_to_all | solution.py:78
  44.1 324.9 %reduce-scatter.2.cloned.1.call-start = ((), (), s32[]{:S(2)}) async-start(), calls=%async_computation.4 | async-start | bytes 1179648 | tf_op jit(solution)/shard_map/reduce_scatter | solution.py:86
  59.5 1.2 copy-start.1
  59.5 2.5 copy-start.5
  340.7 28.4 %copy-start.3 = (bf16[2,128,128]{2,1,0:T(8,128)(2,1)S(1)}, bf16[2,128,128]{2,1,0:T(8,128)(2,1)}, u32[]{:S(2)}) copy-start(bf16[2,128,128]{2,1,0:T(8,128)(2,1)} %param.10) | copy-start | bytes 196612
  340.7 28.4 %copy-start.4 = (f32[2,128]{1,0:T(2,128)S(1)}, f32[2,128]{1,0:T(2,128)}, u32[]{:S(2)}) copy-start(f32[2,128]{1,0:T(2,128)} %param.11) | copy-start | bytes 3076
  340.7 28.3 %all-to-all-start.2 = ((bf16[8,2,128,128]{3,2,1,0:T(8,128)(2,1)}), bf16[8,2,128,128]{3,2,1,0:T(8,128)(2,1)S(1)}, u32[]{:S(2)}, u32[]{:S(2)}) async-start(bf16[8,2,128,128]{3,2,1,0:T(8,128)(2,1)} %bitcast.32), calls=%async_computation.3 | async-start | bytes 1048576 | tf_op jit(solution)/shard_map/all_to_all | solution.py:94
Sparse Core Ops, SparseCore 0:
  59.7 42.6 reduce-scatter.1

commit v5 on v4

--- a/solution.py
+++ b/solution.py
@@ -83,12 +83,21 @@
     ladder = jnp.einsum(
         "pqce,qfe->pcf", ladder_half, ladder_ints, preferred_element_type=jnp.float32
     )
-    ladder_mine = lax.psum_scatter(ladder, "aux", scatter_dimension=0, tiled=True)
+    aux_count = lax.axis_size("aux")
+    aux_me = lax.axis_index("aux")
+    ladder_mine = lax.dynamic_slice_in_dim(ladder, aux_me * own_rows, own_rows, 0)
+    for shift in range(1, aux_count):
+        goes_to = lax.rem(aux_me + shift, aux_count)
+        piece = lax.dynamic_slice_in_dim(ladder, goes_to * own_rows, own_rows, 0)
+        ladder_mine = ladder_mine + lax.ppermute(
+            piece, "aux", [(i, (i + shift) % aux_count) for i in range(aux_count)]
+        )
+
+    flat, ladder_mine = lax.optimization_barrier((flat, ladder_mine))
 
     coef_t = jnp.transpose(pno_coef, (0, 2, 1))
     linked = linked_sum(bucket, coef_t, flat, per_slice)
 
-    aux_count = lax.axis_size("aux")
     pieces = linked.reshape(aux_count, own_rows, pno_width, pno_width)
     linked_mine = jnp.sum(
         lax.all_to_all(pieces, "aux", split_axis=0, concat_axis=0, tiled=True).astype(jnp.float32),

time: 378 us -> 365 us (0.966)
  waiting for transfers between devices: 283 us -> 234 us
  blocking collectives: 0 us -> 28.2 us
  starting transfers between devices: 27.8 us -> 48 us
  between operations: 13.5 us -> 0.25 us
    all_to_all x1, waiting for transfers between devices: 257 us -> 213 us  [local(): lax.all_to_all(items, 'pairs', split_axis=0, concat_axis=0, tiled=True)]
    ppermute x0 -> x7, starting transfers between devices: none -> 30.4 us  [local(): lax.ppermute(piece, 'aux', [(i, (i + shift) % aux_count) for i in range(a...]
    all_to_all x0 -> x1, blocking collectives: none -> 28.2 us  [local(): lax.all_to_all(pieces, 'aux', split_axis=0, concat_axis=0, tiled=True)]
    all_to_all x1 -> x0, waiting for transfers between devices: 18.1 us -> none  [local(): lax.all_to_all(pieces, 'aux', split_axis=0, concat_axis=0, tiled=True)]
    ppermute x0 -> x7, waiting for transfers between devices: none -> 14 us  [local(): lax.ppermute(piece, 'aux', [(i, (i + shift) % aux_count) for i in range(a...]
    all_to_all x1 -> x0, starting transfers between devices: 10.2 us -> none  [local(): lax.all_to_all(pieces, 'aux', split_axis=0, concat_axis=0, tiled=True)]
  transfers between devices with their start and end apart: 4 -> 9, of which waited for: 3 -> 5; matrix products, arithmetic and copies ran while one was open for 5% -> 5% of each run, Pallas kernels for 6% -> 0%
where the time goes in v5:
time: 365 us; the launch traced here: 364 us
  waiting for transfers between devices  234 us (64%)
  starting transfers between devices  48 us (13%)
  blocking collectives  28.2 us (8%)
  Pallas kernels  20.8 us (6%)
  matrix products  14.4 us (4%)
  local copies, waits for them, and re-layouts  11.5 us (3%)
  other arithmetic  6.78 us (2%)
    all_to_all x1, waiting for transfers between devices, local(): lax.all_to_all(items, 'pairs', split_axis=0, concat_axis=0, tiled=True)  213 us
    ppermute x7, starting transfers between devices, local(): lax.ppermute(piece, 'aux', [(i, (i + shift) % aux_count) for i in range(a...  30.4 us
    all_to_all x1, blocking collectives, local(): lax.all_to_all(pieces, 'aux', split_axis=0, concat_axis=0, tiled=True)  28.2 us
    pallas_call x1, Pallas kernels, linked_sum(): pl.pallas_call(lambda *r: linked_kernel(links, pao_width, *r), grid_spec=...  20.8 us
    dot_general x1, matrix products, local(): jnp.einsum('pqce,qfe->pcf', ladder_half, ladder_ints, preferred_element_t...  14.4 us
    ppermute x7, waiting for transfers between devices, local(): lax.ppermute(piece, 'aux', [(i, (i + shift) % aux_count) for i in range(a...  14 us
    all_to_all x1, starting transfers between devices, local(): lax.all_to_all(wanted.reshape(groups, capacity), 'pairs', split_axis=0, c...  11.6 us
    gather x1, local copies, waits for them, and re-layouts, local(): items = both[picked.reshape(groups * capacity)]  8.35 us
  transfers between devices with their start and end apart: 9, of which 5 were waited for; matrix products, arithmetic and copies ran while one was open for 5% of the time, Pallas kernels for 0%

profile of v5, /device:TPU:1, one launch (start us, length us, event | category | flops | bytes accessed | tf_op | source)
XLA Modules:
  0.0 364.3 jit_solution(17694249661473125105)
XLA Ops:
  0.0 0.0 copy-start
  0.0 1.0 convert_reduce_fusion.1
  1.0 0.7 fusion.13
  1.6 0.1 select_reduce_fusion
  1.8 0.8 sub.10
  2.5 11.6 %all-to-all-start = ((s32[64,1,2]{2,1,0:T(1,128)}), s32[64,1,2]{2,1,0:T(1,128)S(1)}, u32[]{:S(2)}, u32[]{:S(2)}) async-start(s32[64,1,2]{2,1,0:T(1,128)} %bitcast.4), calls=%async_computation | async-start | bytes 65536 | tf_op jit(solution)/shard_map/all_to_all | solution.py:72
  14.2 1.5 pad_maximum_fusion
  15.7 7.7 %all-to-all-done = s32[64,1,2]{2,1,0:T(1,128)S(1)} async-done(((s32[64,1,2]{2,1,0:T(1,128)}), s32[64,1,2]{2,1,0:T(1,128)S(1)}, u32[]{:S(2)}, u32[]{:S(2)}) %all-to-all-start) | async-done | bytes 544 | tf_op jit(solution)/shard_map/all_to_all | solution.py:72
  23.4 0.1 maximum_reduce_fusion
  23.5 0.1 reshape.40
  23.6 8.3 %gather_fusion = bf16[128,384,128]{2,1,0:T(8,128)(2,1)} fusion(bf16[16,384,128]{2,1,0:T(8,128)(2,1)S(1)} %pad_maximum_fusion, s32[1024]{0:T(1024)S(1)} %pad_clamp_fusion), kind=kCustom, calls=%fused_computation | custom fusion | bytes 25166336 | tf_op jit(solution)/shard_map/gather | solution.py:77
  32.0 0.0 copy-start.2
  32.0 5.9 %all-to-all-start.1 = ((bf16[128,384,128]{2,1,0:T(8,128)(2,1)}), bf16[128,384,128]{2,1,0:T(8,128)(2,1)}, u32[]{:S(2)}, u32[]{:S(2)}) async-start(bf16[128,384,128]{2,1,0:T(8,128)(2,1)} %gather_fusion), calls=%async_computation.1 | async-start | bytes 25165824 | tf_op jit(solution)/shard_map/all_to_all | solution.py:78
  38.0 0.0 copy-done
  38.0 0.0 copy-done.2
  38.0 14.4 %fusion.5 = f32[16,128,128]{2,1,0:T(8,128)S(1)} fusion(bf16[40,128,128]{2,1,0:T(8,128)(2,1)S(1)} %copy-done, bf16[16,128,128]{2,1,0:T(8,128)(2,1)S(1)} %copy-done.2), kind=kOutput, calls=%fused_computation.6 | convolution fusion | flops 5379194880 | bytes 2883584 | tf_op jit(solution)/shard_map/pqce,qfe->pcf/dot_general | solution.py:83
  52.3 0.0 copy-start.1
  52.4 0.0 copy-start.5
  52.4 0.9 constant_dynamic-slice_fusion.6
  53.3 10.6 %collective-permute-start.6 = (f32[2,128,128]{2,1,0:T(8,128)}, f32[2,128,128]{2,1,0:T(8,128)}, u32[]{:S(2)}, u32[]{:S(2)}) collective-permute-start(f32[2,128,128]{2,1,0:T(8,128)} %get-tuple-element.10), channel_id=1, source_target_pairs={{0,7},{1,0},{2,1},{3,2},{4,3},{5,4},{6,5},{7,6},{8,15},{9,8},{10,9... | collective-permute-start | bytes 393224 | tf_op jit(solution)/shard_map/ppermute | solution.py:92
  63.9 2.2 collective-permute-start.5
  66.1 1.9 collective-permute-start.4
  68.1 7.1 %collective-permute-start.3 = (f32[2,128,128]{2,1,0:T(8,128)}, f32[2,128,128]{2,1,0:T(8,128)}, u32[]{:S(2)}, u32[]{:S(2)}) collective-permute-start(f32[2,128,128]{2,1,0:T(8,128)} %get-tuple-element.13), channel_id=1, source_target_pairs={{0,4},{1,5},{2,6},{3,7},{4,0},{5,1},{6,2},{7,3},{8,12},{9,13},{10,... | collective-permute-start | bytes 393224 | tf_op jit(solution)/shard_map/ppermute | solution.py:92
  75.2 1.9 collective-permute-start.2
  77.1 0.0 copy-done.1
  77.1 1.4 copy.17
  78.5 0.0 collective-permute-done.6
  78.5 3.2 collective-permute-start.1
  81.7 0.0 collective-permute-done.5
  81.7 3.4 collective-permute-start
  85.1 0.0 copy-done.5
  85.1 0.5 multiply_add_fusion.r_0_
  85.6 0.0 collective-permute-done.4
  85.6 0.0 collective-permute-done.3
  85.6 1.5 collective-permute-done.2
  87.1 8.5 %collective-permute-done.1 = f32[2,128,128]{2,1,0:T(8,128)S(1)} collective-permute-done((f32[2,128,128]{2,1,0:T(8,128)}, f32[2,128,128]{2,1,0:T(8,128)S(1)}, u32[]{:S(2)}, u32[]{:S(2)}) %collective-permute-start.1) | collective-permute-done | bytes 131104 | tf_op jit(solution)/shard_map/ppermute | solution.py:92
  95.6 4.0 %collective-permute-done = f32[2,128,128]{2,1,0:T(8,128)S(1)} collective-permute-done((f32[2,128,128]{2,1,0:T(8,128)S(1)}, f32[2,128,128]{2,1,0:T(8,128)S(1)}, u32[]{:S(2)}, u32[]{:S(2)}) %collective-permute-start) | collective-permute-done | bytes 131104 | tf_op jit(solution)/shard_map/ppermute | solution.py:92
  99.6 1.2 add_add_fusion
  100.8 212.8 %all-to-all-done.1.r_2_.r_3_.r_4_.r_5_.r_6_.r_7_ = bf16[128,384,128]{2,1,0:T(8,128)(2,1)} async-done(((bf16[128,384,128]{2,1,0:T(8,128)(2,1)}), bf16[128,384,128]{2,1,0:T(8,128)(2,1)}, u32[]{:S(2)}, u32[]{:S(2)}) %all-to-all-start.1) | async-done | bytes 12582944 | tf_op jit(solution)/shard_map/all_to_all | solution.py:78
  313.6 20.8 %shard_map.73 = bf16[16,128,128]{2,1,0:T(8,128)(2,1)} custom-call(s32[96]{0:T(128)} %multiply_add_fusion.r_0_, bf16[16,128,256]{2,1,0:T(8,128)(2,1)} %bitcast.31, bf16[128,384,128]{2,1,0:T(8,128)(2,1)} %all-to-all-done.1.r_2_.r_3_.r_4_.r_5_.r_6_.r_7_, bf16[128,384,128]{2,1,0:T(8,128)(2,1)} %all-to-all-done.1.r_2_.r_3_.r_4_.r_5_.r_6_.r_7_, ...), custom_call_target="tpu_custom_call" | custom-call | flops 1610612736 | bytes 11010048 | tf_op jit(solution)/shard_map/pallas_call | solution.py:40
  334.4 0.0 copy-start.3
  334.4 0.0 copy-start.4
  334.4 28.2 %all_to_all.16 = bf16[8,2,128,128]{3,2,1,0:T(8,128)(2,1)S(1)} all-to-all(bf16[8,2,128,128]{3,2,1,0:T(8,128)(2,1)} %bitcast.32), channel_id=1, replica_groups=mesh['pairs'=64,'aux'=8] {'aux'}, dimensions={0} | all-to-all | bytes 1048576 | tf_op jit(solution)/shard_map/all_to_all | solution.py:103
  362.6 0.1 convert_reduce_fusion
  362.7 0.0 copy-done.3
  362.7 0.0 copy-done.4
  362.7 1.6 divide_subtract_fusion
  (2 shorter events, 0.0 us)
Async XLA Ops:
  0.0 38.0 %copy-start = (bf16[40,128,128]{2,1,0:T(8,128)(2,1)S(1)}, bf16[40,128,128]{2,1,0:T(8,128)(2,1)}, u32[]{:S(2)}) copy-start(bf16[40,128,128]{2,1,0:T(8,128)(2,1)} %param.9) | copy-start | bytes 3932164
  2.5 20.8 %all-to-all-start = ((s32[64,1,2]{2,1,0:T(1,128)}), s32[64,1,2]{2,1,0:T(1,128)S(1)}, u32[]{:S(2)}, u32[]{:S(2)}) async-start(s32[64,1,2]{2,1,0:T(1,128)} %bitcast.4), calls=%async_computation | async-start | bytes 65536 | tf_op jit(solution)/shard_map/all_to_all | solution.py:72
  32.0 6.0 %copy-start.2 = (bf16[16,128,128]{2,1,0:T(8,128)(2,1)S(1)}, bf16[16,128,128]{2,1,0:T(8,128)(2,1)}, u32[]{:S(2)}) copy-start(bf16[16,128,128]{2,1,0:T(8,128)(2,1)} %param.7) | copy-start | bytes 1572868
  32.0 281.7 %all-to-all-start.1 = ((bf16[128,384,128]{2,1,0:T(8,128)(2,1)}), bf16[128,384,128]{2,1,0:T(8,128)(2,1)}, u32[]{:S(2)}, u32[]{:S(2)}) async-start(bf16[128,384,128]{2,1,0:T(8,128)(2,1)} %gather_fusion), calls=%async_computation.1 | async-start | bytes 25165824 | tf_op jit(solution)/shard_map/all_to_all | solution.py:78
  52.3 24.8 %copy-start.1 = (bf16[16,256,128]{2,1,0:T(8,128)(2,1)S(1)}, bf16[16,256,128]{2,1,0:T(8,128)(2,1)}, u32[]{:S(2)}) copy-start(bf16[16,256,128]{2,1,0:T(8,128)(2,1)} %param.8) | copy-start | bytes 3145732
  52.4 32.7 %copy-start.5 = (s32[96,1]{0,1:T(1,128)S(1)}, s32[96,1]{0,1:T(1,128)}, u32[]{:S(2)}) copy-start(s32[96,1]{0,1:T(1,128)} %param.12) | copy-start | bytes 1156
  53.3 25.2 %collective-permute-start.6 = (f32[2,128,128]{2,1,0:T(8,128)}, f32[2,128,128]{2,1,0:T(8,128)}, u32[]{:S(2)}, u32[]{:S(2)}) collective-permute-start(f32[2,128,128]{2,1,0:T(8,128)} %get-tuple-element.10), channel_id=1, source_target_pairs={{0,7},{1,0},{2,1},{3,2},{4,3},{5,4},{6,5},{7,6},{8,15},{9,8},{10,9... | collective-permute-start | bytes 393224 | tf_op jit(solution)/shard_map/ppermute | solution.py:92
  63.9 17.9 %collective-permute-start.5 = (f32[2,128,128]{2,1,0:T(8,128)}, f32[2,128,128]{2,1,0:T(8,128)}, u32[]{:S(2)}, u32[]{:S(2)}) collective-permute-start(f32[2,128,128]{2,1,0:T(8,128)} %get-tuple-element.11), channel_id=1, source_target_pairs={{0,6},{1,7},{2,0},{3,1},{4,2},{5,3},{6,4},{7,5},{8,14},{9,15},{10,... | collective-permute-start | bytes 393224 | tf_op jit(solution)/shard_map/ppermute | solution.py:92
  66.1 19.5 %collective-permute-start.4 = (f32[2,128,128]{2,1,0:T(8,128)}, f32[2,128,128]{2,1,0:T(8,128)}, u32[]{:S(2)}, u32[]{:S(2)}) collective-permute-start(f32[2,128,128]{2,1,0:T(8,128)} %get-tuple-element.12), channel_id=1, source_target_pairs={{0,5},{1,6},{2,7},{3,0},{4,1},{5,2},{6,3},{7,4},{8,13},{9,14},{10,... | collective-permute-start | bytes 393224 | tf_op jit(solution)/shard_map/ppermute | solution.py:92
  68.1 17.6 %collective-permute-start.3 = (f32[2,128,128]{2,1,0:T(8,128)}, f32[2,128,128]{2,1,0:T(8,128)}, u32[]{:S(2)}, u32[]{:S(2)}) collective-permute-start(f32[2,128,128]{2,1,0:T(8,128)} %get-tuple-element.13), channel_id=1, source_target_pairs={{0,4},{1,5},{2,6},{3,7},{4,0},{5,1},{6,2},{7,3},{8,12},{9,13},{10,... | collective-permute-start | bytes 393224 | tf_op jit(solution)/shard_map/ppermute | solution.py:92
  75.2 11.9 %collective-permute-start.2 = (f32[2,128,128]{2,1,0:T(8,128)}, f32[2,128,128]{2,1,0:T(8,128)}, u32[]{:S(2)}, u32[]{:S(2)}) collective-permute-start(f32[2,128,128]{2,1,0:T(8,128)} %get-tuple-element.14), channel_id=1, source_target_pairs={{0,3},{1,4},{2,5},{3,6},{4,7},{5,0},{6,1},{7,2},{8,11},{9,12},{10,... | collective-permute-start | bytes 393224 | tf_op jit(solution)/shard_map/ppermute | solution.py:92
  78.5 17.2 %collective-permute-start.1 = (f32[2,128,128]{2,1,0:T(8,128)}, f32[2,128,128]{2,1,0:T(8,128)S(1)}, u32[]{:S(2)}, u32[]{:S(2)}) collective-permute-start(f32[2,128,128]{2,1,0:T(8,128)} %get-tuple-element.15), channel_id=1, source_target_pairs={{0,2},{1,3},{2,4},{3,5},{4,6},{5,7},{6,0},{7,1},{8,10},{9,11},{10,... | collective-permute-start | bytes 393224 | tf_op jit(solution)/shard_map/ppermute | solution.py:92
  81.7 17.9 %collective-permute-start = (f32[2,128,128]{2,1,0:T(8,128)S(1)}, f32[2,128,128]{2,1,0:T(8,128)S(1)}, u32[]{:S(2)}, u32[]{:S(2)}) collective-permute-start(f32[2,128,128]{2,1,0:T(8,128)S(1)} %get-tuple-element.9), channel_id=1, source_target_pairs={{0,1},{1,2},{2,3},{3,4},{4,5},{5,6},{6,7},{7,0},{8,9},{9,10},{10,1... | collective-permute-start | bytes 393224 | tf_op jit(solution)/shard_map/ppermute | solution.py:92
  334.4 28.3 %copy-start.3 = (bf16[2,128,128]{2,1,0:T(8,128)(2,1)S(1)}, bf16[2,128,128]{2,1,0:T(8,128)(2,1)}, u32[]{:S(2)}) copy-start(bf16[2,128,128]{2,1,0:T(8,128)(2,1)} %param.10) | copy-start | bytes 196612
  334.4 28.3 %copy-start.4 = (f32[2,128]{1,0:T(2,128)S(1)}, f32[2,128]{1,0:T(2,128)}, u32[]{:S(2)}) copy-start(f32[2,128]{1,0:T(2,128)} %param.11) | copy-start | bytes 3076

commit v6 on v5

--- a/solution.py
+++ b/solution.py
@@ -7,34 +7,47 @@
 
 
 def linked_kernel(links, pao_width, bucket_ref, coef_t_ref, *refs):
-    slot_refs, out_ref = refs[:links], refs[links]
-    coef_t = coef_t_ref[0]
-    total = None
-    for slot_ref in slot_refs:
-        coef_q = slot_ref[0, :pao_width, :]
-        amp_q = slot_ref[0, pao_width:, :]
-        overlap = jnp.dot(coef_t, coef_q, preferred_element_type=jnp.float32).astype(jnp.bfloat16)
-        half = jnp.dot(overlap, amp_q, preferred_element_type=jnp.float32).astype(jnp.bfloat16)
-        term = lax.dot_general(
+    slot_refs, out_ref = refs[:-1], refs[-1]
+    pno_width = out_ref.shape[-1]
+    for i in range(out_ref.shape[0]):
+        mine = slot_refs[i * links:(i + 1) * links]
+        coef_q = jnp.concatenate([r[0, :pao_width, :] for r in mine], axis=1)
+        overlap = jnp.dot(coef_t_ref[i], coef_q, preferred_element_type=jnp.float32).astype(
+            jnp.bfloat16
+        )
+        half = jnp.concatenate(
+            [
+                jnp.dot(
+                    overlap[:, j * pno_width:(j + 1) * pno_width],
+                    r[0, pao_width:, :],
+                    preferred_element_type=jnp.float32,
+                ).astype(jnp.bfloat16)
+                for j, r in enumerate(mine)
+            ],
+            axis=1,
+        )
+        total = lax.dot_general(
             half, overlap, (((1,), (1,)), ((), ())), preferred_element_type=jnp.float32
         )
-        total = term if total is None else total + term
-    out_ref[0] = total.astype(out_ref.dtype)
+        out_ref[i] = total.astype(out_ref.dtype)
 
 
-def linked_sum(bucket, coef_t, flat, links):
+def linked_sum(bucket, coef_t, flat, links, step_pairs=4):
     pair_dev, pno_width, pao_width = coef_t.shape
     row_width = flat.shape[1]
+    step_slots = step_pairs * links
 
     def slot_spec(j):
-        return pl.BlockSpec((1, row_width, pno_width), lambda p, b: (b[p * links + j], 0, 0))
+        return pl.BlockSpec(
+            (1, row_width, pno_width), lambda p, b: (b[p * step_slots + j], 0, 0)
+        )
 
     grid_spec = pltpu.PrefetchScalarGridSpec(
         num_scalar_prefetch=1,
-        grid=(pair_dev,),
-        in_specs=[pl.BlockSpec((1, pno_width, pao_width), lambda p, b: (p, 0, 0))]
-        + [slot_spec(j) for j in range(links)],
-        out_specs=pl.BlockSpec((1, pno_width, pno_width), lambda p, b: (p, 0, 0)),
+        grid=(pair_dev // step_pairs,),
+        in_specs=[pl.BlockSpec((step_pairs, pno_width, pao_width), lambda p, b: (p, 0, 0))]
+        + [slot_spec(j) for j in range(step_slots)],
+        out_specs=pl.BlockSpec((step_pairs, pno_width, pno_width), lambda p, b: (p, 0, 0)),
     )
     flops = pair_dev * links * 2 * pno_width * pno_width * (pao_width + 2 * pno_width)
     return pl.pallas_call(
@@ -46,7 +59,7 @@
             bytes_accessed=pair_dev * (links * row_width + pao_width + pno_width) * pno_width * 2,
             transcendentals=0,
         ),
-    )(bucket, coef_t, *([flat] * links))
+    )(bucket, coef_t, *([flat] * step_slots))
 
 
 def local(amplitudes, pno_coef, ladder_ints, coulomb_ints, pno_energy, link_owner, link_local):

time: 365 us -> 353 us (0.967)
  Pallas kernels: 20.8 us -> 9.4 us
    pallas_call x1, Pallas kernels: 20.8 us -> 9.4 us  [linked_sum(): pl.pallas_call(lambda *r: linked_kernel(links, pao_width, *r), grid_spec=...]
  transfers between devices with their start and end apart: 9 -> 9, of which waited for: 5 -> 5; matrix products, arithmetic and copies ran while one was open for 5% -> 6% of each run, Pallas kernels for 0% -> 0%
where the time goes in v6:
time: 353 us
  waiting for transfers between devices  234 us (66%)
  starting transfers between devices  47.9 us (14%)
  blocking collectives  28.2 us (8%)
  matrix products  14.4 us (4%)
  local copies, waits for them, and re-layouts  11.2 us (3%)
  Pallas kernels  9.4 us (3%)
  other arithmetic  6.78 us (2%)
    all_to_all x1, waiting for transfers between devices, local(): lax.all_to_all(items, 'pairs', split_axis=0, concat_axis=0, tiled=True)  213 us
    ppermute x7, starting transfers between devices, local(): lax.ppermute(piece, 'aux', [(i, (i + shift) % aux_count) for i in range(a...  30.4 us
    all_to_all x1, blocking collectives, local(): lax.all_to_all(pieces, 'aux', split_axis=0, concat_axis=0, tiled=True)  28.2 us
    dot_general x1, matrix products, local(): jnp.einsum('pqce,qfe->pcf', ladder_half, ladder_ints, preferred_element_t...  14.4 us
    ppermute x7, waiting for transfers between devices, local(): lax.ppermute(piece, 'aux', [(i, (i + shift) % aux_count) for i in range(a...  13.9 us
    all_to_all x1, starting transfers between devices, local(): lax.all_to_all(wanted.reshape(groups, capacity), 'pairs', split_axis=0, c...  11.6 us
    pallas_call x1, Pallas kernels, linked_sum(): pl.pallas_call(lambda *r: linked_kernel(links, pao_width, *r), grid_spec=...  9.4 us
    gather x1, local copies, waits for them, and re-layouts, local(): items = both[picked.reshape(groups * capacity)]  8.07 us
  transfers between devices with their start and end apart: 9, of which 5 were waited for; matrix products, arithmetic and copies ran while one was open for 6% of the time, Pallas kernels for 0%

profile of v6, /device:TPU:1, one launch (start us, length us, event | category | flops | bytes accessed | tf_op | source)
XLA Modules:
  0.0 352.7 jit_solution(6999280744528683418)
XLA Ops:
  0.0 0.0 copy-start
  0.0 1.0 convert_reduce_fusion.1
  1.0 0.7 fusion.13
  1.6 0.1 select_reduce_fusion
  1.8 0.8 sub.10
  2.5 11.6 %all-to-all-start = ((s32[64,1,2]{2,1,0:T(1,128)}), s32[64,1,2]{2,1,0:T(1,128)S(1)}, u32[]{:S(2)}, u32[]{:S(2)}) async-start(s32[64,1,2]{2,1,0:T(1,128)} %bitcast.4), calls=%async_computation | async-start | bytes 65536 | tf_op jit(solution)/shard_map/all_to_all | solution.py:85
  14.2 1.5 pad_maximum_fusion
  15.7 7.7 %all-to-all-done = s32[64,1,2]{2,1,0:T(1,128)S(1)} async-done(((s32[64,1,2]{2,1,0:T(1,128)}), s32[64,1,2]{2,1,0:T(1,128)S(1)}, u32[]{:S(2)}, u32[]{:S(2)}) %all-to-all-start) | async-done | bytes 544 | tf_op jit(solution)/shard_map/all_to_all | solution.py:85
  23.4 0.1 maximum_reduce_fusion
  23.5 0.1 reshape.40
  23.6 8.1 %gather_fusion = bf16[128,384,128]{2,1,0:T(8,128)(2,1)} fusion(bf16[16,384,128]{2,1,0:T(8,128)(2,1)S(1)} %pad_maximum_fusion, s32[1024]{0:T(1024)S(1)} %pad_clamp_fusion), kind=kCustom, calls=%fused_computation | custom fusion | bytes 25166336 | tf_op jit(solution)/shard_map/gather | solution.py:90
  31.7 0.0 copy-start.2
  31.7 5.9 %all-to-all-start.1 = ((bf16[128,384,128]{2,1,0:T(8,128)(2,1)}), bf16[128,384,128]{2,1,0:T(8,128)(2,1)}, u32[]{:S(2)}, u32[]{:S(2)}) async-start(bf16[128,384,128]{2,1,0:T(8,128)(2,1)} %gather_fusion), calls=%async_computation.1 | async-start | bytes 25165824 | tf_op jit(solution)/shard_map/all_to_all | solution.py:91
  37.7 0.0 copy-done
  37.7 0.0 copy-done.2
  37.7 14.4 %fusion.5 = f32[16,128,128]{2,1,0:T(8,128)S(1)} fusion(bf16[40,128,128]{2,1,0:T(8,128)(2,1)S(1)} %copy-done, bf16[16,128,128]{2,1,0:T(8,128)(2,1)S(1)} %copy-done.2), kind=kOutput, calls=%fused_computation.6 | convolution fusion | flops 5379194880 | bytes 2883584 | tf_op jit(solution)/shard_map/pqce,qfe->pcf/dot_general | solution.py:96
  52.1 0.0 copy-start.1
  52.2 0.0 copy-start.5
  52.2 0.9 constant_dynamic-slice_fusion.6
  53.1 10.6 %collective-permute-start.6 = (f32[2,128,128]{2,1,0:T(8,128)}, f32[2,128,128]{2,1,0:T(8,128)}, u32[]{:S(2)}, u32[]{:S(2)}) collective-permute-start(f32[2,128,128]{2,1,0:T(8,128)} %get-tuple-element.10), channel_id=1, source_target_pairs={{0,7},{1,0},{2,1},{3,2},{4,3},{5,4},{6,5},{7,6},{8,15},{9,8},{10,9... | collective-permute-start | bytes 393224 | tf_op jit(solution)/shard_map/ppermute | solution.py:105
  63.7 2.3 collective-permute-start.5
  66.0 1.9 collective-permute-start.4
  67.9 7.0 %collective-permute-start.3 = (f32[2,128,128]{2,1,0:T(8,128)}, f32[2,128,128]{2,1,0:T(8,128)}, u32[]{:S(2)}, u32[]{:S(2)}) collective-permute-start(f32[2,128,128]{2,1,0:T(8,128)} %get-tuple-element.13), channel_id=1, source_target_pairs={{0,4},{1,5},{2,6},{3,7},{4,0},{5,1},{6,2},{7,3},{8,12},{9,13},{10,... | collective-permute-start | bytes 393224 | tf_op jit(solution)/shard_map/ppermute | solution.py:105
  74.9 1.9 collective-permute-start.2
  76.9 0.0 copy-done.1
  76.9 1.4 copy.17
  78.2 0.0 collective-permute-done.6
  78.2 3.4 collective-permute-start.1
  81.6 0.0 collective-permute-done.5
  81.6 3.3 collective-permute-start
  84.9 0.0 copy-done.5
  84.9 0.5 multiply_add_fusion.r_0_
  85.4 0.0 collective-permute-done.4
  85.4 0.0 collective-permute-done.3
  85.4 1.3 collective-permute-done.2
  86.7 8.8 %collective-permute-done.1 = f32[2,128,128]{2,1,0:T(8,128)S(1)} collective-permute-done((f32[2,128,128]{2,1,0:T(8,128)}, f32[2,128,128]{2,1,0:T(8,128)S(1)}, u32[]{:S(2)}, u32[]{:S(2)}) %collective-permute-start.1) | collective-permute-done | bytes 131104 | tf_op jit(solution)/shard_map/ppermute | solution.py:105
  95.5 3.8 %collective-permute-done = f32[2,128,128]{2,1,0:T(8,128)S(1)} collective-permute-done((f32[2,128,128]{2,1,0:T(8,128)S(1)}, f32[2,128,128]{2,1,0:T(8,128)S(1)}, u32[]{:S(2)}, u32[]{:S(2)}) %collective-permute-start) | collective-permute-done | bytes 131104 | tf_op jit(solution)/shard_map/ppermute | solution.py:105
  99.3 1.2 add_add_fusion
  100.5 212.8 %all-to-all-done.1.r_2_.r_3_.r_4_.r_5_.r_6_.r_7_.r_8_.r_9_.r_10_.r_11_.r_12_.r_13_.r_14_.r_15_.r_16_.r_17_.r_18_.r_19_.r_20_.r_21_.r_22_.r_23_.r_24_.r_25_ = bf16[128,384,128]{2,1,0:T(8,128)(2,1)} async-done(((bf16[128,384,128]{2,1,0:T(8,128)(2,1)}), bf16[128,384,128]{2,1,0:T(8,128)(2,1)}, u32[]{:S(2)}, u32[]{:S(2)}) %all-to-all-start.1) | async-done | bytes 12582944 | tf_op jit(solution)/shard_map/all_to_all | solution.py:91
  313.3 9.4 %shard_map.73 = bf16[16,128,128]{2,1,0:T(8,128)(2,1)} custom-call(s32[96]{0:T(128)} %multiply_add_fusion.r_0_, bf16[16,128,256]{2,1,0:T(8,128)(2,1)} %bitcast.31, bf16[128,384,128]{2,1,0:T(8,128)(2,1)} %all-to-all-done.1.r_2_.r_3_.r_4_.r_5_.r_6_.r_7_.r_8_.r_9_.r_10_.r_11_.r_12_.r_13_.r_14_.r_15_.r_16_.r_17_.r_18_.r_19_.r_20_.r_21_.r_22_.r_23_.r_24_.r_25_, ...), custom_call_target="tpu_custom_call" | custom-call | flops 1610612736 | bytes 11010048 | tf_op jit(solution)/shard_map/pallas_call | solution.py:53
  322.8 0.0 copy-start.3
  322.8 0.0 copy-start.4
  322.8 28.2 %all_to_all.16 = bf16[8,2,128,128]{3,2,1,0:T(8,128)(2,1)S(1)} all-to-all(bf16[8,2,128,128]{3,2,1,0:T(8,128)(2,1)} %bitcast.32), channel_id=1, replica_groups=mesh['pairs'=64,'aux'=8] {'aux'}, dimensions={0} | all-to-all | bytes 1048576 | tf_op jit(solution)/shard_map/all_to_all | solution.py:116
  351.0 0.1 convert_reduce_fusion
  351.1 0.0 copy-done.3
  351.1 0.0 copy-done.4
  351.1 1.6 divide_subtract_fusion
  (2 shorter events, 0.0 us)
Async XLA Ops:
  0.0 37.7 %copy-start = (bf16[40,128,128]{2,1,0:T(8,128)(2,1)S(1)}, bf16[40,128,128]{2,1,0:T(8,128)(2,1)}, u32[]{:S(2)}) copy-start(bf16[40,128,128]{2,1,0:T(8,128)(2,1)} %param.9) | copy-start | bytes 3932164
  2.5 20.8 %all-to-all-start = ((s32[64,1,2]{2,1,0:T(1,128)}), s32[64,1,2]{2,1,0:T(1,128)S(1)}, u32[]{:S(2)}, u32[]{:S(2)}) async-start(s32[64,1,2]{2,1,0:T(1,128)} %bitcast.4), calls=%async_computation | async-start | bytes 65536 | tf_op jit(solution)/shard_map/all_to_all | solution.py:85
  31.7 6.0 %copy-start.2 = (bf16[16,128,128]{2,1,0:T(8,128)(2,1)S(1)}, bf16[16,128,128]{2,1,0:T(8,128)(2,1)}, u32[]{:S(2)}) copy-start(bf16[16,128,128]{2,1,0:T(8,128)(2,1)} %param.7) | copy-start | bytes 1572868
  31.7 281.7 %all-to-all-start.1 = ((bf16[128,384,128]{2,1,0:T(8,128)(2,1)}), bf16[128,384,128]{2,1,0:T(8,128)(2,1)}, u32[]{:S(2)}, u32[]{:S(2)}) async-start(bf16[128,384,128]{2,1,0:T(8,128)(2,1)} %gather_fusion), calls=%async_computation.1 | async-start | bytes 25165824 | tf_op jit(solution)/shard_map/all_to_all | solution.py:91
  52.1 24.7 %copy-start.1 = (bf16[16,256,128]{2,1,0:T(8,128)(2,1)S(1)}, bf16[16,256,128]{2,1,0:T(8,128)(2,1)}, u32[]{:S(2)}) copy-start(bf16[16,256,128]{2,1,0:T(8,128)(2,1)} %param.8) | copy-start | bytes 3145732
  52.2 32.7 %copy-start.5 = (s32[96,1]{0,1:T(1,128)S(1)}, s32[96,1]{0,1:T(1,128)}, u32[]{:S(2)}) copy-start(s32[96,1]{0,1:T(1,128)} %param.12) | copy-start | bytes 1156
  53.1 25.2 %collective-permute-start.6 = (f32[2,128,128]{2,1,0:T(8,128)}, f32[2,128,128]{2,1,0:T(8,128)}, u32[]{:S(2)}, u32[]{:S(2)}) collective-permute-start(f32[2,128,128]{2,1,0:T(8,128)} %get-tuple-element.10), channel_id=1, source_target_pairs={{0,7},{1,0},{2,1},{3,2},{4,3},{5,4},{6,5},{7,6},{8,15},{9,8},{10,9... | collective-permute-start | bytes 393224 | tf_op jit(solution)/shard_map/ppermute | solution.py:105
  63.7 17.9 %collective-permute-start.5 = (f32[2,128,128]{2,1,0:T(8,128)}, f32[2,128,128]{2,1,0:T(8,128)}, u32[]{:S(2)}, u32[]{:S(2)}) collective-permute-start(f32[2,128,128]{2,1,0:T(8,128)} %get-tuple-element.11), channel_id=1, source_target_pairs={{0,6},{1,7},{2,0},{3,1},{4,2},{5,3},{6,4},{7,5},{8,14},{9,15},{10,... | collective-permute-start | bytes 393224 | tf_op jit(solution)/shard_map/ppermute | solution.py:105
  66.0 19.4 %collective-permute-start.4 = (f32[2,128,128]{2,1,0:T(8,128)}, f32[2,128,128]{2,1,0:T(8,128)}, u32[]{:S(2)}, u32[]{:S(2)}) collective-permute-start(f32[2,128,128]{2,1,0:T(8,128)} %get-tuple-element.12), channel_id=1, source_target_pairs={{0,5},{1,6},{2,7},{3,0},{4,1},{5,2},{6,3},{7,4},{8,13},{9,14},{10,... | collective-permute-start | bytes 393224 | tf_op jit(solution)/shard_map/ppermute | solution.py:105
  67.9 17.5 %collective-permute-start.3 = (f32[2,128,128]{2,1,0:T(8,128)}, f32[2,128,128]{2,1,0:T(8,128)}, u32[]{:S(2)}, u32[]{:S(2)}) collective-permute-start(f32[2,128,128]{2,1,0:T(8,128)} %get-tuple-element.13), channel_id=1, source_target_pairs={{0,4},{1,5},{2,6},{3,7},{4,0},{5,1},{6,2},{7,3},{8,12},{9,13},{10,... | collective-permute-start | bytes 393224 | tf_op jit(solution)/shard_map/ppermute | solution.py:105
  74.9 11.8 %collective-permute-start.2 = (f32[2,128,128]{2,1,0:T(8,128)}, f32[2,128,128]{2,1,0:T(8,128)}, u32[]{:S(2)}, u32[]{:S(2)}) collective-permute-start(f32[2,128,128]{2,1,0:T(8,128)} %get-tuple-element.14), channel_id=1, source_target_pairs={{0,3},{1,4},{2,5},{3,6},{4,7},{5,0},{6,1},{7,2},{8,11},{9,12},{10,... | collective-permute-start | bytes 393224 | tf_op jit(solution)/shard_map/ppermute | solution.py:105
  78.2 17.3 %collective-permute-start.1 = (f32[2,128,128]{2,1,0:T(8,128)}, f32[2,128,128]{2,1,0:T(8,128)S(1)}, u32[]{:S(2)}, u32[]{:S(2)}) collective-permute-start(f32[2,128,128]{2,1,0:T(8,128)} %get-tuple-element.15), channel_id=1, source_target_pairs={{0,2},{1,3},{2,4},{3,5},{4,6},{5,7},{6,0},{7,1},{8,10},{9,11},{10,... | collective-permute-start | bytes 393224 | tf_op jit(solution)/shard_map/ppermute | solution.py:105
  81.6 17.7 %collective-permute-start = (f32[2,128,128]{2,1,0:T(8,128)S(1)}, f32[2,128,128]{2,1,0:T(8,128)S(1)}, u32[]{:S(2)}, u32[]{:S(2)}) collective-permute-start(f32[2,128,128]{2,1,0:T(8,128)S(1)} %get-tuple-element.9), channel_id=1, source_target_pairs={{0,1},{1,2},{2,3},{3,4},{4,5},{5,6},{6,7},{7,0},{8,9},{9,10},{10,1... | collective-permute-start | bytes 393224 | tf_op jit(solution)/shard_map/ppermute | solution.py:105
  322.8 28.3 %copy-start.3 = (bf16[2,128,128]{2,1,0:T(8,128)(2,1)S(1)}, bf16[2,128,128]{2,1,0:T(8,128)(2,1)}, u32[]{:S(2)}) copy-start(bf16[2,128,128]{2,1,0:T(8,128)(2,1)} %param.10) | copy-start | bytes 196612
  322.8 28.3 %copy-start.4 = (f32[2,128]{1,0:T(2,128)S(1)}, f32[2,128]{1,0:T(2,128)}, u32[]{:S(2)}) copy-start(f32[2,128]{1,0:T(2,128)} %param.11) | copy-start | bytes 3076

commit v7 on v6

--- a/solution.py
+++ b/solution.py
@@ -111,11 +111,15 @@
     coef_t = jnp.transpose(pno_coef, (0, 2, 1))
     linked = linked_sum(bucket, coef_t, flat, per_slice)
 
-    pieces = linked.reshape(aux_count, own_rows, pno_width, pno_width)
-    linked_mine = jnp.sum(
-        lax.all_to_all(pieces, "aux", split_axis=0, concat_axis=0, tiled=True).astype(jnp.float32),
-        axis=0,
+    linked_mine = lax.dynamic_slice_in_dim(linked, aux_me * own_rows, own_rows, 0).astype(
+        jnp.float32
     )
+    for shift in range(1, aux_count):
+        goes_to = lax.rem(aux_me + shift, aux_count)
+        piece = lax.dynamic_slice_in_dim(linked, goes_to * own_rows, own_rows, 0)
+        linked_mine = linked_mine + lax.ppermute(
+            piece, "aux", [(i, (i + shift) % aux_count) for i in range(aux_count)]
+        ).astype(jnp.float32)
     reduced = ladder_mine + linked_mine
     first_row = lax.axis_index("aux") * own_rows
     amp_mine = lax.dynamic_slice_in_dim(amplitudes, first_row, own_rows, 0)

time: 353 us -> 364 us (1.031)
  starting transfers between devices: 47.9 us -> 78.8 us
  blocking collectives: 28.2 us -> 0 us
  waiting for transfers between devices: 234 us -> 241 us
    ppermute x7 -> x14, starting transfers between devices: 30.4 us -> 61 us  [local(): lax.ppermute(piece, 'aux', [(i, (i + shift) % aux_count) for i in range(a...]
    all_to_all x1 -> x0, blocking collectives: 28.2 us -> none  [local(): lax.all_to_all(pieces, 'aux', split_axis=0, concat_axis=0, tiled=True)]
    ppermute x7 -> x14, waiting for transfers between devices: 13.9 us -> 20.2 us  [local(): lax.ppermute(piece, 'aux', [(i, (i + shift) % aux_count) for i in range(a...]
  transfers between devices with their start and end apart: 9 -> 16, of which waited for: 5 -> 8; matrix products, arithmetic and copies ran while one was open for 6% -> 5% of each run, Pallas kernels for 0% -> 0%
where the time goes in v7:
time: 364 us; the launch traced here: 363 us
  waiting for transfers between devices  241 us (66%)
  starting transfers between devices  78.8 us (22%)
  matrix products  14.2 us (4%)
  local copies, waits for them, and re-layouts  12.4 us (3%)
  Pallas kernels  9.53 us (3%)
  other arithmetic  6.69 us (2%)
    all_to_all x1, waiting for transfers between devices, local(): lax.all_to_all(items, 'pairs', split_axis=0, concat_axis=0, tiled=True)  213 us
    ppermute x14, starting transfers between devices, local(): lax.ppermute(piece, 'aux', [(i, (i + shift) % aux_count) for i in range(a...  61 us
    ppermute x14, waiting for transfers between devices, local(): lax.ppermute(piece, 'aux', [(i, (i + shift) % aux_count) for i in range(a...  20.2 us
    dot_general x1, matrix products, local(): jnp.einsum('pqce,qfe->pcf', ladder_half, ladder_ints, preferred_element_t...  14.2 us
    all_to_all x1, starting transfers between devices, local(): lax.all_to_all(wanted.reshape(groups, capacity), 'pairs', split_axis=0, c...  11.6 us
    pallas_call x1, Pallas kernels, linked_sum(): pl.pallas_call(lambda *r: linked_kernel(links, pao_width, *r), grid_spec=...  9.53 us
    gather x1, local copies, waits for them, and re-layouts, local(): items = both[picked.reshape(groups * capacity)]  8.08 us
    all_to_all x1, waiting for transfers between devices, local(): lax.all_to_all(wanted.reshape(groups, capacity), 'pairs', split_axis=0, c...  7.7 us
  transfers between devices with their start and end apart: 16, of which 8 were waited for; matrix products, arithmetic and copies ran while one was open for 5% of the time, Pallas kernels for 0%

profile of v7, /device:TPU:1, one launch (start us, length us, event | category | flops | bytes accessed | tf_op | source)
XLA Modules:
  0.0 363.2 jit_solution(15393682407676693591)
XLA Ops:
  0.0 0.0 copy-start
  0.0 1.0 convert_reduce_fusion
  1.0 0.7 fusion.13
  1.6 0.1 select_reduce_fusion
  1.8 0.8 sub.10
  2.5 11.6 %all-to-all-start = ((s32[64,1,2]{2,1,0:T(1,128)}), s32[64,1,2]{2,1,0:T(1,128)S(1)}, u32[]{:S(2)}, u32[]{:S(2)}) async-start(s32[64,1,2]{2,1,0:T(1,128)} %bitcast.4), calls=%async_computation | async-start | bytes 65536 | tf_op jit(solution)/shard_map/all_to_all | solution.py:85
  14.2 1.5 pad_maximum_fusion
  15.7 7.7 %all-to-all-done = s32[64,1,2]{2,1,0:T(1,128)S(1)} async-done(((s32[64,1,2]{2,1,0:T(1,128)}), s32[64,1,2]{2,1,0:T(1,128)S(1)}, u32[]{:S(2)}, u32[]{:S(2)}) %all-to-all-start) | async-done | bytes 544 | tf_op jit(solution)/shard_map/all_to_all | solution.py:85
  23.4 0.1 maximum_reduce_fusion
  23.5 0.1 reshape.36
  23.6 8.1 %gather_fusion = bf16[128,384,128]{2,1,0:T(8,128)(2,1)} fusion(bf16[16,384,128]{2,1,0:T(8,128)(2,1)S(1)} %pad_maximum_fusion, s32[1024]{0:T(1024)S(1)} %pad_clamp_fusion), kind=kCustom, calls=%fused_computation | custom fusion | bytes 25166336 | tf_op jit(solution)/shard_map/gather | solution.py:90
  31.7 0.0 copy-start.2
  31.7 6.2 %all-to-all-start.1 = ((bf16[128,384,128]{2,1,0:T(8,128)(2,1)}), bf16[128,384,128]{2,1,0:T(8,128)(2,1)}, u32[]{:S(2)}, u32[]{:S(2)}) async-start(bf16[128,384,128]{2,1,0:T(8,128)(2,1)} %gather_fusion), calls=%async_computation.1 | async-start | bytes 25165824 | tf_op jit(solution)/shard_map/all_to_all | solution.py:91
  38.0 0.0 copy-done
  38.0 0.0 copy-done.2
  38.0 14.2 %fusion.5 = f32[16,128,128]{2,1,0:T(8,128)S(1)} fusion(bf16[40,128,128]{2,1,0:T(8,128)(2,1)S(1)} %copy-done, bf16[16,128,128]{2,1,0:T(8,128)(2,1)S(1)} %copy-done.2), kind=kOutput, calls=%fused_computation.6 | convolution fusion | flops 5379194880 | bytes 2883584 | tf_op jit(solution)/shard_map/pqce,qfe->pcf/dot_general | solution.py:96
  52.2 0.0 copy-start.1
  52.2 0.0 copy-start.5
  52.2 0.9 constant_dynamic-slice_fusion.12
  53.2 10.9 %collective-permute-start.6 = (f32[2,128,128]{2,1,0:T(8,128)}, f32[2,128,128]{2,1,0:T(8,128)S(1)}, u32[]{:S(2)}, u32[]{:S(2)}) collective-permute-start(f32[2,128,128]{2,1,0:T(8,128)} %get-tuple-element.10), channel_id=1, source_target_pairs={{0,7},{1,0},{2,1},{3,2},{4,3},{5,4},{6,5},{7,6},{8,15},{9,8},{10,9... | collective-permute-start | bytes 393224 | tf_op jit(solution)/shard_map/ppermute | solution.py:105
  64.1 2.0 collective-permute-start.5
  66.0 2.1 collective-permute-start.4
  68.1 7.4 %collective-permute-start.3 = (f32[2,128,128]{2,1,0:T(8,128)}, f32[2,128,128]{2,1,0:T(8,128)}, u32[]{:S(2)}, u32[]{:S(2)}) collective-permute-start(f32[2,128,128]{2,1,0:T(8,128)} %get-tuple-element.13), channel_id=1, source_target_pairs={{0,4},{1,5},{2,6},{3,7},{4,0},{5,1},{6,2},{7,3},{8,12},{9,13},{10,... | collective-permute-start | bytes 393224 | tf_op jit(solution)/shard_map/ppermute | solution.py:105
  75.5 1.9 collective-permute-start.2
  77.4 0.0 copy-done.1
  77.4 1.4 copy.17
  78.8 0.0 collective-permute-done.6
  78.8 3.1 collective-permute-start.1
  81.9 0.0 collective-permute-done.5
  81.9 3.2 collective-permute-start
  85.1 0.0 copy-done.5
  85.1 0.5 multiply_add_fusion.r_0_
  85.7 0.0 collective-permute-done.4
  85.7 0.0 collective-permute-done.3
  85.7 2.0 collective-permute-done.2
  87.7 8.0 %collective-permute-done.1 = f32[2,128,128]{2,1,0:T(8,128)S(1)} collective-permute-done((f32[2,128,128]{2,1,0:T(8,128)}, f32[2,128,128]{2,1,0:T(8,128)S(1)}, u32[]{:S(2)}, u32[]{:S(2)}) %collective-permute-start.1) | collective-permute-done | bytes 131104 | tf_op jit(solution)/shard_map/ppermute | solution.py:105
  95.7 3.4 collective-permute-done
  99.1 1.1 add_add_fusion
  100.3 213.3 %all-to-all-done.1.r_2_.r_3_.r_4_.r_5_.r_6_.r_7_.r_8_.r_9_.r_10_.r_11_.r_12_.r_13_.r_14_.r_15_.r_16_.r_17_.r_18_.r_19_.r_20_.r_21_.r_22_.r_23_.r_24_.r_25_ = bf16[128,384,128]{2,1,0:T(8,128)(2,1)} async-done(((bf16[128,384,128]{2,1,0:T(8,128)(2,1)}), bf16[128,384,128]{2,1,0:T(8,128)(2,1)}, u32[]{:S(2)}, u32[]{:S(2)}) %all-to-all-start.1) | async-done | bytes 12582944 | tf_op jit(solution)/shard_map/all_to_all | solution.py:91
  313.6 0.0 copy-start.3
  313.6 0.0 copy-start.4
  313.6 9.5 %shard_map.73 = bf16[16,128,128]{2,1,0:T(8,128)(2,1)} custom-call(s32[96]{0:T(128)} %multiply_add_fusion.r_0_, bf16[16,128,256]{2,1,0:T(8,128)(2,1)} %bitcast.30, bf16[128,384,128]{2,1,0:T(8,128)(2,1)} %all-to-all-done.1.r_2_.r_3_.r_4_.r_5_.r_6_.r_7_.r_8_.r_9_.r_10_.r_11_.r_12_.r_13_.r_14_.r_15_.r_16_.r_17_.r_18_.r_19_.r_20_.r_21_.r_22_.r_23_.r_24_.r_25_, ...), custom_call_target="tpu_custom_call" | custom-call | flops 1610612736 | bytes 11010048 | tf_op jit(solution)/shard_map/pallas_call | solution.py:53
  323.2 1.1 constant_dynamic-slice_fusion.5
  324.2 10.7 %collective-permute-start.13 = (bf16[2,128,128]{2,1,0:T(8,128)(2,1)S(1)}, bf16[2,128,128]{2,1,0:T(8,128)(2,1)S(1)}, u32[]{:S(2)}, u32[]{:S(2)}) collective-permute-start(bf16[2,128,128]{2,1,0:T(8,128)(2,1)S(1)} %get-tuple-element.17), channel_id=1, source_target_pairs={{0,7},{1,0},{2,1},{3,2},{4,3},{5,4},{6,5},{7,6},{8,15},{9,8},{10,9... | collective-permute-start | bytes 196616 | tf_op jit(solution)/shard_map/ppermute | solution.py:120
  334.9 2.2 collective-permute-start.12
  337.1 1.9 collective-permute-start.11
  339.1 7.3 %collective-permute-start.10 = (bf16[2,128,128]{2,1,0:T(8,128)(2,1)S(1)}, bf16[2,128,128]{2,1,0:T(8,128)(2,1)S(1)}, u32[]{:S(2)}, u32[]{:S(2)}) collective-permute-start(bf16[2,128,128]{2,1,0:T(8,128)(2,1)S(1)} %get-tuple-element.20), channel_id=1, source_target_pairs={{0,4},{1,5},{2,6},{3,7},{4,0},{5,1},{6,2},{7,3},{8,12},{9,13},{10,... | collective-permute-start | bytes 196616 | tf_op jit(solution)/shard_map/ppermute | solution.py:120
  346.4 1.9 collective-permute-start.9
  348.3 0.0 collective-permute-done.13
  348.3 3.1 collective-permute-start.8
  351.4 0.0 collective-permute-done.12
  351.4 3.3 collective-permute-start.7
  354.7 0.0 collective-permute-done.11
  354.8 0.0 collective-permute-done.10
  354.8 1.2 collective-permute-done.9
  355.9 3.9 %collective-permute-done.8 = bf16[2,128,128]{2,1,0:T(8,128)(2,1)S(1)} collective-permute-done((bf16[2,128,128]{2,1,0:T(8,128)(2,1)S(1)}, bf16[2,128,128]{2,1,0:T(8,128)(2,1)S(1)}, u32[]{:S(2)}, u32[]{:S(2)}) %collective-permute-start.8) | collective-permute-done | bytes 65568 | tf_op jit(solution)/shard_map/ppermute | solution.py:120
  359.9 1.6 collective-permute-done.7
  361.5 0.0 copy-done.3
  361.5 0.0 copy-done.4
  361.5 1.6 divide_subtract_fusion
  (2 shorter events, 0.0 us)
Async XLA Ops:
  0.0 38.0 %copy-start = (bf16[40,128,128]{2,1,0:T(8,128)(2,1)S(1)}, bf16[40,128,128]{2,1,0:T(8,128)(2,1)}, u32[]{:S(2)}) copy-start(bf16[40,128,128]{2,1,0:T(8,128)(2,1)} %param.9) | copy-start | bytes 3932164
  2.5 20.8 %all-to-all-start = ((s32[64,1,2]{2,1,0:T(1,128)}), s32[64,1,2]{2,1,0:T(1,128)S(1)}, u32[]{:S(2)}, u32[]{:S(2)}) async-start(s32[64,1,2]{2,1,0:T(1,128)} %bitcast.4), calls=%async_computation | async-start | bytes 65536 | tf_op jit(solution)/shard_map/all_to_all | solution.py:85
  31.7 6.3 %copy-start.2 = (bf16[16,128,128]{2,1,0:T(8,128)(2,1)S(1)}, bf16[16,128,128]{2,1,0:T(8,128)(2,1)}, u32[]{:S(2)}) copy-start(bf16[16,128,128]{2,1,0:T(8,128)(2,1)} %param.7) | copy-start | bytes 1572868
  31.7 281.9 %all-to-all-start.1 = ((bf16[128,384,128]{2,1,0:T(8,128)(2,1)}), bf16[128,384,128]{2,1,0:T(8,128)(2,1)}, u32[]{:S(2)}, u32[]{:S(2)}) async-start(bf16[128,384,128]{2,1,0:T(8,128)(2,1)} %gather_fusion), calls=%async_computation.1 | async-start | bytes 25165824 | tf_op jit(solution)/shard_map/all_to_all | solution.py:91
  52.2 25.2 %copy-start.1 = (bf16[16,256,128]{2,1,0:T(8,128)(2,1)S(1)}, bf16[16,256,128]{2,1,0:T(8,128)(2,1)}, u32[]{:S(2)}) copy-start(bf16[16,256,128]{2,1,0:T(8,128)(2,1)} %param.8) | copy-start | bytes 3145732
  52.2 32.9 %copy-start.5 = (s32[96,1]{0,1:T(1,128)S(1)}, s32[96,1]{0,1:T(1,128)}, u32[]{:S(2)}) copy-start(s32[96,1]{0,1:T(1,128)} %param.12) | copy-start | bytes 1156
  53.2 25.6 %collective-permute-start.6 = (f32[2,128,128]{2,1,0:T(8,128)}, f32[2,128,128]{2,1,0:T(8,128)S(1)}, u32[]{:S(2)}, u32[]{:S(2)}) collective-permute-start(f32[2,128,128]{2,1,0:T(8,128)} %get-tuple-element.10), channel_id=1, source_target_pairs={{0,7},{1,0},{2,1},{3,2},{4,3},{5,4},{6,5},{7,6},{8,15},{9,8},{10,9... | collective-permute-start | bytes 393224 | tf_op jit(solution)/shard_map/ppermute | solution.py:105
  64.1 17.8 %collective-permute-start.5 = (f32[2,128,128]{2,1,0:T(8,128)}, f32[2,128,128]{2,1,0:T(8,128)}, u32[]{:S(2)}, u32[]{:S(2)}) collective-permute-start(f32[2,128,128]{2,1,0:T(8,128)} %get-tuple-element.11), channel_id=1, source_target_pairs={{0,6},{1,7},{2,0},{3,1},{4,2},{5,3},{6,4},{7,5},{8,14},{9,15},{10,... | collective-permute-start | bytes 393224 | tf_op jit(solution)/shard_map/ppermute | solution.py:105
  66.0 19.7 %collective-permute-start.4 = (f32[2,128,128]{2,1,0:T(8,128)}, f32[2,128,128]{2,1,0:T(8,128)}, u32[]{:S(2)}, u32[]{:S(2)}) collective-permute-start(f32[2,128,128]{2,1,0:T(8,128)} %get-tuple-element.12), channel_id=1, source_target_pairs={{0,5},{1,6},{2,7},{3,0},{4,1},{5,2},{6,3},{7,4},{8,13},{9,14},{10,... | collective-permute-start | bytes 393224 | tf_op jit(solution)/shard_map/ppermute | solution.py:105
  68.1 17.6 %collective-permute-start.3 = (f32[2,128,128]{2,1,0:T(8,128)}, f32[2,128,128]{2,1,0:T(8,128)}, u32[]{:S(2)}, u32[]{:S(2)}) collective-permute-start(f32[2,128,128]{2,1,0:T(8,128)} %get-tuple-element.13), channel_id=1, source_target_pairs={{0,4},{1,5},{2,6},{3,7},{4,0},{5,1},{6,2},{7,3},{8,12},{9,13},{10,... | collective-permute-start | bytes 393224 | tf_op jit(solution)/shard_map/ppermute | solution.py:105
  75.5 12.2 %collective-permute-start.2 = (f32[2,128,128]{2,1,0:T(8,128)}, f32[2,128,128]{2,1,0:T(8,128)}, u32[]{:S(2)}, u32[]{:S(2)}) collective-permute-start(f32[2,128,128]{2,1,0:T(8,128)} %get-tuple-element.14), channel_id=1, source_target_pairs={{0,3},{1,4},{2,5},{3,6},{4,7},{5,0},{6,1},{7,2},{8,11},{9,12},{10,... | collective-permute-start | bytes 393224 | tf_op jit(solution)/shard_map/ppermute | solution.py:105
  78.8 16.9 %collective-permute-start.1 = (f32[2,128,128]{2,1,0:T(8,128)}, f32[2,128,128]{2,1,0:T(8,128)S(1)}, u32[]{:S(2)}, u32[]{:S(2)}) collective-permute-start(f32[2,128,128]{2,1,0:T(8,128)} %get-tuple-element.15), channel_id=1, source_target_pairs={{0,2},{1,3},{2,4},{3,5},{4,6},{5,7},{6,0},{7,1},{8,10},{9,11},{10,... | collective-permute-start | bytes 393224 | tf_op jit(solution)/shard_map/ppermute | solution.py:105
  81.9 17.2 %collective-permute-start = (f32[2,128,128]{2,1,0:T(8,128)}, f32[2,128,128]{2,1,0:T(8,128)S(1)}, u32[]{:S(2)}, u32[]{:S(2)}) collective-permute-start(f32[2,128,128]{2,1,0:T(8,128)} %get-tuple-element.9), channel_id=1, source_target_pairs={{0,1},{1,2},{2,3},{3,4},{4,5},{5,6},{6,7},{7,0},{8,9},{9,10},{10,1... | collective-permute-start | bytes 393224 | tf_op jit(solution)/shard_map/ppermute | solution.py:105
  313.6 47.9 %copy-start.3 = (bf16[2,128,128]{2,1,0:T(8,128)(2,1)S(1)}, bf16[2,128,128]{2,1,0:T(8,128)(2,1)}, u32[]{:S(2)}) copy-start(bf16[2,128,128]{2,1,0:T(8,128)(2,1)} %param.10) | copy-start | bytes 196612
  313.6 47.9 %copy-start.4 = (f32[2,128]{1,0:T(2,128)S(1)}, f32[2,128]{1,0:T(2,128)}, u32[]{:S(2)}) copy-start(f32[2,128]{1,0:T(2,128)} %param.11) | copy-start | bytes 3076
  324.2 24.0 %collective-permute-start.13 = (bf16[2,128,128]{2,1,0:T(8,128)(2,1)S(1)}, bf16[2,128,128]{2,1,0:T(8,128)(2,1)S(1)}, u32[]{:S(2)}, u32[]{:S(2)}) collective-permute-start(bf16[2,128,128]{2,1,0:T(8,128)(2,1)S(1)} %get-tuple-element.17), channel_id=1, source_target_pairs={{0,7},{1,0},{2,1},{3,2},{4,3},{5,4},{6,5},{7,6},{8,15},{9,8},{10,9... | collective-permute-start | bytes 196616 | tf_op jit(solution)/shard_map/ppermute | solution.py:120
  334.9 16.5 %collective-permute-start.12 = (bf16[2,128,128]{2,1,0:T(8,128)(2,1)S(1)}, bf16[2,128,128]{2,1,0:T(8,128)(2,1)S(1)}, u32[]{:S(2)}, u32[]{:S(2)}) collective-permute-start(bf16[2,128,128]{2,1,0:T(8,128)(2,1)S(1)} %get-tuple-element.18), channel_id=1, source_target_pairs={{0,6},{1,7},{2,0},{3,1},{4,2},{5,3},{6,4},{7,5},{8,14},{9,15},{10,... | collective-permute-start | bytes 196616 | tf_op jit(solution)/shard_map/ppermute | solution.py:120
  337.1 17.6 %collective-permute-start.11 = (bf16[2,128,128]{2,1,0:T(8,128)(2,1)S(1)}, bf16[2,128,128]{2,1,0:T(8,128)(2,1)S(1)}, u32[]{:S(2)}, u32[]{:S(2)}) collective-permute-start(bf16[2,128,128]{2,1,0:T(8,128)(2,1)S(1)} %get-tuple-element.19), channel_id=1, source_target_pairs={{0,5},{1,6},{2,7},{3,0},{4,1},{5,2},{6,3},{7,4},{8,13},{9,14},{10,... | collective-permute-start | bytes 196616 | tf_op jit(solution)/shard_map/ppermute | solution.py:120
  339.1 15.7 %collective-permute-start.10 = (bf16[2,128,128]{2,1,0:T(8,128)(2,1)S(1)}, bf16[2,128,128]{2,1,0:T(8,128)(2,1)S(1)}, u32[]{:S(2)}, u32[]{:S(2)}) collective-permute-start(bf16[2,128,128]{2,1,0:T(8,128)(2,1)S(1)} %get-tuple-element.20), channel_id=1, source_target_pairs={{0,4},{1,5},{2,6},{3,7},{4,0},{5,1},{6,2},{7,3},{8,12},{9,13},{10,... | collective-permute-start | bytes 196616 | tf_op jit(solution)/shard_map/ppermute | solution.py:120
  346.4 9.6 %collective-permute-start.9 = (bf16[2,128,128]{2,1,0:T(8,128)(2,1)S(1)}, bf16[2,128,128]{2,1,0:T(8,128)(2,1)S(1)}, u32[]{:S(2)}, u32[]{:S(2)}) collective-permute-start(bf16[2,128,128]{2,1,0:T(8,128)(2,1)S(1)} %get-tuple-element.21), channel_id=1, source_target_pairs={{0,3},{1,4},{2,5},{3,6},{4,7},{5,0},{6,1},{7,2},{8,11},{9,12},{10,... | collective-permute-start | bytes 196616 | tf_op jit(solution)/shard_map/ppermute | solution.py:120
  348.3 11.6 %collective-permute-start.8 = (bf16[2,128,128]{2,1,0:T(8,128)(2,1)S(1)}, bf16[2,128,128]{2,1,0:T(8,128)(2,1)S(1)}, u32[]{:S(2)}, u32[]{:S(2)}) collective-permute-start(bf16[2,128,128]{2,1,0:T(8,128)(2,1)S(1)} %get-tuple-element.22), channel_id=1, source_target_pairs={{0,2},{1,3},{2,4},{3,5},{4,6},{5,7},{6,0},{7,1},{8,10},{9,11},{10,... | collective-permute-start | bytes 196616 | tf_op jit(solution)/shard_map/ppermute | solution.py:120
  351.4 10.1 %collective-permute-start.7 = (bf16[2,128,128]{2,1,0:T(8,128)(2,1)S(1)}, bf16[2,128,128]{2,1,0:T(8,128)(2,1)S(1)}, u32[]{:S(2)}, u32[]{:S(2)}) collective-permute-start(bf16[2,128,128]{2,1,0:T(8,128)(2,1)S(1)} %get-tuple-element.16), channel_id=1, source_target_pairs={{0,1},{1,2},{2,3},{3,4},{4,5},{5,6},{6,7},{7,0},{8,9},{9,10},{10,1... | collective-permute-start | bytes 196616 | tf_op jit(solution)/shard_map/ppermute | solution.py:120

commit v8 on v6

--- a/solution.py
+++ b/solution.py
@@ -85,17 +85,24 @@
     asked_rows = lax.all_to_all(
         wanted.reshape(groups, capacity), "pairs", split_axis=0, concat_axis=0, tiled=True
     )
+    def ladder_of(amps):
+        ladder_half = jnp.einsum(
+            "qcd,pde->pqce", ladder_ints, amps, preferred_element_type=jnp.float32
+        ).astype(jnp.bfloat16)
+        return jnp.einsum(
+            "pqce,qfe->pcf", ladder_half, ladder_ints, preferred_element_type=jnp.float32
+        )
+
+    split = pair_dev // 2
+    ladder_first = ladder_of(amplitudes[:split])
     picked = jnp.maximum(asked_rows, 0)
+    picked, ladder_first = lax.optimization_barrier((picked, ladder_first))
     both = jnp.concatenate([pno_coef, amplitudes], axis=1)
     items = both[picked.reshape(groups * capacity)]
     flat = lax.all_to_all(items, "pairs", split_axis=0, concat_axis=0, tiled=True)
 
-    ladder_half = jnp.einsum(
-        "qcd,pde->pqce", ladder_ints, amplitudes, preferred_element_type=jnp.float32
-    ).astype(jnp.bfloat16)
-    ladder = jnp.einsum(
-        "pqce,qfe->pcf", ladder_half, ladder_ints, preferred_element_type=jnp.float32
-    )
+    ladder = jnp.concatenate([ladder_first, ladder_of(amplitudes[split:])], axis=0)
+
     aux_count = lax.axis_size("aux")
     aux_me = lax.axis_index("aux")
     ladder_mine = lax.dynamic_slice_in_dim(ladder, aux_me * own_rows, own_rows, 0)

time: 353 us -> 359 us (1.017)
  starting transfers between devices: 47.9 us -> 53.9 us
    all_to_all x1, waiting for transfers between devices: 7.7 us -> 0.01 us  [local(): lax.all_to_all(wanted.reshape(groups, capacity), 'pairs', split_axis=0, c...]
    all_to_all x1, waiting for transfers between devices: 213 us -> 220 us  [local(): lax.all_to_all(items, 'pairs', split_axis=0, concat_axis=0, tiled=True)]
    all_to_all x1, starting transfers between devices: 5.93 us -> 10.7 us  [local(): lax.all_to_all(items, 'pairs', split_axis=0, concat_axis=0, tiled=True)]
    dot_general x1 -> x2, matrix products: 14.4 us -> 15.4 us  [ladder_of(): jnp.einsum('pqce,qfe->pcf', ladder_half, ladder_ints, preferred_element_t...]
  transfers between devices with their start and end apart: 9 -> 9, of which waited for: 5 -> 4; matrix products, arithmetic and copies ran while one was open for 6% -> 6% of each run, Pallas kernels for 0% -> 0%
where the time goes in v8:
time: 359 us; the launch traced here: 358 us
  waiting for transfers between devices  233 us (65%)
  starting transfers between devices  53.9 us (15%)
  blocking collectives  28.3 us (8%)
  matrix products  15.4 us (4%)
  local copies, waits for them, and re-layouts  10.6 us (3%)
  Pallas kernels  9.39 us (3%)
  other arithmetic  7.39 us (2%)
    all_to_all x1, waiting for transfers between devices, local(): lax.all_to_all(items, 'pairs', split_axis=0, concat_axis=0, tiled=True)  220 us
    ppermute x7, starting transfers between devices, local(): lax.ppermute(piece, 'aux', [(i, (i + shift) % aux_count) for i in range(a...  31.6 us
    all_to_all x1, blocking collectives, local(): lax.all_to_all(pieces, 'aux', split_axis=0, concat_axis=0, tiled=True)  28.3 us
    dot_general x2, matrix products, ladder_of(): jnp.einsum('pqce,qfe->pcf', ladder_half, ladder_ints, preferred_element_t...  15.4 us
    ppermute x7, waiting for transfers between devices, local(): lax.ppermute(piece, 'aux', [(i, (i + shift) % aux_count) for i in range(a...  12.6 us
    all_to_all x1, starting transfers between devices, local(): lax.all_to_all(wanted.reshape(groups, capacity), 'pairs', split_axis=0, c...  11.6 us
    all_to_all x1, starting transfers between devices, local(): lax.all_to_all(items, 'pairs', split_axis=0, concat_axis=0, tiled=True)  10.7 us
    pallas_call x1, Pallas kernels, linked_sum(): pl.pallas_call(lambda *r: linked_kernel(links, pao_width, *r), grid_spec=...  9.39 us
  transfers between devices with their start and end apart: 9, of which 4 were waited for; matrix products, arithmetic and copies ran while one was open for 6% of the time, Pallas kernels for 0%

profile of v8, /device:TPU:1, one launch (start us, length us, event | category | flops | bytes accessed | tf_op | source)
XLA Modules:
  0.0 358.0 jit_solution(10995382918621355523)
XLA Ops:
  0.0 0.0 copy-start
  0.0 1.0 convert_reduce_fusion.1
  1.0 0.7 fusion.53
  1.6 0.1 select_reduce_fusion
  1.8 0.8 sub.10
  2.5 11.6 %all-to-all-start = ((s32[64,1,2]{2,1,0:T(1,128)}), s32[64,1,2]{2,1,0:T(1,128)S(1)}, u32[]{:S(2)}, u32[]{:S(2)}) async-start(s32[64,1,2]{2,1,0:T(1,128)} %bitcast.4), calls=%async_computation | async-start | bytes 65536 | tf_op jit(solution)/shard_map/all_to_all | solution.py:85
  14.2 0.0 copy-done
  14.2 8.0 %fusion.14 = f32[8,128,128]{2,1,0:T(8,128)S(1)} fusion(bf16[40,128,128]{2,1,0:T(8,128)(2,1)S(1)} %copy-done, bf16[16,128,128]{2,1,0:T(8,128)(2,1)} %param.7), kind=kOutput, calls=%fused_computation.28 | convolution fusion | flops 2689597440 | bytes 3407872 | tf_op jit(solution)/shard_map/pqce,qfe->pcf/dot_general | solution.py:92
  22.2 1.5 pad_maximum_fusion
  23.7 0.0 all-to-all-done
  23.7 0.1 copy.31
  23.8 0.1 copy.34
  23.9 0.1 reshape.56
  24.1 8.1 %gather_fusion = bf16[128,384,128]{2,1,0:T(8,128)(2,1)} fusion(bf16[16,384,128]{2,1,0:T(8,128)(2,1)S(1)} %pad_maximum_fusion, s32[1024]{0:T(1024)S(1)} %pad_clamp_fusion), kind=kCustom, calls=%fused_computation | custom fusion | bytes 25166336 | tf_op jit(solution)/shard_map/gather | solution.py:101
  32.2 0.0 copy-start.2
  32.2 10.7 %all-to-all-start.1 = ((bf16[128,384,128]{2,1,0:T(8,128)(2,1)}), bf16[128,384,128]{2,1,0:T(8,128)(2,1)}, u32[]{:S(2)}, u32[]{:S(2)}) async-start(bf16[128,384,128]{2,1,0:T(8,128)(2,1)} %gather_fusion), calls=%async_computation.1 | async-start | bytes 25165824 | tf_op jit(solution)/shard_map/all_to_all | solution.py:102
  42.9 0.0 copy-done.2
  42.9 7.4 %fusion.21 = f32[8,128,128]{2,1,0:T(8,128)S(1)} fusion(bf16[40,128,128]{2,1,0:T(8,128)(2,1)S(1)} %copy-done, bf16[16,128,128]{2,1,0:T(8,128)(2,1)S(1)} %copy-done.2), kind=kOutput, calls=%fused_computation.29 | convolution fusion | flops 2689597440 | bytes 3407872 | tf_op jit(solution)/shard_map/pqce,qfe->pcf/dot_general | solution.py:92
  50.3 0.0 copy-start.1
  50.3 0.9 fusion.45
  51.3 4.0 %collective-permute-start = (f32[2,128,128]{2,1,0:T(8,128)}, f32[2,128,128]{2,1,0:T(8,128)S(1)}, u32[]{:S(2)}, u32[]{:S(2)}) collective-permute-start(f32[2,128,128]{2,1,0:T(8,128)} %get-tuple-element.13), channel_id=1, source_target_pairs={{0,1},{1,2},{2,3},{3,4},{4,5},{5,6},{6,7},{7,0},{8,9},{9,10},{10,1... | collective-permute-start | bytes 393224 | tf_op jit(solution)/shard_map/ppermute | solution.py:112
  55.2 5.9 %collective-permute-start.1 = (f32[2,128,128]{2,1,0:T(8,128)}, f32[2,128,128]{2,1,0:T(8,128)}, u32[]{:S(2)}, u32[]{:S(2)}) collective-permute-start(f32[2,128,128]{2,1,0:T(8,128)} %get-tuple-element.14), channel_id=1, source_target_pairs={{0,2},{1,3},{2,4},{3,5},{4,6},{5,7},{6,0},{7,1},{8,10},{9,11},{10,... | collective-permute-start | bytes 393224 | tf_op jit(solution)/shard_map/ppermute | solution.py:112
  61.1 0.0 copy-done.1
  61.1 0.0 copy-start.5
  61.1 1.4 copy.37
  62.5 7.0 %collective-permute-start.2 = (f32[2,128,128]{2,1,0:T(8,128)}, f32[2,128,128]{2,1,0:T(8,128)S(1)}, u32[]{:S(2)}, u32[]{:S(2)}) collective-permute-start(f32[2,128,128]{2,1,0:T(8,128)} %get-tuple-element.15), channel_id=1, source_target_pairs={{0,3},{1,4},{2,5},{3,6},{4,7},{5,0},{6,1},{7,2},{8,11},{9,12},{10,... | collective-permute-start | bytes 393224 | tf_op jit(solution)/shard_map/ppermute | solution.py:112
  69.5 3.0 collective-permute-start.3
  72.4 6.4 %collective-permute-start.4 = (f32[2,128,128]{2,1,0:T(8,128)}, f32[2,128,128]{2,1,0:T(8,128)S(1)}, u32[]{:S(2)}, u32[]{:S(2)}) collective-permute-start(f32[2,128,128]{2,1,0:T(8,128)} %get-tuple-element.17), channel_id=1, source_target_pairs={{0,5},{1,6},{2,7},{3,0},{4,1},{5,2},{6,3},{7,4},{8,13},{9,14},{10,... | collective-permute-start | bytes 393224 | tf_op jit(solution)/shard_map/ppermute | solution.py:112
  78.9 0.0 collective-permute-done
  78.9 3.2 collective-permute-start.5
  82.1 0.0 collective-permute-done.1
  82.1 2.2 collective-permute-start.6
  84.3 0.0 copy-done.5
  84.3 0.5 multiply_add_fusion.r_0_
  84.9 0.0 collective-permute-done.2
  84.9 0.5 collective-permute-done.3
  85.3 0.0 collective-permute-done.4
  85.3 11.6 %collective-permute-done.5 = f32[2,128,128]{2,1,0:T(8,128)S(1)} collective-permute-done((f32[2,128,128]{2,1,0:T(8,128)}, f32[2,128,128]{2,1,0:T(8,128)S(1)}, u32[]{:S(2)}, u32[]{:S(2)}) %collective-permute-start.5) | collective-permute-done | bytes 131104 | tf_op jit(solution)/shard_map/ppermute | solution.py:112
  96.9 0.5 collective-permute-done.6
  97.4 1.0 fusion.44
  98.4 220.2 %all-to-all-done.1.r_2_.r_3_.r_4_.r_5_.r_6_.r_7_.r_8_.r_9_.r_10_.r_11_.r_12_.r_13_.r_14_.r_15_.r_16_.r_17_.r_18_.r_19_.r_20_.r_21_.r_22_.r_23_.r_24_.r_25_ = bf16[128,384,128]{2,1,0:T(8,128)(2,1)} async-done(((bf16[128,384,128]{2,1,0:T(8,128)(2,1)}), bf16[128,384,128]{2,1,0:T(8,128)(2,1)}, u32[]{:S(2)}, u32[]{:S(2)}) %all-to-all-start.1) | async-done | bytes 12582944 | tf_op jit(solution)/shard_map/all_to_all | solution.py:102
  318.5 9.4 %shard_map.73 = bf16[16,128,128]{2,1,0:T(8,128)(2,1)} custom-call(s32[96]{0:T(128)} %multiply_add_fusion.r_0_, bf16[16,128,256]{2,1,0:T(8,128)(2,1)} %bitcast.62, bf16[128,384,128]{2,1,0:T(8,128)(2,1)} %all-to-all-done.1.r_2_.r_3_.r_4_.r_5_.r_6_.r_7_.r_8_.r_9_.r_10_.r_11_.r_12_.r_13_.r_14_.r_15_.r_16_.r_17_.r_18_.r_19_.r_20_.r_21_.r_22_.r_23_.r_24_.r_25_, ...), custom_call_target="tpu_custom_call" | custom-call | flops 1610612736 | bytes 11010048 | tf_op jit(solution)/shard_map/pallas_call | solution.py:53
  327.9 0.0 copy-start.3
  327.9 0.0 copy-start.4
  328.0 28.3 %all_to_all.16 = bf16[8,2,128,128]{3,2,1,0:T(8,128)(2,1)S(1)} all-to-all(bf16[8,2,128,128]{3,2,1,0:T(8,128)(2,1)} %bitcast.63), channel_id=1, replica_groups=mesh['pairs'=64,'aux'=8] {'aux'}, dimensions={0} | all-to-all | bytes 1048576 | tf_op jit(solution)/shard_map/all_to_all | solution.py:123
  356.3 0.1 convert_reduce_fusion
  356.3 0.0 copy-done.3
  356.3 0.0 copy-done.4
  356.4 1.6 divide_subtract_fusion
  (5 shorter events, 0.1 us)
Async XLA Ops:
  0.0 14.2 %copy-start = (bf16[40,128,128]{2,1,0:T(8,128)(2,1)S(1)}, bf16[40,128,128]{2,1,0:T(8,128)(2,1)}, u32[]{:S(2)}) copy-start(bf16[40,128,128]{2,1,0:T(8,128)(2,1)} %param.9) | copy-start | bytes 3932164
  2.5 21.2 %all-to-all-start = ((s32[64,1,2]{2,1,0:T(1,128)}), s32[64,1,2]{2,1,0:T(1,128)S(1)}, u32[]{:S(2)}, u32[]{:S(2)}) async-start(s32[64,1,2]{2,1,0:T(1,128)} %bitcast.4), calls=%async_computation | async-start | bytes 65536 | tf_op jit(solution)/shard_map/all_to_all | solution.py:85
  32.2 10.8 %copy-start.2 = (bf16[16,128,128]{2,1,0:T(8,128)(2,1)S(1)}, bf16[16,128,128]{2,1,0:T(8,128)(2,1)}, u32[]{:S(2)}) copy-start(bf16[16,128,128]{2,1,0:T(8,128)(2,1)} %param.7) | copy-start | bytes 1572868
  32.2 286.4 %all-to-all-start.1 = ((bf16[128,384,128]{2,1,0:T(8,128)(2,1)}), bf16[128,384,128]{2,1,0:T(8,128)(2,1)}, u32[]{:S(2)}, u32[]{:S(2)}) async-start(bf16[128,384,128]{2,1,0:T(8,128)(2,1)} %gather_fusion), calls=%async_computation.1 | async-start | bytes 25165824 | tf_op jit(solution)/shard_map/all_to_all | solution.py:102
  50.3 10.8 %copy-start.1 = (bf16[16,256,128]{2,1,0:T(8,128)(2,1)S(1)}, bf16[16,256,128]{2,1,0:T(8,128)(2,1)}, u32[]{:S(2)}) copy-start(bf16[16,256,128]{2,1,0:T(8,128)(2,1)} %param.8) | copy-start | bytes 3145732
  51.3 27.6 %collective-permute-start = (f32[2,128,128]{2,1,0:T(8,128)}, f32[2,128,128]{2,1,0:T(8,128)S(1)}, u32[]{:S(2)}, u32[]{:S(2)}) collective-permute-start(f32[2,128,128]{2,1,0:T(8,128)} %get-tuple-element.13), channel_id=1, source_target_pairs={{0,1},{1,2},{2,3},{3,4},{4,5},{5,6},{6,7},{7,0},{8,9},{9,10},{10,1... | collective-permute-start | bytes 393224 | tf_op jit(solution)/shard_map/ppermute | solution.py:112
  55.2 26.8 %collective-permute-start.1 = (f32[2,128,128]{2,1,0:T(8,128)}, f32[2,128,128]{2,1,0:T(8,128)}, u32[]{:S(2)}, u32[]{:S(2)}) collective-permute-start(f32[2,128,128]{2,1,0:T(8,128)} %get-tuple-element.14), channel_id=1, source_target_pairs={{0,2},{1,3},{2,4},{3,5},{4,6},{5,7},{6,0},{7,1},{8,10},{9,11},{10,... | collective-permute-start | bytes 393224 | tf_op jit(solution)/shard_map/ppermute | solution.py:112
  61.1 23.2 %copy-start.5 = (s32[96,1]{0,1:T(1,128)S(1)}, s32[96,1]{0,1:T(1,128)}, u32[]{:S(2)}) copy-start(s32[96,1]{0,1:T(1,128)} %param.12) | copy-start | bytes 1156
  62.5 22.4 %collective-permute-start.2 = (f32[2,128,128]{2,1,0:T(8,128)}, f32[2,128,128]{2,1,0:T(8,128)S(1)}, u32[]{:S(2)}, u32[]{:S(2)}) collective-permute-start(f32[2,128,128]{2,1,0:T(8,128)} %get-tuple-element.15), channel_id=1, source_target_pairs={{0,3},{1,4},{2,5},{3,6},{4,7},{5,0},{6,1},{7,2},{8,11},{9,12},{10,... | collective-permute-start | bytes 393224 | tf_op jit(solution)/shard_map/ppermute | solution.py:112
  69.5 15.9 %collective-permute-start.3 = (f32[2,128,128]{2,1,0:T(8,128)}, f32[2,128,128]{2,1,0:T(8,128)S(1)}, u32[]{:S(2)}, u32[]{:S(2)}) collective-permute-start(f32[2,128,128]{2,1,0:T(8,128)} %get-tuple-element.16), channel_id=1, source_target_pairs={{0,4},{1,5},{2,6},{3,7},{4,0},{5,1},{6,2},{7,3},{8,12},{9,13},{10,... | collective-permute-start | bytes 393224 | tf_op jit(solution)/shard_map/ppermute | solution.py:112
  72.4 12.9 %collective-permute-start.4 = (f32[2,128,128]{2,1,0:T(8,128)}, f32[2,128,128]{2,1,0:T(8,128)S(1)}, u32[]{:S(2)}, u32[]{:S(2)}) collective-permute-start(f32[2,128,128]{2,1,0:T(8,128)} %get-tuple-element.17), channel_id=1, source_target_pairs={{0,5},{1,6},{2,7},{3,0},{4,1},{5,2},{6,3},{7,4},{8,13},{9,14},{10,... | collective-permute-start | bytes 393224 | tf_op jit(solution)/shard_map/ppermute | solution.py:112
  78.9 18.1 %collective-permute-start.5 = (f32[2,128,128]{2,1,0:T(8,128)}, f32[2,128,128]{2,1,0:T(8,128)S(1)}, u32[]{:S(2)}, u32[]{:S(2)}) collective-permute-start(f32[2,128,128]{2,1,0:T(8,128)} %get-tuple-element.18), channel_id=1, source_target_pairs={{0,6},{1,7},{2,0},{3,1},{4,2},{5,3},{6,4},{7,5},{8,14},{9,15},{10,... | collective-permute-start | bytes 393224 | tf_op jit(solution)/shard_map/ppermute | solution.py:112
  82.1 15.3 %collective-permute-start.6 = (f32[2,128,128]{2,1,0:T(8,128)S(1)}, f32[2,128,128]{2,1,0:T(8,128)S(1)}, u32[]{:S(2)}, u32[]{:S(2)}) collective-permute-start(f32[2,128,128]{2,1,0:T(8,128)S(1)} %fusion.36), channel_id=1, source_target_pairs={{0,7},{1,0},{2,1},{3,2},{4,3},{5,4},{6,5},{7,6},{8,15},{9,8},{10,9... | collective-permute-start | bytes 393224 | tf_op jit(solution)/shard_map/ppermute | solution.py:112
  327.9 28.4 %copy-start.3 = (bf16[2,128,128]{2,1,0:T(8,128)(2,1)S(1)}, bf16[2,128,128]{2,1,0:T(8,128)(2,1)}, u32[]{:S(2)}) copy-start(bf16[2,128,128]{2,1,0:T(8,128)(2,1)} %param.10) | copy-start | bytes 196612
  327.9 28.4 %copy-start.4 = (f32[2,128]{1,0:T(2,128)S(1)}, f32[2,128]{1,0:T(2,128)}, u32[]{:S(2)}) copy-start(f32[2,128]{1,0:T(2,128)} %param.11) | copy-start | bytes 3076

commit v9 on v6

--- a/solution.py
+++ b/solution.py
@@ -109,13 +109,22 @@
     flat, ladder_mine = lax.optimization_barrier((flat, ladder_mine))
 
     coef_t = jnp.transpose(pno_coef, (0, 2, 1))
-    linked = linked_sum(bucket, coef_t, flat, per_slice)
-
-    pieces = linked.reshape(aux_count, own_rows, pno_width, pno_width)
-    linked_mine = jnp.sum(
-        lax.all_to_all(pieces, "aux", split_axis=0, concat_axis=0, tiled=True).astype(jnp.float32),
-        axis=0,
-    )
+    bucket_rows = bucket.reshape(pair_dev, per_slice)
+    sums = []
+    for parity in range(own_rows):
+        linked = linked_sum(
+            bucket_rows[parity::own_rows].reshape(-1), coef_t[parity::own_rows], flat, per_slice
+        )
+        pieces = linked.reshape(aux_count, 1, pno_width, pno_width)
+        sums.append(
+            jnp.sum(
+                lax.all_to_all(pieces, "aux", split_axis=0, concat_axis=0, tiled=True).astype(
+                    jnp.float32
+                ),
+                axis=0,
+            )
+        )
+    linked_mine = jnp.concatenate(sums, axis=0)
     reduced = ladder_mine + linked_mine
     first_row = lax.axis_index("aux") * own_rows
     amp_mine = lax.dynamic_slice_in_dim(amplitudes, first_row, own_rows, 0)

time: 353 us -> 361 us (1.023)
  blocking collectives: 28.2 us -> 0 us
  waiting for transfers between devices: 234 us -> 251 us
  starting transfers between devices: 47.9 us -> 61.5 us
    all_to_all x1 -> x0, blocking collectives: 28.2 us -> none  [local(): lax.all_to_all(pieces, 'aux', split_axis=0, concat_axis=0, tiled=True)]
    all_to_all x0 -> x2, waiting for transfers between devices: none -> 17.7 us  [local(): lax.all_to_all(pieces, 'aux', split_axis=0, concat_axis=0, tiled=True)]
    all_to_all x0 -> x2, starting transfers between devices: none -> 13.4 us  [local(): lax.all_to_all(pieces, 'aux', split_axis=0, concat_axis=0, tiled=True)]
    pallas_call x1 -> x2, Pallas kernels: 9.4 us -> 12.3 us  [linked_sum(): pl.pallas_call(lambda *r: linked_kernel(links, pao_width, *r), grid_spec=...]
  transfers between devices with their start and end apart: 9 -> 11, of which waited for: 5 -> 7; matrix products, arithmetic and copies ran while one was open for 6% -> 6% of each run, Pallas kernels for 0% -> 2%
where the time goes in v9:
time: 361 us; the launch traced here: 360 us
  waiting for transfers between devices  251 us (70%)
  starting transfers between devices  61.5 us (17%)
  matrix products  14.5 us (4%)
  local copies, waits for them, and re-layouts  13.1 us (4%)
  Pallas kernels  12.3 us (3%)
  other arithmetic  7.69 us (2%)
    all_to_all x1, waiting for transfers between devices, local(): lax.all_to_all(items, 'pairs', split_axis=0, concat_axis=0, tiled=True)  212 us
    ppermute x7, starting transfers between devices, local(): lax.ppermute(piece, 'aux', [(i, (i + shift) % aux_count) for i in range(a...  30.5 us
    all_to_all x2, waiting for transfers between devices, local(): lax.all_to_all(pieces, 'aux', split_axis=0, concat_axis=0, tiled=True)  17.7 us
    dot_general x1, matrix products, local(): jnp.einsum('pqce,qfe->pcf', ladder_half, ladder_ints, preferred_element_t...  14.5 us
    all_to_all x2, starting transfers between devices, local(): lax.all_to_all(pieces, 'aux', split_axis=0, concat_axis=0, tiled=True)  13.4 us
    ppermute x7, waiting for transfers between devices, local(): lax.ppermute(piece, 'aux', [(i, (i + shift) % aux_count) for i in range(a...  13.2 us
    pallas_call x2, Pallas kernels, linked_sum(): pl.pallas_call(lambda *r: linked_kernel(links, pao_width, *r), grid_spec=...  12.3 us
    all_to_all x1, starting transfers between devices, local(): lax.all_to_all(wanted.reshape(groups, capacity), 'pairs', split_axis=0, c...  11.6 us
  transfers between devices with their start and end apart: 11, of which 7 were waited for; matrix products, arithmetic and copies ran while one was open for 6% of the time, Pallas kernels for 2%

profile of v9, /device:TPU:1, one launch (start us, length us, event | category | flops | bytes accessed | tf_op | source)
XLA Modules:
  0.0 360.1 jit_solution(5505399479932037538)
XLA Ops:
  0.0 0.0 copy-start
  0.0 0.8 add_bitcast_fusion
  0.8 0.9 convert_reduce_fusion.2
  1.7 0.7 multiply_reduce_fusion
  2.4 0.1 select_reduce_fusion
  2.5 0.8 sub.10
  3.2 11.6 %all-to-all-start = ((s32[64,1,2]{2,1,0:T(1,128)}), s32[64,1,2]{2,1,0:T(1,128)S(1)}, u32[]{:S(2)}, u32[]{:S(2)}) async-start(s32[64,1,2]{2,1,0:T(1,128)} %bitcast.4), calls=%async_computation | async-start | bytes 65536 | tf_op jit(solution)/shard_map/all_to_all | solution.py:85
  14.9 1.5 pad_maximum_fusion
  16.4 7.7 %all-to-all-done = s32[64,1,2]{2,1,0:T(1,128)S(1)} async-done(((s32[64,1,2]{2,1,0:T(1,128)}), s32[64,1,2]{2,1,0:T(1,128)S(1)}, u32[]{:S(2)}, u32[]{:S(2)}) %all-to-all-start) | async-done | bytes 544 | tf_op jit(solution)/shard_map/all_to_all | solution.py:85
  24.1 0.1 maximum_reduce_fusion
  24.2 0.1 reshape.59
  24.3 8.3 %gather_fusion = bf16[128,384,128]{2,1,0:T(8,128)(2,1)} fusion(bf16[16,384,128]{2,1,0:T(8,128)(2,1)S(1)} %pad_maximum_fusion, s32[1024]{0:T(1024)S(1)} %pad_clamp_fusion), kind=kCustom, calls=%fused_computation | custom fusion | bytes 25166336 | tf_op jit(solution)/shard_map/gather | solution.py:90
  32.6 0.0 copy-start.3
  32.6 6.0 %all-to-all-start.1 = ((bf16[128,384,128]{2,1,0:T(8,128)(2,1)}), bf16[128,384,128]{2,1,0:T(8,128)(2,1)}, u32[]{:S(2)}, u32[]{:S(2)}) async-start(bf16[128,384,128]{2,1,0:T(8,128)(2,1)} %gather_fusion), calls=%async_computation.1 | async-start | bytes 25165824 | tf_op jit(solution)/shard_map/all_to_all | solution.py:91
  38.7 0.0 copy-done
  38.7 0.0 copy-done.3
  38.7 14.5 %fusion.5 = f32[16,128,128]{2,1,0:T(8,128)S(1)} fusion(bf16[40,128,128]{2,1,0:T(8,128)(2,1)S(1)} %copy-done, bf16[16,128,128]{2,1,0:T(8,128)(2,1)S(1)} %copy-done.3), kind=kOutput, calls=%fused_computation.6 | convolution fusion | flops 5379194880 | bytes 2883584 | tf_op jit(solution)/shard_map/pqce,qfe->pcf/dot_general | solution.py:96
  53.2 0.0 copy-start.2
  53.2 0.0 copy-start.1
  53.2 0.9 constant_dynamic-slice_fusion.6
  54.1 10.6 %collective-permute-start.6 = (f32[2,128,128]{2,1,0:T(8,128)}, f32[2,128,128]{2,1,0:T(8,128)}, u32[]{:S(2)}, u32[]{:S(2)}) collective-permute-start(f32[2,128,128]{2,1,0:T(8,128)} %get-tuple-element.12), channel_id=1, source_target_pairs={{0,7},{1,0},{2,1},{3,2},{4,3},{5,4},{6,5},{7,6},{8,15},{9,8},{10,9... | collective-permute-start | bytes 393224 | tf_op jit(solution)/shard_map/ppermute | solution.py:105
  64.7 2.2 collective-permute-start.5
  66.9 1.9 collective-permute-start.4
  68.8 7.3 %collective-permute-start.3 = (f32[2,128,128]{2,1,0:T(8,128)}, f32[2,128,128]{2,1,0:T(8,128)}, u32[]{:S(2)}, u32[]{:S(2)}) collective-permute-start(f32[2,128,128]{2,1,0:T(8,128)} %get-tuple-element.15), channel_id=1, source_target_pairs={{0,4},{1,5},{2,6},{3,7},{4,0},{5,1},{6,2},{7,3},{8,12},{9,13},{10,... | collective-permute-start | bytes 393224 | tf_op jit(solution)/shard_map/ppermute | solution.py:105
  76.1 0.0 copy-done.2
  76.1 1.9 collective-permute-start.2
  78.1 0.0 copy-done.1
  78.1 0.5 copy.19
  78.6 0.0 collective-permute-done.6
  78.6 3.1 collective-permute-start.1
  81.7 0.0 collective-permute-done.5
  81.7 3.5 collective-permute-start
  85.3 1.0 fusion.17
  86.3 0.1 reduce_sum.47
  86.4 0.1 mul.59
  86.5 0.6 reshape.55.r_0_
  87.1 0.0 collective-permute-done.4
  87.1 0.0 collective-permute-done.3
  87.1 0.9 collective-permute-done.2
  88.1 8.4 %collective-permute-done.1 = f32[2,128,128]{2,1,0:T(8,128)S(1)} collective-permute-done((f32[2,128,128]{2,1,0:T(8,128)}, f32[2,128,128]{2,1,0:T(8,128)S(1)}, u32[]{:S(2)}, u32[]{:S(2)}) %collective-permute-start.1) | collective-permute-done | bytes 131104 | tf_op jit(solution)/shard_map/ppermute | solution.py:105
  96.5 3.9 %collective-permute-done = f32[2,128,128]{2,1,0:T(8,128)S(1)} collective-permute-done((f32[2,128,128]{2,1,0:T(8,128)S(1)}, f32[2,128,128]{2,1,0:T(8,128)S(1)}, u32[]{:S(2)}, u32[]{:S(2)}) %collective-permute-start) | collective-permute-done | bytes 131104 | tf_op jit(solution)/shard_map/ppermute | solution.py:105
  100.4 1.9 add_add_fusion
  102.3 212.1 %all-to-all-done.1.r_2_.r_3_.r_4_.r_5_.r_6_.r_7_.r_8_.r_9_.r_10_.r_11_.r_12_.r_13_.r_14_.r_15_.r_16_.r_17_.r_18_.r_19_.r_20_.r_21_.r_22_.r_23_.r_24_.r_25_ = bf16[128,384,128]{2,1,0:T(8,128)(2,1)} async-done(((bf16[128,384,128]{2,1,0:T(8,128)(2,1)}), bf16[128,384,128]{2,1,0:T(8,128)(2,1)}, u32[]{:S(2)}, u32[]{:S(2)}) %all-to-all-start.1) | async-done | bytes 12582944 | tf_op jit(solution)/shard_map/all_to_all | solution.py:91
  314.3 6.1 %shard_map.74 = bf16[8,128,128]{2,1,0:T(8,128)(2,1)} custom-call(s32[48]{0:T(128)} %reshape.55.r_0_, bf16[8,128,256]{2,1,0:T(8,128)(2,1)} %get-tuple-element.10.r_1_, bf16[128,384,128]{2,1,0:T(8,128)(2,1)} %all-to-all-done.1.r_2_.r_3_.r_4_.r_5_.r_6_.r_7_.r_8_.r_9_.r_10_.r_11_.r_12_.r_13_.r_14_.r_15_.r_16_.r_17_.r_18_.r_19_.r_20_.r_21_.r_22_.r_23_.r_24_.r_25_, ...), custom_call_target="tpu_custom_call" | custom-call | flops 805306368 | bytes 5505024 | tf_op jit(solution)/shard_map/pallas_call | solution.py:53
  320.4 10.0 %all-to-all-start.3 = ((bf16[8,1,128,128]{3,2,1,0:T(8,128)(2,1)}), bf16[8,1,128,128]{3,2,1,0:T(8,128)(2,1)S(1)}, u32[]{:S(2)}, u32[]{:S(2)}) async-start(bf16[8,1,128,128]{3,2,1,0:T(8,128)(2,1)} %bitcast.38), calls=%async_computation.3 | async-start | bytes 524288 | tf_op jit(solution)/shard_map/all_to_all | solution.py:121
  330.4 0.6 reshape.53.r_0_
  331.0 0.0 copy-start.4
  331.0 0.0 copy-start.5
  331.0 0.0 copy-start.6
  331.0 6.2 %shard_map.73 = bf16[8,128,128]{2,1,0:T(8,128)(2,1)} custom-call(s32[48]{0:T(128)} %reshape.53.r_0_, bf16[8,128,256]{2,1,0:T(8,128)(2,1)} %get-tuple-element.9.r_1_, bf16[128,384,128]{2,1,0:T(8,128)(2,1)} %all-to-all-done.1.r_2_.r_3_.r_4_.r_5_.r_6_.r_7_.r_8_.r_9_.r_10_.r_11_.r_12_.r_13_.r_14_.r_15_.r_16_.r_17_.r_18_.r_19_.r_20_.r_21_.r_22_.r_23_.r_24_.r_25_, ...), custom_call_target="tpu_custom_call" | custom-call | flops 805306368 | bytes 5505024 | tf_op jit(solution)/shard_map/pallas_call | solution.py:53
  337.2 5.6 %all-to-all-done.3 = bf16[8,1,128,128]{3,2,1,0:T(8,128)(2,1)S(1)} async-done(((bf16[8,1,128,128]{3,2,1,0:T(8,128)(2,1)}), bf16[8,1,128,128]{3,2,1,0:T(8,128)(2,1)S(1)}, u32[]{:S(2)}, u32[]{:S(2)}) %all-to-all-start.3) | async-done | bytes 262176 | tf_op jit(solution)/shard_map/all_to_all | solution.py:121
  342.8 3.4 all-to-all-start.2
  346.3 12.2 %all-to-all-done.2 = bf16[8,1,128,128]{3,2,1,0:T(8,128)(2,1)S(1)} async-done(((bf16[8,1,128,128]{3,2,1,0:T(8,128)(2,1)}), bf16[8,1,128,128]{3,2,1,0:T(8,128)(2,1)S(1)}, u32[]{:S(2)}, u32[]{:S(2)}) %all-to-all-start.2) | async-done | bytes 262176 | tf_op jit(solution)/shard_map/all_to_all | solution.py:121
  358.5 0.0 copy-done.4
  358.5 0.0 copy-done.5
  358.5 0.0 copy-done.6
  358.5 1.6 fusion.14
  (7 shorter events, 0.1 us)
Async XLA Ops:
  0.0 38.7 %copy-start = (bf16[40,128,128]{2,1,0:T(8,128)(2,1)S(1)}, bf16[40,128,128]{2,1,0:T(8,128)(2,1)}, u32[]{:S(2)}) copy-start(bf16[40,128,128]{2,1,0:T(8,128)(2,1)} %param.9) | copy-start | bytes 3932164
  3.2 20.8 %all-to-all-start = ((s32[64,1,2]{2,1,0:T(1,128)}), s32[64,1,2]{2,1,0:T(1,128)S(1)}, u32[]{:S(2)}, u32[]{:S(2)}) async-start(s32[64,1,2]{2,1,0:T(1,128)} %bitcast.4), calls=%async_computation | async-start | bytes 65536 | tf_op jit(solution)/shard_map/all_to_all | solution.py:85
  32.6 6.0 %copy-start.3 = (bf16[16,128,128]{2,1,0:T(8,128)(2,1)S(1)}, bf16[16,128,128]{2,1,0:T(8,128)(2,1)}, u32[]{:S(2)}) copy-start(bf16[16,128,128]{2,1,0:T(8,128)(2,1)} %param.7) | copy-start | bytes 1572868
  32.6 281.7 %all-to-all-start.1 = ((bf16[128,384,128]{2,1,0:T(8,128)(2,1)}), bf16[128,384,128]{2,1,0:T(8,128)(2,1)}, u32[]{:S(2)}, u32[]{:S(2)}) async-start(bf16[128,384,128]{2,1,0:T(8,128)(2,1)} %gather_fusion), calls=%async_computation.1 | async-start | bytes 25165824 | tf_op jit(solution)/shard_map/all_to_all | solution.py:91
  53.2 22.9 %copy-start.2 = (f32[16,128,128]{2,1,0:T(8,128)}, f32[16,128,128]{2,1,0:T(8,128)S(1)}, u32[]{:S(2)}) copy-start(f32[16,128,128]{2,1,0:T(8,128)S(1)} %fusion.5) | copy-start | bytes 3145732
  53.2 24.9 %copy-start.1 = (bf16[16,256,128]{2,1,0:T(8,128)(2,1)S(1)}, bf16[16,256,128]{2,1,0:T(8,128)(2,1)}, u32[]{:S(2)}) copy-start(bf16[16,256,128]{2,1,0:T(8,128)(2,1)} %param.8) | copy-start | bytes 3145732
  54.1 24.5 %collective-permute-start.6 = (f32[2,128,128]{2,1,0:T(8,128)}, f32[2,128,128]{2,1,0:T(8,128)}, u32[]{:S(2)}, u32[]{:S(2)}) collective-permute-start(f32[2,128,128]{2,1,0:T(8,128)} %get-tuple-element.12), channel_id=1, source_target_pairs={{0,7},{1,0},{2,1},{3,2},{4,3},{5,4},{6,5},{7,6},{8,15},{9,8},{10,9... | collective-permute-start | bytes 393224 | tf_op jit(solution)/shard_map/ppermute | solution.py:105
  64.7 17.0 %collective-permute-start.5 = (f32[2,128,128]{2,1,0:T(8,128)}, f32[2,128,128]{2,1,0:T(8,128)}, u32[]{:S(2)}, u32[]{:S(2)}) collective-permute-start(f32[2,128,128]{2,1,0:T(8,128)} %get-tuple-element.13), channel_id=1, source_target_pairs={{0,6},{1,7},{2,0},{3,1},{4,2},{5,3},{6,4},{7,5},{8,14},{9,15},{10,... | collective-permute-start | bytes 393224 | tf_op jit(solution)/shard_map/ppermute | solution.py:105
  66.9 20.2 %collective-permute-start.4 = (f32[2,128,128]{2,1,0:T(8,128)}, f32[2,128,128]{2,1,0:T(8,128)}, u32[]{:S(2)}, u32[]{:S(2)}) collective-permute-start(f32[2,128,128]{2,1,0:T(8,128)} %get-tuple-element.14), channel_id=1, source_target_pairs={{0,5},{1,6},{2,7},{3,0},{4,1},{5,2},{6,3},{7,4},{8,13},{9,14},{10,... | collective-permute-start | bytes 393224 | tf_op jit(solution)/shard_map/ppermute | solution.py:105
  68.8 18.3 %collective-permute-start.3 = (f32[2,128,128]{2,1,0:T(8,128)}, f32[2,128,128]{2,1,0:T(8,128)}, u32[]{:S(2)}, u32[]{:S(2)}) collective-permute-start(f32[2,128,128]{2,1,0:T(8,128)} %get-tuple-element.15), channel_id=1, source_target_pairs={{0,4},{1,5},{2,6},{3,7},{4,0},{5,1},{6,2},{7,3},{8,12},{9,13},{10,... | collective-permute-start | bytes 393224 | tf_op jit(solution)/shard_map/ppermute | solution.py:105
  76.1 11.9 %collective-permute-start.2 = (f32[2,128,128]{2,1,0:T(8,128)}, f32[2,128,128]{2,1,0:T(8,128)}, u32[]{:S(2)}, u32[]{:S(2)}) collective-permute-start(f32[2,128,128]{2,1,0:T(8,128)} %get-tuple-element.16), channel_id=1, source_target_pairs={{0,3},{1,4},{2,5},{3,6},{4,7},{5,0},{6,1},{7,2},{8,11},{9,12},{10,... | collective-permute-start | bytes 393224 | tf_op jit(solution)/shard_map/ppermute | solution.py:105
  78.6 17.9 %collective-permute-start.1 = (f32[2,128,128]{2,1,0:T(8,128)}, f32[2,128,128]{2,1,0:T(8,128)S(1)}, u32[]{:S(2)}, u32[]{:S(2)}) collective-permute-start(f32[2,128,128]{2,1,0:T(8,128)} %get-tuple-element.17), channel_id=1, source_target_pairs={{0,2},{1,3},{2,4},{3,5},{4,6},{5,7},{6,0},{7,1},{8,10},{9,11},{10,... | collective-permute-start | bytes 393224 | tf_op jit(solution)/shard_map/ppermute | solution.py:105
  81.7 18.6 %collective-permute-start = (f32[2,128,128]{2,1,0:T(8,128)S(1)}, f32[2,128,128]{2,1,0:T(8,128)S(1)}, u32[]{:S(2)}, u32[]{:S(2)}) collective-permute-start(f32[2,128,128]{2,1,0:T(8,128)S(1)} %get-tuple-element.11), channel_id=1, source_target_pairs={{0,1},{1,2},{2,3},{3,4},{4,5},{5,6},{6,7},{7,0},{8,9},{9,10},{10,1... | collective-permute-start | bytes 393224 | tf_op jit(solution)/shard_map/ppermute | solution.py:105
  320.4 22.4 %all-to-all-start.3 = ((bf16[8,1,128,128]{3,2,1,0:T(8,128)(2,1)}), bf16[8,1,128,128]{3,2,1,0:T(8,128)(2,1)S(1)}, u32[]{:S(2)}, u32[]{:S(2)}) async-start(bf16[8,1,128,128]{3,2,1,0:T(8,128)(2,1)} %bitcast.38), calls=%async_computation.3 | async-start | bytes 524288 | tf_op jit(solution)/shard_map/all_to_all | solution.py:121
  331.0 27.5 %copy-start.4 = (f32[2,128,128]{2,1,0:T(8,128)S(1)}, f32[2,128,128]{2,1,0:T(8,128)}, u32[]{:S(2)}) copy-start(f32[2,128,128]{2,1,0:T(8,128)} %add_add_fusion) | copy-start | bytes 393220
  331.0 27.5 %copy-start.5 = (bf16[2,128,128]{2,1,0:T(8,128)(2,1)S(1)}, bf16[2,128,128]{2,1,0:T(8,128)(2,1)}, u32[]{:S(2)}) copy-start(bf16[2,128,128]{2,1,0:T(8,128)(2,1)} %param.10) | copy-start | bytes 196612
  331.0 27.5 %copy-start.6 = (f32[2,128]{1,0:T(2,128)S(1)}, f32[2,128]{1,0:T(2,128)}, u32[]{:S(2)}) copy-start(f32[2,128]{1,0:T(2,128)} %param.11) | copy-start | bytes 3076
  342.8 15.6 %all-to-all-start.2 = ((bf16[8,1,128,128]{3,2,1,0:T(8,128)(2,1)}), bf16[8,1,128,128]{3,2,1,0:T(8,128)(2,1)S(1)}, u32[]{:S(2)}, u32[]{:S(2)}) async-start(bf16[8,1,128,128]{3,2,1,0:T(8,128)(2,1)} %bitcast.39), calls=%async_computation.2 | async-start | bytes 524288 | tf_op jit(solution)/shard_map/all_to_all | solution.py:121

commit v10 on v6

--- a/solution.py
+++ b/solution.py
@@ -106,7 +106,12 @@
             piece, "aux", [(i, (i + shift) % aux_count) for i in range(aux_count)]
         )
 
-    flat, ladder_mine = lax.optimization_barrier((flat, ladder_mine))
+    amp_mine = lax.dynamic_slice_in_dim(amplitudes, aux_me * own_rows, own_rows, 0)
+    denominator = pno_energy[:, :, None] + pno_energy[:, None, :]
+    base = amp_mine.astype(jnp.float32) - (
+        coulomb_ints.astype(jnp.float32) + ladder_mine
+    ) / denominator
+    flat, base = lax.optimization_barrier((flat, base))
 
     coef_t = jnp.transpose(pno_coef, (0, 2, 1))
     linked = linked_sum(bucket, coef_t, flat, per_slice)
@@ -116,12 +121,7 @@
         lax.all_to_all(pieces, "aux", split_axis=0, concat_axis=0, tiled=True).astype(jnp.float32),
         axis=0,
     )
-    reduced = ladder_mine + linked_mine
-    first_row = lax.axis_index("aux") * own_rows
-    amp_mine = lax.dynamic_slice_in_dim(amplitudes, first_row, own_rows, 0)
-    residual = coulomb_ints.astype(jnp.float32) + reduced
-    denominator = pno_energy[:, :, None] + pno_energy[:, None, :]
-    return amp_mine.astype(jnp.float32) - residual / denominator
+    return base - linked_mine / denominator
 
 
 def solution(mesh):

time: 353 us -> 352 us (level)
  no operation moved by 1% of the time
where the time goes in v10:
time: 352 us
  waiting for transfers between devices  235 us (67%)
  starting transfers between devices  47.8 us (14%)
  blocking collectives  28.1 us (8%)
  matrix products  14.4 us (4%)
  local copies, waits for them, and re-layouts  11.5 us (3%)
  Pallas kernels  9.41 us (3%)
  other arithmetic  6.02 us (2%)
    all_to_all x1, waiting for transfers between devices, local(): lax.all_to_all(items, 'pairs', split_axis=0, concat_axis=0, tiled=True)  213 us
    ppermute x7, starting transfers between devices, local(): lax.ppermute(piece, 'aux', [(i, (i + shift) % aux_count) for i in range(a...  30.3 us
    all_to_all x1, blocking collectives, local(): lax.all_to_all(pieces, 'aux', split_axis=0, concat_axis=0, tiled=True)  28.1 us
    dot_general x1, matrix products, local(): jnp.einsum('pqce,qfe->pcf', ladder_half, ladder_ints, preferred_element_t...  14.4 us
    ppermute x7, waiting for transfers between devices, local(): lax.ppermute(piece, 'aux', [(i, (i + shift) % aux_count) for i in range(a...  14 us
    all_to_all x1, starting transfers between devices, local(): lax.all_to_all(wanted.reshape(groups, capacity), 'pairs', split_axis=0, c...  11.6 us
    pallas_call x1, Pallas kernels, linked_sum(): pl.pallas_call(lambda *r: linked_kernel(links, pao_width, *r), grid_spec=...  9.41 us
    gather x1, local copies, waits for them, and re-layouts, local(): items = both[picked.reshape(groups * capacity)]  8.31 us
  transfers between devices with their start and end apart: 9, of which 5 were waited for; matrix products, arithmetic and copies ran while one was open for 6% of the time, Pallas kernels for 0%

profile of v10, /device:TPU:1, one launch (start us, length us, event | category | flops | bytes accessed | tf_op | source)
XLA Modules:
  0.0 351.9 jit_solution(6107438556827591782)
XLA Ops:
  0.0 0.0 copy-start
  0.0 1.0 convert_reduce_fusion.1
  1.0 0.7 fusion.15
  1.6 0.1 select_reduce_fusion
  1.8 0.8 sub.13
  2.5 11.6 %all-to-all-start = ((s32[64,1,2]{2,1,0:T(1,128)}), s32[64,1,2]{2,1,0:T(1,128)S(1)}, u32[]{:S(2)}, u32[]{:S(2)}) async-start(s32[64,1,2]{2,1,0:T(1,128)} %bitcast.4), calls=%async_computation | async-start | bytes 65536 | tf_op jit(solution)/shard_map/all_to_all | solution.py:85
  14.2 1.5 pad_maximum_fusion
  15.7 7.7 %all-to-all-done = s32[64,1,2]{2,1,0:T(1,128)S(1)} async-done(((s32[64,1,2]{2,1,0:T(1,128)}), s32[64,1,2]{2,1,0:T(1,128)S(1)}, u32[]{:S(2)}, u32[]{:S(2)}) %all-to-all-start) | async-done | bytes 544 | tf_op jit(solution)/shard_map/all_to_all | solution.py:85
  23.4 0.1 maximum_reduce_fusion
  23.5 0.1 reshape.40
  23.6 8.3 %gather_fusion = bf16[128,384,128]{2,1,0:T(8,128)(2,1)} fusion(bf16[16,384,128]{2,1,0:T(8,128)(2,1)S(1)} %pad_maximum_fusion, s32[1024]{0:T(1024)S(1)} %pad_clamp_fusion), kind=kCustom, calls=%fused_computation | custom fusion | bytes 25166336 | tf_op jit(solution)/shard_map/gather | solution.py:90
  31.9 0.0 copy-start.2
  31.9 5.9 %all-to-all-start.1 = ((bf16[128,384,128]{2,1,0:T(8,128)(2,1)}), bf16[128,384,128]{2,1,0:T(8,128)(2,1)}, u32[]{:S(2)}, u32[]{:S(2)}) async-start(bf16[128,384,128]{2,1,0:T(8,128)(2,1)} %gather_fusion), calls=%async_computation.1 | async-start | bytes 25165824 | tf_op jit(solution)/shard_map/all_to_all | solution.py:91
  37.9 0.0 copy-done
  37.9 0.0 copy-done.2
  37.9 14.4 %fusion.5 = f32[16,128,128]{2,1,0:T(8,128)S(1)} fusion(bf16[40,128,128]{2,1,0:T(8,128)(2,1)S(1)} %copy-done, bf16[16,128,128]{2,1,0:T(8,128)(2,1)S(1)} %copy-done.2), kind=kOutput, calls=%fused_computation.6 | convolution fusion | flops 5379194880 | bytes 2883584 | tf_op jit(solution)/shard_map/pqce,qfe->pcf/dot_general | solution.py:96
  52.3 0.0 copy-start.1
  52.3 0.0 copy-start.4
  52.3 0.0 copy-start.3
  52.3 0.9 constant_dynamic-slice_fusion.5
  53.2 10.7 %collective-permute-start.6 = (f32[2,128,128]{2,1,0:T(8,128)}, f32[2,128,128]{2,1,0:T(8,128)}, u32[]{:S(2)}, u32[]{:S(2)}) collective-permute-start(f32[2,128,128]{2,1,0:T(8,128)} %get-tuple-element.10), channel_id=1, source_target_pairs={{0,7},{1,0},{2,1},{3,2},{4,3},{5,4},{6,5},{7,6},{8,15},{9,8},{10,9... | collective-permute-start | bytes 393224 | tf_op jit(solution)/shard_map/ppermute | solution.py:105
  64.0 2.1 collective-permute-start.5
  66.1 1.9 collective-permute-start.4
  68.1 7.2 %collective-permute-start.3 = (f32[2,128,128]{2,1,0:T(8,128)}, f32[2,128,128]{2,1,0:T(8,128)}, u32[]{:S(2)}, u32[]{:S(2)}) collective-permute-start(f32[2,128,128]{2,1,0:T(8,128)} %get-tuple-element.13), channel_id=1, source_target_pairs={{0,4},{1,5},{2,6},{3,7},{4,0},{5,1},{6,2},{7,3},{8,12},{9,13},{10,... | collective-permute-start | bytes 393224 | tf_op jit(solution)/shard_map/ppermute | solution.py:105
  75.3 1.9 collective-permute-start.2
  77.2 0.0 copy-done.1
  77.2 1.4 copy.17
  78.6 0.0 collective-permute-done.6
  78.6 3.2 collective-permute-start.1
  81.8 0.0 collective-permute-done.5
  81.8 3.1 collective-permute-start
  84.9 0.0 copy-done.4
  84.9 0.5 multiply_add_fusion.r_0_
  85.5 0.0 collective-permute-done.4
  85.5 0.0 collective-permute-done.3
  85.5 1.6 collective-permute-done.2
  87.1 8.5 %collective-permute-done.1 = f32[2,128,128]{2,1,0:T(8,128)S(1)} collective-permute-done((f32[2,128,128]{2,1,0:T(8,128)}, f32[2,128,128]{2,1,0:T(8,128)S(1)}, u32[]{:S(2)}, u32[]{:S(2)}) %collective-permute-start.1) | collective-permute-done | bytes 131104 | tf_op jit(solution)/shard_map/ppermute | solution.py:105
  95.6 3.8 %collective-permute-done = f32[2,128,128]{2,1,0:T(8,128)S(1)} collective-permute-done((f32[2,128,128]{2,1,0:T(8,128)S(1)}, f32[2,128,128]{2,1,0:T(8,128)S(1)}, u32[]{:S(2)}, u32[]{:S(2)}) %collective-permute-start) | collective-permute-done | bytes 131104 | tf_op jit(solution)/shard_map/ppermute | solution.py:105
  99.4 0.0 copy-done.3
  99.4 1.3 fusion.12
  100.7 212.9 %all-to-all-done.1.r_2_.r_3_.r_4_.r_5_.r_6_.r_7_.r_8_.r_9_.r_10_.r_11_.r_12_.r_13_.r_14_.r_15_.r_16_.r_17_.r_18_.r_19_.r_20_.r_21_.r_22_.r_23_.r_24_.r_25_ = bf16[128,384,128]{2,1,0:T(8,128)(2,1)} async-done(((bf16[128,384,128]{2,1,0:T(8,128)(2,1)}), bf16[128,384,128]{2,1,0:T(8,128)(2,1)}, u32[]{:S(2)}, u32[]{:S(2)}) %all-to-all-start.1) | async-done | bytes 12582944 | tf_op jit(solution)/shard_map/all_to_all | solution.py:91
  313.6 9.4 %shard_map.73 = bf16[16,128,128]{2,1,0:T(8,128)(2,1)} custom-call(s32[96]{0:T(128)} %multiply_add_fusion.r_0_, bf16[16,128,256]{2,1,0:T(8,128)(2,1)} %bitcast.31, bf16[128,384,128]{2,1,0:T(8,128)(2,1)} %all-to-all-done.1.r_2_.r_3_.r_4_.r_5_.r_6_.r_7_.r_8_.r_9_.r_10_.r_11_.r_12_.r_13_.r_14_.r_15_.r_16_.r_17_.r_18_.r_19_.r_20_.r_21_.r_22_.r_23_.r_24_.r_25_, ...), custom_call_target="tpu_custom_call" | custom-call | flops 1610612736 | bytes 11010048 | tf_op jit(solution)/shard_map/pallas_call | solution.py:53
  323.0 28.1 %all_to_all.16 = bf16[8,2,128,128]{3,2,1,0:T(8,128)(2,1)S(1)} all-to-all(bf16[8,2,128,128]{3,2,1,0:T(8,128)(2,1)} %bitcast.32), channel_id=1, replica_groups=mesh['pairs'=64,'aux'=8] {'aux'}, dimensions={0} | all-to-all | bytes 1048576 | tf_op jit(solution)/shard_map/all_to_all | solution.py:121
  351.1 0.1 convert_reduce_fusion
  351.1 0.8 fusion.13
  (2 shorter events, 0.0 us)
Async XLA Ops:
  0.0 37.9 %copy-start = (bf16[40,128,128]{2,1,0:T(8,128)(2,1)S(1)}, bf16[40,128,128]{2,1,0:T(8,128)(2,1)}, u32[]{:S(2)}) copy-start(bf16[40,128,128]{2,1,0:T(8,128)(2,1)} %param.9) | copy-start | bytes 3932164
  2.5 20.8 %all-to-all-start = ((s32[64,1,2]{2,1,0:T(1,128)}), s32[64,1,2]{2,1,0:T(1,128)S(1)}, u32[]{:S(2)}, u32[]{:S(2)}) async-start(s32[64,1,2]{2,1,0:T(1,128)} %bitcast.4), calls=%async_computation | async-start | bytes 65536 | tf_op jit(solution)/shard_map/all_to_all | solution.py:85
  31.9 6.0 %copy-start.2 = (bf16[16,128,128]{2,1,0:T(8,128)(2,1)S(1)}, bf16[16,128,128]{2,1,0:T(8,128)(2,1)}, u32[]{:S(2)}) copy-start(bf16[16,128,128]{2,1,0:T(8,128)(2,1)} %param.7) | copy-start | bytes 1572868
  31.9 281.7 %all-to-all-start.1 = ((bf16[128,384,128]{2,1,0:T(8,128)(2,1)}), bf16[128,384,128]{2,1,0:T(8,128)(2,1)}, u32[]{:S(2)}, u32[]{:S(2)}) async-start(bf16[128,384,128]{2,1,0:T(8,128)(2,1)} %gather_fusion), calls=%async_computation.1 | async-start | bytes 25165824 | tf_op jit(solution)/shard_map/all_to_all | solution.py:91
  52.3 24.9 %copy-start.1 = (bf16[16,256,128]{2,1,0:T(8,128)(2,1)S(1)}, bf16[16,256,128]{2,1,0:T(8,128)(2,1)}, u32[]{:S(2)}) copy-start(bf16[16,256,128]{2,1,0:T(8,128)(2,1)} %param.8) | copy-start | bytes 3145732
  52.3 32.6 %copy-start.4 = (s32[96,1]{0,1:T(1,128)S(1)}, s32[96,1]{0,1:T(1,128)}, u32[]{:S(2)}) copy-start(s32[96,1]{0,1:T(1,128)} %param.12) | copy-start | bytes 1156
  52.3 47.1 %copy-start.3 = (f32[2,128]{1,0:T(2,128)S(1)}, f32[2,128]{1,0:T(2,128)}, u32[]{:S(2)}) copy-start(f32[2,128]{1,0:T(2,128)} %param.11) | copy-start | bytes 3076
  53.2 25.4 %collective-permute-start.6 = (f32[2,128,128]{2,1,0:T(8,128)}, f32[2,128,128]{2,1,0:T(8,128)}, u32[]{:S(2)}, u32[]{:S(2)}) collective-permute-start(f32[2,128,128]{2,1,0:T(8,128)} %get-tuple-element.10), channel_id=1, source_target_pairs={{0,7},{1,0},{2,1},{3,2},{4,3},{5,4},{6,5},{7,6},{8,15},{9,8},{10,9... | collective-permute-start | bytes 393224 | tf_op jit(solution)/shard_map/ppermute | solution.py:105
  64.0 17.8 %collective-permute-start.5 = (f32[2,128,128]{2,1,0:T(8,128)}, f32[2,128,128]{2,1,0:T(8,128)}, u32[]{:S(2)}, u32[]{:S(2)}) collective-permute-start(f32[2,128,128]{2,1,0:T(8,128)} %get-tuple-element.11), channel_id=1, source_target_pairs={{0,6},{1,7},{2,0},{3,1},{4,2},{5,3},{6,4},{7,5},{8,14},{9,15},{10,... | collective-permute-start | bytes 393224 | tf_op jit(solution)/shard_map/ppermute | solution.py:105
  66.1 19.3 %collective-permute-start.4 = (f32[2,128,128]{2,1,0:T(8,128)}, f32[2,128,128]{2,1,0:T(8,128)}, u32[]{:S(2)}, u32[]{:S(2)}) collective-permute-start(f32[2,128,128]{2,1,0:T(8,128)} %get-tuple-element.12), channel_id=1, source_target_pairs={{0,5},{1,6},{2,7},{3,0},{4,1},{5,2},{6,3},{7,4},{8,13},{9,14},{10,... | collective-permute-start | bytes 393224 | tf_op jit(solution)/shard_map/ppermute | solution.py:105
  68.1 17.4 %collective-permute-start.3 = (f32[2,128,128]{2,1,0:T(8,128)}, f32[2,128,128]{2,1,0:T(8,128)}, u32[]{:S(2)}, u32[]{:S(2)}) collective-permute-start(f32[2,128,128]{2,1,0:T(8,128)} %get-tuple-element.13), channel_id=1, source_target_pairs={{0,4},{1,5},{2,6},{3,7},{4,0},{5,1},{6,2},{7,3},{8,12},{9,13},{10,... | collective-permute-start | bytes 393224 | tf_op jit(solution)/shard_map/ppermute | solution.py:105
  75.3 11.8 %collective-permute-start.2 = (f32[2,128,128]{2,1,0:T(8,128)}, f32[2,128,128]{2,1,0:T(8,128)}, u32[]{:S(2)}, u32[]{:S(2)}) collective-permute-start(f32[2,128,128]{2,1,0:T(8,128)} %get-tuple-element.14), channel_id=1, source_target_pairs={{0,3},{1,4},{2,5},{3,6},{4,7},{5,0},{6,1},{7,2},{8,11},{9,12},{10,... | collective-permute-start | bytes 393224 | tf_op jit(solution)/shard_map/ppermute | solution.py:105
  78.6 17.0 %collective-permute-start.1 = (f32[2,128,128]{2,1,0:T(8,128)}, f32[2,128,128]{2,1,0:T(8,128)S(1)}, u32[]{:S(2)}, u32[]{:S(2)}) collective-permute-start(f32[2,128,128]{2,1,0:T(8,128)} %get-tuple-element.15), channel_id=1, source_target_pairs={{0,2},{1,3},{2,4},{3,5},{4,6},{5,7},{6,0},{7,1},{8,10},{9,11},{10,... | collective-permute-start | bytes 393224 | tf_op jit(solution)/shard_map/ppermute | solution.py:105
  81.8 17.6 %collective-permute-start = (f32[2,128,128]{2,1,0:T(8,128)S(1)}, f32[2,128,128]{2,1,0:T(8,128)S(1)}, u32[]{:S(2)}, u32[]{:S(2)}) collective-permute-start(f32[2,128,128]{2,1,0:T(8,128)S(1)} %get-tuple-element.9), channel_id=1, source_target_pairs={{0,1},{1,2},{2,3},{3,4},{4,5},{5,6},{6,7},{7,0},{8,9},{9,10},{10,1... | collective-permute-start | bytes 393224 | tf_op jit(solution)/shard_map/ppermute | solution.py:105

commit v11 on v10

--- a/solution.py
+++ b/solution.py
@@ -117,10 +117,10 @@
     linked = linked_sum(bucket, coef_t, flat, per_slice)
 
     pieces = linked.reshape(aux_count, own_rows, pno_width, pno_width)
-    linked_mine = jnp.sum(
-        lax.all_to_all(pieces, "aux", split_axis=0, concat_axis=0, tiled=True).astype(jnp.float32),
-        axis=0,
-    )
+    got = lax.all_to_all(pieces, "aux", split_axis=0, concat_axis=0, tiled=True)
+    linked_mine = got[0].astype(jnp.float32)
+    for source in range(1, aux_count):
+        linked_mine = linked_mine + got[source].astype(jnp.float32)
     return base - linked_mine / denominator
 
 

time: 352 us -> 352 us (level)
  transfers between devices with their start and end apart: 9 -> 9, of which waited for: 5 -> 4; matrix products, arithmetic and copies ran while one was open for 6% -> 6% of each run, Pallas kernels for 0% -> 0%
where the time goes in v11:
time: 352 us
  waiting for transfers between devices  234 us (66%)
  starting transfers between devices  47.9 us (14%)
  blocking collectives  28.1 us (8%)
  matrix products  14.2 us (4%)
  local copies, waits for them, and re-layouts  11.5 us (3%)
  Pallas kernels  9.4 us (3%)
  other arithmetic  5.95 us (2%)
    all_to_all x1, waiting for transfers between devices, local(): lax.all_to_all(items, 'pairs', split_axis=0, concat_axis=0, tiled=True)  213 us
    ppermute x7, starting transfers between devices, local(): lax.ppermute(piece, 'aux', [(i, (i + shift) % aux_count) for i in range(a...  30.6 us
    all_to_all x1, blocking collectives, local(): got = lax.all_to_all(pieces, 'aux', split_axis=0, concat_axis=0, tiled=True)  28.1 us
    dot_general x1, matrix products, local(): jnp.einsum('pqce,qfe->pcf', ladder_half, ladder_ints, preferred_element_t...  14.2 us
    ppermute x7, waiting for transfers between devices, local(): lax.ppermute(piece, 'aux', [(i, (i + shift) % aux_count) for i in range(a...  13.9 us
    all_to_all x1, starting transfers between devices, local(): lax.all_to_all(wanted.reshape(groups, capacity), 'pairs', split_axis=0, c...  11.6 us
    pallas_call x1, Pallas kernels, linked_sum(): pl.pallas_call(lambda *r: linked_kernel(links, pao_width, *r), grid_spec=...  9.4 us
    gather x1, local copies, waits for them, and re-layouts, local(): items = both[picked.reshape(groups * capacity)]  8.34 us
  transfers between devices with their start and end apart: 9, of which 4 were waited for; matrix products, arithmetic and copies ran while one was open for 6% of the time, Pallas kernels for 0%

profile of v11, /device:TPU:1, one launch (start us, length us, event | category | flops | bytes accessed | tf_op | source)
XLA Modules:
  0.0 351.6 jit_solution(7712992018471198819)
XLA Ops:
  0.0 0.0 copy-start
  0.0 1.0 convert_reduce_fusion
  1.0 0.7 fusion.15
  1.6 0.1 select_reduce_fusion
  1.8 0.8 sub.13
  2.5 11.6 %all-to-all-start = ((s32[64,1,2]{2,1,0:T(1,128)}), s32[64,1,2]{2,1,0:T(1,128)S(1)}, u32[]{:S(2)}, u32[]{:S(2)}) async-start(s32[64,1,2]{2,1,0:T(1,128)} %bitcast.4), calls=%async_computation | async-start | bytes 65536 | tf_op jit(solution)/shard_map/all_to_all | solution.py:85
  14.2 1.5 pad_maximum_fusion
  15.7 7.7 %all-to-all-done = s32[64,1,2]{2,1,0:T(1,128)S(1)} async-done(((s32[64,1,2]{2,1,0:T(1,128)}), s32[64,1,2]{2,1,0:T(1,128)S(1)}, u32[]{:S(2)}, u32[]{:S(2)}) %all-to-all-start) | async-done | bytes 544 | tf_op jit(solution)/shard_map/all_to_all | solution.py:85
  23.4 0.1 maximum_reduce_fusion
  23.5 0.1 reshape.62
  23.6 8.3 %gather_fusion = bf16[128,384,128]{2,1,0:T(8,128)(2,1)} fusion(bf16[16,384,128]{2,1,0:T(8,128)(2,1)S(1)} %pad_maximum_fusion, s32[1024]{0:T(1024)S(1)} %pad_clamp_fusion), kind=kCustom, calls=%fused_computation | custom fusion | bytes 25166336 | tf_op jit(solution)/shard_map/gather | solution.py:90
  32.0 0.0 copy-start.2
  32.0 5.7 %all-to-all-start.1 = ((bf16[128,384,128]{2,1,0:T(8,128)(2,1)}), bf16[128,384,128]{2,1,0:T(8,128)(2,1)}, u32[]{:S(2)}, u32[]{:S(2)}) async-start(bf16[128,384,128]{2,1,0:T(8,128)(2,1)} %gather_fusion), calls=%async_computation.1 | async-start | bytes 25165824 | tf_op jit(solution)/shard_map/all_to_all | solution.py:91
  37.7 0.0 copy-done
  37.7 0.0 copy-done.2
  37.7 14.2 %fusion.5 = f32[16,128,128]{2,1,0:T(8,128)S(1)} fusion(bf16[40,128,128]{2,1,0:T(8,128)(2,1)S(1)} %copy-done, bf16[16,128,128]{2,1,0:T(8,128)(2,1)S(1)} %copy-done.2), kind=kOutput, calls=%fused_computation.6 | convolution fusion | flops 5379194880 | bytes 2883584 | tf_op jit(solution)/shard_map/pqce,qfe->pcf/dot_general | solution.py:96
  51.9 0.0 copy-start.1
  52.0 0.0 copy-start.4
  52.0 0.0 copy-start.3
  52.0 0.9 constant_dynamic-slice_fusion.5
  52.9 10.9 %collective-permute-start.6 = (f32[2,128,128]{2,1,0:T(8,128)}, f32[2,128,128]{2,1,0:T(8,128)}, u32[]{:S(2)}, u32[]{:S(2)}) collective-permute-start(f32[2,128,128]{2,1,0:T(8,128)} %get-tuple-element.10), channel_id=1, source_target_pairs={{0,7},{1,0},{2,1},{3,2},{4,3},{5,4},{6,5},{7,6},{8,15},{9,8},{10,9... | collective-permute-start | bytes 393224 | tf_op jit(solution)/shard_map/ppermute | solution.py:105
  63.7 2.2 collective-permute-start.5
  65.9 1.9 collective-permute-start.4
  67.9 7.0 %collective-permute-start.3 = (f32[2,128,128]{2,1,0:T(8,128)}, f32[2,128,128]{2,1,0:T(8,128)}, u32[]{:S(2)}, u32[]{:S(2)}) collective-permute-start(f32[2,128,128]{2,1,0:T(8,128)} %get-tuple-element.13), channel_id=1, source_target_pairs={{0,4},{1,5},{2,6},{3,7},{4,0},{5,1},{6,2},{7,3},{8,12},{9,13},{10,... | collective-permute-start | bytes 393224 | tf_op jit(solution)/shard_map/ppermute | solution.py:105
  74.9 1.9 collective-permute-start.2
  76.9 0.0 copy-done.1
  76.9 1.4 copy.17
  78.2 0.0 collective-permute-done.6
  78.2 3.3 collective-permute-start.1
  81.5 0.0 collective-permute-done.5
  81.5 3.4 collective-permute-start
  84.9 0.0 copy-done.4
  84.9 0.5 multiply_add_fusion.r_0_
  85.4 0.0 collective-permute-done.4
  85.4 0.0 collective-permute-done.3
  85.4 0.0 collective-permute-done.2
  85.5 10.0 %collective-permute-done.1 = f32[2,128,128]{2,1,0:T(8,128)S(1)} collective-permute-done((f32[2,128,128]{2,1,0:T(8,128)}, f32[2,128,128]{2,1,0:T(8,128)S(1)}, u32[]{:S(2)}, u32[]{:S(2)}) %collective-permute-start.1) | collective-permute-done | bytes 131104 | tf_op jit(solution)/shard_map/ppermute | solution.py:105
  95.5 3.9 %collective-permute-done = f32[2,128,128]{2,1,0:T(8,128)S(1)} collective-permute-done((f32[2,128,128]{2,1,0:T(8,128)S(1)}, f32[2,128,128]{2,1,0:T(8,128)S(1)}, u32[]{:S(2)}, u32[]{:S(2)}) %collective-permute-start) | collective-permute-done | bytes 131104 | tf_op jit(solution)/shard_map/ppermute | solution.py:105
  99.4 0.0 copy-done.3
  99.4 1.3 fusion.12
  100.7 212.7 %all-to-all-done.1.r_2_.r_3_.r_4_.r_5_.r_6_.r_7_.r_8_.r_9_.r_10_.r_11_.r_12_.r_13_.r_14_.r_15_.r_16_.r_17_.r_18_.r_19_.r_20_.r_21_.r_22_.r_23_.r_24_.r_25_ = bf16[128,384,128]{2,1,0:T(8,128)(2,1)} async-done(((bf16[128,384,128]{2,1,0:T(8,128)(2,1)}), bf16[128,384,128]{2,1,0:T(8,128)(2,1)}, u32[]{:S(2)}, u32[]{:S(2)}) %all-to-all-start.1) | async-done | bytes 12582944 | tf_op jit(solution)/shard_map/all_to_all | solution.py:91
  313.4 9.4 %shard_map.73 = bf16[16,128,128]{2,1,0:T(8,128)(2,1)} custom-call(s32[96]{0:T(128)} %multiply_add_fusion.r_0_, bf16[16,128,256]{2,1,0:T(8,128)(2,1)} %bitcast.33, bf16[128,384,128]{2,1,0:T(8,128)(2,1)} %all-to-all-done.1.r_2_.r_3_.r_4_.r_5_.r_6_.r_7_.r_8_.r_9_.r_10_.r_11_.r_12_.r_13_.r_14_.r_15_.r_16_.r_17_.r_18_.r_19_.r_20_.r_21_.r_22_.r_23_.r_24_.r_25_, ...), custom_call_target="tpu_custom_call" | custom-call | flops 1610612736 | bytes 11010048 | tf_op jit(solution)/shard_map/pallas_call | solution.py:53
  322.8 28.1 %all_to_all.16 = bf16[8,2,128,128]{3,2,1,0:T(8,128)(2,1)S(1)} all-to-all(bf16[8,2,128,128]{3,2,1,0:T(8,128)(2,1)} %bitcast.34), channel_id=1, replica_groups=mesh['pairs'=64,'aux'=8] {'aux'}, dimensions={0} | all-to-all | bytes 1048576 | tf_op jit(solution)/shard_map/all_to_all | solution.py:120
  350.8 0.8 fusion.13
  (2 shorter events, 0.0 us)
Async XLA Ops:
  0.0 37.7 %copy-start = (bf16[40,128,128]{2,1,0:T(8,128)(2,1)S(1)}, bf16[40,128,128]{2,1,0:T(8,128)(2,1)}, u32[]{:S(2)}) copy-start(bf16[40,128,128]{2,1,0:T(8,128)(2,1)} %param.9) | copy-start | bytes 3932164
  2.5 20.8 %all-to-all-start = ((s32[64,1,2]{2,1,0:T(1,128)}), s32[64,1,2]{2,1,0:T(1,128)S(1)}, u32[]{:S(2)}, u32[]{:S(2)}) async-start(s32[64,1,2]{2,1,0:T(1,128)} %bitcast.4), calls=%async_computation | async-start | bytes 65536 | tf_op jit(solution)/shard_map/all_to_all | solution.py:85
  32.0 5.8 %copy-start.2 = (bf16[16,128,128]{2,1,0:T(8,128)(2,1)S(1)}, bf16[16,128,128]{2,1,0:T(8,128)(2,1)}, u32[]{:S(2)}) copy-start(bf16[16,128,128]{2,1,0:T(8,128)(2,1)} %param.7) | copy-start | bytes 1572868
  32.0 281.4 %all-to-all-start.1 = ((bf16[128,384,128]{2,1,0:T(8,128)(2,1)}), bf16[128,384,128]{2,1,0:T(8,128)(2,1)}, u32[]{:S(2)}, u32[]{:S(2)}) async-start(bf16[128,384,128]{2,1,0:T(8,128)(2,1)} %gather_fusion), calls=%async_computation.1 | async-start | bytes 25165824 | tf_op jit(solution)/shard_map/all_to_all | solution.py:91
  51.9 24.9 %copy-start.1 = (bf16[16,256,128]{2,1,0:T(8,128)(2,1)S(1)}, bf16[16,256,128]{2,1,0:T(8,128)(2,1)}, u32[]{:S(2)}) copy-start(bf16[16,256,128]{2,1,0:T(8,128)(2,1)} %param.8) | copy-start | bytes 3145732
  52.0 33.0 %copy-start.4 = (s32[96,1]{0,1:T(1,128)S(1)}, s32[96,1]{0,1:T(1,128)}, u32[]{:S(2)}) copy-start(s32[96,1]{0,1:T(1,128)} %param.12) | copy-start | bytes 1156
  52.0 47.4 %copy-start.3 = (f32[2,128]{1,0:T(2,128)S(1)}, f32[2,128]{1,0:T(2,128)}, u32[]{:S(2)}) copy-start(f32[2,128]{1,0:T(2,128)} %param.11) | copy-start | bytes 3076
  52.9 25.4 %collective-permute-start.6 = (f32[2,128,128]{2,1,0:T(8,128)}, f32[2,128,128]{2,1,0:T(8,128)}, u32[]{:S(2)}, u32[]{:S(2)}) collective-permute-start(f32[2,128,128]{2,1,0:T(8,128)} %get-tuple-element.10), channel_id=1, source_target_pairs={{0,7},{1,0},{2,1},{3,2},{4,3},{5,4},{6,5},{7,6},{8,15},{9,8},{10,9... | collective-permute-start | bytes 393224 | tf_op jit(solution)/shard_map/ppermute | solution.py:105
  63.7 17.8 %collective-permute-start.5 = (f32[2,128,128]{2,1,0:T(8,128)}, f32[2,128,128]{2,1,0:T(8,128)}, u32[]{:S(2)}, u32[]{:S(2)}) collective-permute-start(f32[2,128,128]{2,1,0:T(8,128)} %get-tuple-element.11), channel_id=1, source_target_pairs={{0,6},{1,7},{2,0},{3,1},{4,2},{5,3},{6,4},{7,5},{8,14},{9,15},{10,... | collective-permute-start | bytes 393224 | tf_op jit(solution)/shard_map/ppermute | solution.py:105
  65.9 19.5 %collective-permute-start.4 = (f32[2,128,128]{2,1,0:T(8,128)}, f32[2,128,128]{2,1,0:T(8,128)}, u32[]{:S(2)}, u32[]{:S(2)}) collective-permute-start(f32[2,128,128]{2,1,0:T(8,128)} %get-tuple-element.12), channel_id=1, source_target_pairs={{0,5},{1,6},{2,7},{3,0},{4,1},{5,2},{6,3},{7,4},{8,13},{9,14},{10,... | collective-permute-start | bytes 393224 | tf_op jit(solution)/shard_map/ppermute | solution.py:105
  67.9 17.6 %collective-permute-start.3 = (f32[2,128,128]{2,1,0:T(8,128)}, f32[2,128,128]{2,1,0:T(8,128)}, u32[]{:S(2)}, u32[]{:S(2)}) collective-permute-start(f32[2,128,128]{2,1,0:T(8,128)} %get-tuple-element.13), channel_id=1, source_target_pairs={{0,4},{1,5},{2,6},{3,7},{4,0},{5,1},{6,2},{7,3},{8,12},{9,13},{10,... | collective-permute-start | bytes 393224 | tf_op jit(solution)/shard_map/ppermute | solution.py:105
  74.9 10.5 %collective-permute-start.2 = (f32[2,128,128]{2,1,0:T(8,128)}, f32[2,128,128]{2,1,0:T(8,128)}, u32[]{:S(2)}, u32[]{:S(2)}) collective-permute-start(f32[2,128,128]{2,1,0:T(8,128)} %get-tuple-element.14), channel_id=1, source_target_pairs={{0,3},{1,4},{2,5},{3,6},{4,7},{5,0},{6,1},{7,2},{8,11},{9,12},{10,... | collective-permute-start | bytes 393224 | tf_op jit(solution)/shard_map/ppermute | solution.py:105
  78.2 17.3 %collective-permute-start.1 = (f32[2,128,128]{2,1,0:T(8,128)}, f32[2,128,128]{2,1,0:T(8,128)S(1)}, u32[]{:S(2)}, u32[]{:S(2)}) collective-permute-start(f32[2,128,128]{2,1,0:T(8,128)} %get-tuple-element.15), channel_id=1, source_target_pairs={{0,2},{1,3},{2,4},{3,5},{4,6},{5,7},{6,0},{7,1},{8,10},{9,11},{10,... | collective-permute-start | bytes 393224 | tf_op jit(solution)/shard_map/ppermute | solution.py:105
  81.5 17.8 %collective-permute-start = (f32[2,128,128]{2,1,0:T(8,128)S(1)}, f32[2,128,128]{2,1,0:T(8,128)S(1)}, u32[]{:S(2)}, u32[]{:S(2)}) collective-permute-start(f32[2,128,128]{2,1,0:T(8,128)S(1)} %get-tuple-element.9), channel_id=1, source_target_pairs={{0,1},{1,2},{2,3},{3,4},{4,5},{5,6},{6,7},{7,0},{8,9},{9,10},{10,1... | collective-permute-start | bytes 393224 | tf_op jit(solution)/shard_map/ppermute | solution.py:105
